TPU v7x, 32 devices: a whole 2x2x4 slice. The times are simulated.
32 devices in a mesh: dp: 8 (over z, y), tensor: 4 (over x, core).
Axes of the slice: x: 2, y: 2, z: 4, core: 2. Of those that a mesh axis runs over, the one named last changes fastest.
Arguments:
- tokens: bfloat16 [8, 1024, 1536], P('dp'), may hold values from -6 to 6
- piece_starts: int32 [8, 2], P('dp'), may hold values from -1 to 768, as said below
- attn_gain: bfloat16 [1536], P('dp'), may hold values from 0.5 to 1.5
- w_query: bfloat16 [1536, 1536], P('dp', 'tensor'), may hold values from -0.15625 to 0.15625
- w_key: bfloat16 [1536, 1536], P('dp', 'tensor'), may hold values from -0.15625 to 0.15625
- w_value: bfloat16 [1536, 1536], P('dp', 'tensor'), may hold values from -0.15625 to 0.15625
- w_outgate: bfloat16 [1536, 1536], P('dp', 'tensor'), may hold values from -0.15625 to 0.15625
- w_forget: bfloat16 [1536, 24], P('dp', 'tensor'), may hold values from -0.3125 to 0.3125
- forget_bias: float32 [24], P('tensor'), may hold values from 2 to 8
- w_output: bfloat16 [1536, 1536], P('tensor', 'dp'), may hold values from -0.4375 to 0.4375
- ffn_gain: bfloat16 [1536], P('dp'), may hold values from 0.5 to 1.5
- w_gate: bfloat16 [1536, 4096], P('dp', 'tensor'), may hold values from -0.15625 to 0.15625
- w_up: bfloat16 [1536, 4096], P('dp', 'tensor'), may hold values from -0.15625 to 0.15625
- w_down: bfloat16 [4096, 1536], P('tensor', 'dp'), may hold values from -0.09375 to 0.09375
- cotangent: bfloat16 [8, 1024, 1536], P('dp'), may hold values from -6 to 6
Outputs:
- output: bfloat16 [8, 1024, 1536], P('dp')
- tokens_grad: bfloat16 [8, 1024, 1536], P('dp')
- attn_gain_grad: float32 [1536], P('dp')
- w_query_grad: float32 [1536, 1536], P('dp', 'tensor')
- w_key_grad: float32 [1536, 1536], P('dp', 'tensor')
- w_value_grad: float32 [1536, 1536], P('dp', 'tensor')
- w_outgate_grad: float32 [1536, 1536], P('dp', 'tensor')
- w_forget_grad: float32 [1536, 24], P('dp', 'tensor')
- forget_bias_grad: float32 [24], P('tensor')
- w_output_grad: float32 [1536, 1536], P('tensor', 'dp')
- ffn_gain_grad: float32 [1536], P('dp')
- w_gate_grad: float32 [1536, 4096], P('dp', 'tensor')
- w_up_grad: float32 [1536, 4096], P('dp', 'tensor')
- w_down_grad: float32 [4096, 1536], P('tensor', 'dp')
Inputs may be any that keep to these rules, and one draw needn't show every extreme that they name: `piece_starts`: slot k of a sequence's row holds -1 (no piece) or a start in [k * 512, (k + 1) * 512 - 256], so pieces never intersect; the number of pieces differs between sequences.
All inputs are finite; a program needn't handle non-finite values.
Results may differ from a plain program's by a relative error of at most 0.025.
Values may be sent and summed in bfloat16 or wider, within the bound.
No kernel may reach another device: no remote copies, remote signals or barrier semaphores. Data moves between devices by JAX's collectives and lax.ppermute only.
A program may use at most 256 MiB of HBM per device.

v0:
```python
import jax
import jax.numpy as jnp
from jax import lax
from jax.sharding import PartitionSpec as P

PIECE = 256


epsilon = 1e-06
masked_value = -1e30


def project(left, right):
    return jnp.dot(left, right, preferred_element_type=jnp.float32)


def contract_rows(left, right):
    return lax.dot_general(
        left, right, (((0,), (0,)), ((), ())), preferred_element_type=jnp.float32
    )


def contract_cols(left, right):
    return lax.dot_general(
        left, right, (((1,), (1,)), ((), ())), preferred_element_type=jnp.float32
    )


def allowed_pairs(starts, length):
    places = jnp.arange(length, dtype=jnp.int32)
    inside = (
        (starts[:, None] >= 0)
        & (places[None, :] >= starts[:, None])
        & (places[None, :] < starts[:, None] + PIECE)
    )
    labels = jnp.sum(
        jnp.where(inside, jnp.arange(1, starts.shape[0] + 1, dtype=jnp.int32)[:, None], 0), axis=0
    )
    same = (labels[:, None] == labels[None, :]) & (labels[:, None] > 0)
    return (places[None, :] <= places[:, None]) | same


def block_scores(query_rows, key_all, decay, allowed_rows, first_row):
    count = query_rows.shape[0]
    raw = jnp.einsum(
        "qhd,khd->hqk", query_rows, key_all, preferred_element_type=jnp.float32
    ) * query_rows.shape[-1] ** (-0.5)
    apart = (
        lax.slice_in_dim(decay, first_row, first_row + count, axis=1)[:, :, None]
        - decay[:, None, :]
    )
    return (jnp.where(allowed_rows[None], raw - jnp.abs(apart), masked_value), apart)


def attend_forward(items):
    query_all, key_all, value_all, log_forget, starts = items
    length = query_all.shape[0]
    block_rows = min(512, length)
    decay = jnp.cumsum(log_forget, axis=0).T
    allowed = allowed_pairs(starts, length)
    results = []
    normalizers = []
    for first_row in range(0, length, block_rows):
        scores, apart = block_scores(
            query_all[first_row : first_row + block_rows],
            key_all,
            decay,
            allowed[first_row : first_row + block_rows],
            first_row,
        )
        largest = jnp.max(scores, axis=-1, keepdims=True)
        weights = jnp.exp(scores - largest)
        denominator = jnp.sum(weights, axis=-1, keepdims=True)
        chances = (weights / denominator).astype(jnp.bfloat16)
        results.append(
            jnp.einsum("hqk,khd->qhd", chances, value_all, preferred_element_type=jnp.float32)
        )
        normalizers.append(largest + jnp.log(denominator))
    return (jnp.concatenate(results, axis=0), jnp.concatenate(normalizers, axis=1))


def attend_backward(items):
    query_all, key_all, value_all, log_forget, starts, attended, normalizer, grad_out = items
    length = query_all.shape[0]
    block_rows = min(512, length)
    scale = query_all.shape[-1] ** (-0.5)
    decay = jnp.cumsum(log_forget, axis=0).T
    allowed = allowed_pairs(starts, length)
    grad_key = jnp.zeros(key_all.shape, jnp.float32)
    grad_value = jnp.zeros(value_all.shape, jnp.float32)
    grad_decay = jnp.zeros(decay.shape, jnp.float32)
    query_parts = []
    row_parts = []
    for first_row in range(0, length, block_rows):
        query_rows = query_all[first_row : first_row + block_rows]
        out_rows = grad_out[first_row : first_row + block_rows]
        scores, apart = block_scores(
            query_rows, key_all, decay, allowed[first_row : first_row + block_rows], first_row
        )
        chances = jnp.exp(scores - normalizer[:, first_row : first_row + block_rows])
        grad_chance = jnp.einsum(
            "qhd,khd->hqk", out_rows, value_all, preferred_element_type=jnp.float32
        )
        offset = jnp.sum(
            out_rows.astype(jnp.float32) * attended[first_row : first_row + block_rows], axis=-1
        ).T[:, :, None]
        grad_score = chances * (grad_chance - offset)
        grad_rounded = grad_score.astype(jnp.bfloat16)
        grad_value = grad_value + jnp.einsum(
            "hqk,qhd->khd",
            chances.astype(jnp.bfloat16),
            out_rows,
            preferred_element_type=jnp.float32,
        )
        grad_key = (
            grad_key
            + jnp.einsum(
                "hqk,qhd->khd", grad_rounded, query_rows, preferred_element_type=jnp.float32
            )
            * scale
        )
        query_parts.append(
            jnp.einsum("hqk,khd->qhd", grad_rounded, key_all, preferred_element_type=jnp.float32)
            * scale
        )
        signed = grad_score * jnp.sign(apart)
        grad_decay = grad_decay + jnp.sum(signed, axis=1)
        row_parts.append(-jnp.sum(signed, axis=-1))
    grad_decay = grad_decay + jnp.concatenate(row_parts, axis=1)
    grad_log = jnp.flip(jnp.cumsum(jnp.flip(grad_decay, axis=1), axis=1), axis=1).T
    grad_query = jnp.concatenate(query_parts, axis=0)
    return (
        grad_query.astype(jnp.bfloat16),
        grad_key.astype(jnp.bfloat16),
        grad_value.astype(jnp.bfloat16),
        grad_log,
    )


def on_device(
    tokens,
    piece_starts,
    attn_gain,
    w_query,
    w_key,
    w_value,
    w_outgate,
    w_forget,
    forget_bias,
    w_output,
    ffn_gain,
    w_gate,
    w_up,
    w_down,
    cotangent,
):
    sequences, length, width = tokens.shape
    heads_here = w_forget.shape[1]
    share_width = w_query.shape[1]
    head_size = share_width // heads_here
    row_count = sequences * length
    dp_count = lax.axis_size("dp")

    def head_view(values):
        return values.reshape(sequences, length, heads_here, head_size)

    attn_set = (
        lax.all_gather(attn_gain, "dp", axis=0, tiled=True),
        lax.all_gather(w_query, "dp", axis=0, tiled=True),
        lax.all_gather(w_key, "dp", axis=0, tiled=True),
        lax.all_gather(w_value, "dp", axis=0, tiled=True),
        lax.all_gather(w_outgate, "dp", axis=0, tiled=True),
        lax.all_gather(w_forget, "dp", axis=0, tiled=True),
        lax.all_gather(w_output, "dp", axis=1, tiled=True),
    )
    inputs = tokens.reshape(row_count, width).astype(jnp.float32)
    scale_one = lax.rsqrt(jnp.mean(inputs * inputs, axis=-1, keepdims=True) + epsilon)
    unit_one = inputs * scale_one
    normed = (unit_one * attn_set[0].astype(jnp.float32)).astype(jnp.bfloat16)
    joined = jnp.concatenate(attn_set[1:5], axis=1)
    projected = project(normed, joined)
    query_all = head_view(projected[:, :share_width].astype(jnp.bfloat16))
    key_all = head_view(projected[:, share_width : 2 * share_width].astype(jnp.bfloat16))
    value_all = head_view(projected[:, 2 * share_width : 3 * share_width].astype(jnp.bfloat16))
    gate_pre = projected[:, 3 * share_width :]
    forget_pre = project(normed, attn_set[5]) + forget_bias[None, :]
    log_forget = jax.nn.log_sigmoid(forget_pre).reshape(sequences, length, heads_here)
    attended, normalizer = lax.map(
        attend_forward, (query_all, key_all, value_all, log_forget, piece_starts)
    )
    attended_flat = attended.reshape(row_count, share_width)
    gate_open = jax.nn.sigmoid(gate_pre)
    gated = (attended_flat * gate_open).astype(jnp.bfloat16)
    attention = lax.psum(project(gated, attn_set[6]).astype(jnp.bfloat16), "tensor").astype(
        jnp.float32
    )
    hidden = inputs + attention
    ffn_set = (
        lax.all_gather(ffn_gain, "dp", axis=0, tiled=True),
        lax.all_gather(w_gate, "dp", axis=0, tiled=True),
        lax.all_gather(w_up, "dp", axis=0, tiled=True),
        lax.all_gather(w_down, "dp", axis=1, tiled=True),
    )
    scale_two = lax.rsqrt(jnp.mean(hidden * hidden, axis=-1, keepdims=True) + epsilon)
    unit_two = hidden * scale_two
    normed_two = (unit_two * ffn_set[0].astype(jnp.float32)).astype(jnp.bfloat16)
    units = ffn_set[1].shape[1]
    inner_pre = project(normed_two, jnp.concatenate(ffn_set[1:3], axis=1))
    gate_part = inner_pre[:, :units]
    up_part = inner_pre[:, units:]
    inner = (jax.nn.silu(gate_part) * up_part).astype(jnp.bfloat16)
    ffn_out = lax.psum(project(inner, ffn_set[3]).astype(jnp.bfloat16), "tensor").astype(
        jnp.float32
    )
    output = (hidden + ffn_out).astype(jnp.bfloat16).reshape(tokens.shape)
    upstream_low = cotangent.reshape(row_count, width)
    upstream = upstream_low.astype(jnp.float32)
    ffn_set = (
        lax.all_gather(ffn_gain, "dp", axis=0, tiled=True),
        lax.all_gather(w_gate, "dp", axis=0, tiled=True),
        lax.all_gather(w_up, "dp", axis=0, tiled=True),
        lax.all_gather(w_down, "dp", axis=1, tiled=True),
    )
    grad_down_w = contract_rows(inner, upstream_low)
    grad_inner = contract_cols(upstream_low, ffn_set[3])
    sigma = jax.nn.sigmoid(gate_part)
    grad_gate = (grad_inner * up_part * sigma * (1.0 + gate_part * (1.0 - sigma))).astype(
        jnp.bfloat16
    )
    grad_up = (grad_inner * gate_part * sigma).astype(jnp.bfloat16)
    grad_gate_w = contract_rows(normed_two, grad_gate)
    grad_up_w = contract_rows(normed_two, grad_up)
    grad_normed_two = lax.psum(
        (contract_cols(grad_gate, ffn_set[1]) + contract_cols(grad_up, ffn_set[2])).astype(
            jnp.bfloat16
        ),
        "tensor",
    ).astype(jnp.float32)
    grad_ffn_gain = jnp.sum(grad_normed_two * unit_two, axis=0)
    grad_unit_two = grad_normed_two * ffn_set[0].astype(jnp.float32)
    grad_hidden = upstream + scale_two * (
        grad_unit_two - unit_two * jnp.mean(grad_unit_two * unit_two, axis=-1, keepdims=True)
    )
    hidden_low = grad_hidden.astype(jnp.bfloat16)
    attn_set = (
        lax.all_gather(attn_gain, "dp", axis=0, tiled=True),
        lax.all_gather(w_query, "dp", axis=0, tiled=True),
        lax.all_gather(w_key, "dp", axis=0, tiled=True),
        lax.all_gather(w_value, "dp", axis=0, tiled=True),
        lax.all_gather(w_outgate, "dp", axis=0, tiled=True),
        lax.all_gather(w_forget, "dp", axis=0, tiled=True),
        lax.all_gather(w_output, "dp", axis=1, tiled=True),
    )
    joined = jnp.concatenate(attn_set[1:5], axis=1)
    grad_output_w = contract_rows(gated, hidden_low)
    grad_gated = contract_cols(hidden_low, attn_set[6])
    grad_attended = (grad_gated * gate_open).astype(jnp.bfloat16)
    grad_gate_pre = (grad_gated * attended_flat * gate_open * (1.0 - gate_open)).astype(
        jnp.bfloat16
    )
    grad_query, grad_key, grad_value, grad_log = lax.map(
        attend_backward,
        (
            query_all,
            key_all,
            value_all,
            log_forget,
            piece_starts,
            attended,
            normalizer,
            head_view(grad_attended),
        ),
    )
    grad_forget = (grad_log.reshape(row_count, heads_here) * jax.nn.sigmoid(-forget_pre)).astype(
        jnp.bfloat16
    )
    grad_four = jnp.concatenate(
        [
            grad_query.reshape(row_count, share_width),
            grad_key.reshape(row_count, share_width),
            grad_value.reshape(row_count, share_width),
            grad_gate_pre,
        ],
        axis=1,
    )
    grad_joined = contract_rows(normed, grad_four)
    grad_forget_w = contract_rows(normed, grad_forget)
    grad_bias = jnp.sum(grad_forget.astype(jnp.float32), axis=0)
    bias_rows = jnp.broadcast_to(grad_bias[None, :], (dp_count, heads_here))
    grad_normed = lax.psum(
        (contract_cols(grad_four, joined) + contract_cols(grad_forget, attn_set[5])).astype(
            jnp.bfloat16
        ),
        "tensor",
    ).astype(jnp.float32)
    grad_attn_gain = jnp.sum(grad_normed * unit_one, axis=0)
    grad_unit_one = grad_normed * attn_set[0].astype(jnp.float32)
    grad_inputs = grad_hidden + scale_one * (
        grad_unit_one - unit_one * jnp.mean(grad_unit_one * unit_one, axis=-1, keepdims=True)
    )
    tokens_grad = grad_inputs.astype(jnp.bfloat16).reshape(tokens.shape)
    grad_query_w = grad_joined[:, :share_width]
    grad_key_w = grad_joined[:, share_width : 2 * share_width]
    grad_value_w = grad_joined[:, 2 * share_width : 3 * share_width]
    grad_outgate_w = grad_joined[:, 3 * share_width :]
    combined = (
        lax.psum_scatter(grad_attn_gain, "dp", scatter_dimension=0, tiled=True),
        lax.psum_scatter(grad_query_w, "dp", scatter_dimension=0, tiled=True),
        lax.psum_scatter(grad_key_w, "dp", scatter_dimension=0, tiled=True),
        lax.psum_scatter(grad_value_w, "dp", scatter_dimension=0, tiled=True),
        lax.psum_scatter(grad_outgate_w, "dp", scatter_dimension=0, tiled=True),
        lax.psum_scatter(grad_forget_w, "dp", scatter_dimension=0, tiled=True),
        lax.psum_scatter(bias_rows, "dp", scatter_dimension=0, tiled=True),
        lax.psum_scatter(grad_output_w, "dp", scatter_dimension=1, tiled=True),
        lax.psum_scatter(grad_ffn_gain, "dp", scatter_dimension=0, tiled=True),
        lax.psum_scatter(grad_gate_w, "dp", scatter_dimension=0, tiled=True),
        lax.psum_scatter(grad_up_w, "dp", scatter_dimension=0, tiled=True),
        lax.psum_scatter(grad_down_w, "dp", scatter_dimension=1, tiled=True),
    )
    attn_sums = combined[:8]
    ffn_sums = combined[8:]
    return (
        output,
        tokens_grad,
        attn_sums[0],
        attn_sums[1],
        attn_sums[2],
        attn_sums[3],
        attn_sums[4],
        attn_sums[5],
        attn_sums[6].reshape(heads_here),
        attn_sums[7],
        ffn_sums[0],
        ffn_sums[1],
        ffn_sums[2],
        ffn_sums[3],
    )


def solution(mesh):
    placed = (
        P("dp", None, None),
        P("dp", None),
        P("dp"),
        P("dp", "tensor"),
        P("dp", "tensor"),
        P("dp", "tensor"),
        P("dp", "tensor"),
        P("dp", "tensor"),
        P("tensor"),
        P("tensor", "dp"),
        P("dp"),
        P("dp", "tensor"),
        P("dp", "tensor"),
        P("tensor", "dp"),
        P("dp", None, None),
    )
    return jax.shard_map(
        on_device,
        mesh=mesh,
        in_specs=placed,
        out_specs=(
            P("dp", None, None),
            P("dp", None, None),
            P("dp"),
            P("dp", "tensor"),
            P("dp", "tensor"),
            P("dp", "tensor"),
            P("dp", "tensor"),
            P("dp", "tensor"),
            P("tensor"),
            P("tensor", "dp"),
            P("dp"),
            P("dp", "tensor"),
            P("dp", "tensor"),
            P("tensor", "dp"),
        ),
        check_vma=False,
    )
```

profile of v0, /device:TPU:0, one launch (start us, length us, event | category | flops | bytes accessed | tf_op | source)
XLA Modules:
  0.0 1601.4 jit_solution(6284833572578524509)
XLA Ops:
  19.0 24.2 %all-reduce.6 = (bf16[1536]{0:T(1024)(128)(2,1)S(1)}, bf16[1536]{0:T(1024)(128)(2,1)}) all-reduce(bf16[1536]{0:T(1024)(128)(2,1)S(1)} %dynamic-update-slice, bf16[1536]{0:T(1024)(128)(2,1)S(1)} %dynamic-update-slice.1), channel_id=1, replica_groups=mesh['dp'=8,'tensor'=4] {'dp'}, use_global_device_ids=true, to_apply=%add | all-reduce | flops 3072 | bytes 12288
  43.2 30.8 %all-gather = bf16[8,192,6]{1,2,0:T(8,128)(2,1)S(1)} all-gather(bf16[1,192,6]{1,2,0:T(8,128)(2,1)} %bitcast.187), channel_id=1, replica_groups=mesh['dp'=8,'tensor'=4] {'dp'}, dimensions={0}, use_global_device_ids=true | all-gather | bytes 20736 | tf_op jit(solution)/shard_map/all_gather | solution.py:173
  86.0 10.1 all-gather.12.cloned.1.call-done
  98.8 39.4 %all-gather.14.cloned.1.call-done = bf16[1536,384]{1,0:T(8,128)(2,1)} async-done(((bf16[192,384]{1,0:T(8,128)(2,1)}), bf16[1536,384]{1,0:T(8,128)(2,1)}) %all-gather.14.cloned.1.call-update) | async-done | bytes 1179664 | tf_op jit(solution)/shard_map/all_gather | solution.py:171
  140.7 39.3 %all-gather.16.cloned.1.call-done = bf16[1536,384]{1,0:T(8,128)(2,1)} async-done(((bf16[192,384]{1,0:T(8,128)(2,1)}), bf16[1536,384]{1,0:T(8,128)(2,1)}) %all-gather.16.cloned.1.call-update) | async-done | bytes 1179664 | tf_op jit(solution)/shard_map/all_gather | solution.py:172
  182.5 9.5 fusion.110
  241.9 65.1 %all-reduce.12.cloned.1.call-done = bf16[1024,1536]{1,0:T(8,128)(2,1)} async-done(((bf16[1024,1536]{1,0:T(8,128)(2,1)}), bf16[1024,1536]{1,0:T(8,128)(2,1)}) %all-reduce.12.cloned.1.call-update) | async-done | bytes 3145744 | tf_op jit(solution)/shard_map/psum | solution.py:194
  313.0 56.4 %all-gather.20.cloned.1.call-done = bf16[1536,1024]{1,0:T(8,128)(2,1)} async-done(((bf16[192,1024]{1,0:T(8,128)(2,1)}), bf16[1536,1024]{1,0:T(8,128)(2,1)}) %all-gather.20.cloned.1.call-update) | async-done | bytes 3145744 | tf_op jit(solution)/shard_map/all_gather | solution.py:200
  369.4 60.9 %all-gather.22.cloned.1.call-done = bf16[1536,1024]{1,0:T(8,128)(2,1)} async-done(((bf16[192,1024]{1,0:T(8,128)(2,1)}), bf16[1536,1024]{1,0:T(8,128)(2,1)}) %all-gather.22.cloned.1.call-update) | async-done | bytes 3145744 | tf_op jit(solution)/shard_map/all_gather | solution.py:201
  430.3 12.3 fusion.36
  442.6 48.6 %all-gather.24.cloned.1.call-done = bf16[1024,1536]{0,1:T(8,128)(2,1)} async-done(((bf16[1024,192]{0,1:T(8,128)(2,1)}), bf16[1024,1536]{0,1:T(8,128)(2,1)}) %all-gather.24.cloned.1.call-update) | async-done | bytes 3145744 | tf_op jit(solution)/shard_map/all_gather | solution.py:202
  491.2 11.7 multiply_convert_fusion.1
  511.9 7.7 convolution_convert_fusion.1
  519.6 58.9 %all-reduce.14.cloned.1.call-done = bf16[1024,1536]{1,0:T(8,128)(2,1)} async-done(((bf16[1024,1536]{1,0:T(8,128)(2,1)}), bf16[1024,1536]{1,0:T(8,128)(2,1)}) %all-reduce.14.cloned.1.call-update) | async-done | bytes 3145744 | tf_op jit(solution)/shard_map/psum | solution.py:233
  600.4 7.9 fusion.32
  608.3 8.9 subtract_multiply_fusion.1
  617.3 17.9 %fusion.11 = (f32[6,1024]{1,0:T(8,128)}, f32[6,512]{1,0:T(8,128)}, f32[6,512]{1,0:T(8,128)}, f32[6,1024]{1,0:T(8,128)}, bf16[6,512,1024]{2,1,0:T(8,128)(2,1)}) fusion(f32[6,512]{1,0:T(8,128)S(1)} %copy-done.38, f32[6,1024]{1,0:T(8,128)S(1)} %bitcast.178, f32[6,512,1024]{2,1,0:T(8,128)} %subtract_multiply_fusion.1, f32[6,512]{1,0:T(8,128)S(1)} %copy-done.37, ...), kind=kOutput, calls=%fused_computation.23 | convolution fusion | flops 446674944 | bytes 32784384 | tf_op jit(solution)/shard_map/while/body/eval_jaxpr/qhd,khd->hqk/dot_general | solution.py:101
  679.7 9.0 fusion.95
  711.0 8.7 fusion.115
  720.0 8.6 fusion.114
  728.7 8.7 fusion.48
  744.7 119.9 %all-reduce.16.cloned.1.call-done = (bf16[1024,1536]{1,0:T(8,128)(2,1)}, bf16[1024,1536]{1,0:T(8,128)(2,1)}) async-done(((bf16[1024,1536]{1,0:T(8,128)(2,1)}, bf16[1024,1536]{1,0:T(8,128)(2,1)}), (bf16[1024,1536]{1,0:T(8,128)(2,1)}, bf16[1024,1536]{1,0:T(8,128)(2,1)})) %all-reduce.16.cloned.1.call-update) | async-done | bytes 6291472 | tf_op jit(solution)/shard_map/psum | solution.py:212
  868.4 37.3 %all-reduce.5 = (f32[1536]{0:T(1024)S(1)}, f32[8,6]{1,0:T(8,128)S(1)}, f32[1536]{0:T(1024)S(1)}) all-reduce(f32[1536]{0:T(1024)S(1)} %get-tuple-element.70, f32[8,6]{1,0:T(8,128)S(1)} %broadcast_in_dim.174, f32[1536]{0:T(1024)S(1)} %copy-done.35), channel_id=2, replica_groups=mesh['dp'=8,'tensor'=4] {'dp'}, use_global_device_ids=true, to_apply=%region_24.25.clone | all-reduce | flops 3120 | bytes 24960
  908.2 8.8 fusion.47
  917.0 22.0 %reduce-scatter.20.cloned.1.call-done = f32[384,192]{0,1:T(8,128)} async-done(((f32[384,1536]{0,1:T(8,128)}), f32[384,192]{0,1:T(8,128)}) %reduce-scatter.20.cloned.1.call-update) | async-done | bytes 294928 | tf_op jit(solution)/shard_map/reduce_scatter | solution.py:314
  939.0 72.8 %reduce-scatter.18.cloned.1.call-done = f32[192,384]{1,0:T(8,128)} async-done(((f32[1536,384]{1,0:T(8,128)}), f32[192,384]{1,0:T(8,128)}) %reduce-scatter.18.cloned.1.call-update) | async-done | bytes 294928 | tf_op jit(solution)/shard_map/reduce_scatter | solution.py:311
  1011.8 72.8 %reduce-scatter.16.cloned.1.call-done = f32[192,384]{1,0:T(8,128)} async-done(((f32[1536,384]{1,0:T(8,128)}), f32[192,384]{1,0:T(8,128)}) %reduce-scatter.16.cloned.1.call-update) | async-done | bytes 294928 | tf_op jit(solution)/shard_map/reduce_scatter | solution.py:310
  1084.5 72.7 %reduce-scatter.14.cloned.1.call-done = f32[192,384]{1,0:T(8,128)} async-done(((f32[1536,384]{1,0:T(8,128)}), f32[192,384]{1,0:T(8,128)}) %reduce-scatter.14.cloned.1.call-update) | async-done | bytes 294928 | tf_op jit(solution)/shard_map/reduce_scatter | solution.py:309
  1157.2 72.7 %reduce-scatter.12.cloned.1.call-done = f32[192,384]{1,0:T(8,128)} async-done(((f32[1536,384]{1,0:T(8,128)}), f32[192,384]{1,0:T(8,128)}) %reduce-scatter.12.cloned.1.call-update) | async-done | bytes 294928 | tf_op jit(solution)/shard_map/reduce_scatter | solution.py:308
  1230.0 121.3 %reduce-scatter.24.cloned.1.call-done = f32[192,1024]{1,0:T(8,128)} async-done(((f32[1536,1024]{1,0:T(8,128)}), f32[192,1024]{1,0:T(8,128)}) %reduce-scatter.24.cloned.1.call-update) | async-done | bytes 786448 | tf_op jit(solution)/shard_map/reduce_scatter | solution.py:317
  1351.3 121.5 %reduce-scatter.22.cloned.1.call-done = f32[192,1024]{1,0:T(8,128)} async-done(((f32[1536,1024]{1,0:T(8,128)}), f32[192,1024]{1,0:T(8,128)}) %reduce-scatter.22.cloned.1.call-update) | async-done | bytes 786448 | tf_op jit(solution)/shard_map/reduce_scatter | solution.py:316
  1472.8 121.3 %reduce-scatter.26.cloned.1.call-done = f32[1024,192]{0,1:T(8,128)} async-done(((f32[1024,1536]{0,1:T(8,128)}), f32[1024,192]{0,1:T(8,128)}) %reduce-scatter.26.cloned.1.call-update) | async-done | bytes 786448 | tf_op jit(solution)/shard_map/reduce_scatter | solution.py:318
  (235 shorter events, 197.0 us)
Async XLA Ops:
  7.2 76.4 %all-gather.10.cloned.1.call-start = ((), (), s32[]{:S(2)}) async-start(), calls=%async_computation.9 | async-start | bytes 1327104 | tf_op jit(solution)/shard_map/all_gather | solution.py:169
  7.9 88.2 %all-gather.12.cloned.1.call-start = ((), (), s32[]{:S(2)}) async-start(), calls=%async_computation.10 | async-start | bytes 1327104 | tf_op jit(solution)/shard_map/all_gather | solution.py:170
  8.7 129.5 %all-gather.14.cloned.1.call-start = ((), (), s32[]{:S(2)}) async-start(), calls=%async_computation.11 | async-start | bytes 1327104 | tf_op jit(solution)/shard_map/all_gather | solution.py:171
  9.4 170.6 %all-gather.16.cloned.1.call-start = ((), (), s32[]{:S(2)}) async-start(), calls=%async_computation.12 | async-start | bytes 1327104 | tf_op jit(solution)/shard_map/all_gather | solution.py:172
  10.0 224.6 %all-gather.18.cloned.1.call-start = ((), (), s32[]{:S(2)}) async-start(), calls=%async_computation.13 | async-start | bytes 1327104 | tf_op jit(solution)/shard_map/all_gather | solution.py:174
  10.6 296.5 %all-reduce.12.cloned.1.call-start = ((), (), s32[]{:S(2)}) async-start(), calls=%async_computation.14 | async-start | bytes 6291456 | tf_op jit(solution)/shard_map/psum | solution.py:194
  15.3 167.2 %copy-start.33 = (f32[1024]{0:T(1024)}, f32[1024]{0:T(1024)S(1)}, u32[]{:S(2)}) copy-start(f32[1024]{0:T(1024)S(1)} %add_rsqrt_fusion.1) | copy-start | bytes 12292
  43.2 139.3 %copy-start.28 = (f32[1536]{0:T(1024)}, f32[1536]{0:T(1024)S(1)}, u32[]{:S(2)}) copy-start(f32[1536]{0:T(1024)S(1)} %convert_element_type.134) | copy-start | bytes 18436
  81.0 101.5 %copy-start = (bf16[1,1024,1536]{2,1,0:T(8,128)(2,1)S(1)}, bf16[1,1024,1536]{2,1,0:T(8,128)(2,1)}, u32[]{:S(2)}) copy-start(bf16[1,1024,1536]{2,1,0:T(8,128)(2,1)} %param.15) | copy-start | bytes 9437188
  214.6 12.3 copy-start.13
  239.6 129.7 %all-gather.20.cloned.1.call-start = ((), (), s32[]{:S(2)}) async-start(), calls=%async_computation.15 | async-start | bytes 3538944 | tf_op jit(solution)/shard_map/all_gather | solution.py:200
  240.4 189.9 %all-gather.22.cloned.1.call-start = ((), (), s32[]{:S(2)}) async-start(), calls=%async_computation.16 | async-start | bytes 3538944 | tf_op jit(solution)/shard_map/all_gather | solution.py:201
  241.1 250.0 %all-gather.24.cloned.1.call-start = ((), (), s32[]{:S(2)}) async-start(), calls=%async_computation.17 | async-start | bytes 3538944 | tf_op jit(solution)/shard_map/all_gather | solution.py:202
  241.9 336.6 %all-reduce.14.cloned.1.call-start = ((), (), s32[]{:S(2)}) async-start(), calls=%async_computation.18 | async-start | bytes 6291456 | tf_op jit(solution)/shard_map/psum | solution.py:233
  491.2 11.7 copy-start.40
  511.3 231.9 %reduce-scatter.28.cloned.1.call-start = ((), (), s32[]{:S(2)}) async-start(), calls=%async_computation.27 | async-start | bytes 884736
  635.2 11.3 copy-start.2
  641.1 9.5 slice-start
  641.2 9.5 slice-start.1
  664.2 11.5 copy-start.18
  664.2 12.4 copy-start.29
  664.2 12.4 copy-start.34
  679.6 185.0 %all-reduce.16.cloned.1.call-start = ((), (), s32[]{:S(2)}) async-start(), calls=%async_computation.28 | async-start | bytes 12582912 | tf_op jit(solution)/shard_map/psum | solution.py:212
  691.4 247.5 %reduce-scatter.20.cloned.1.call-start = ((), (), s32[]{:S(2)}) async-start(), calls=%async_computation.23 | async-start | bytes 2654208 | tf_op jit(solution)/shard_map/reduce_scatter | solution.py:314
  698.0 313.8 %reduce-scatter.18.cloned.1.call-start = ((), (), s32[]{:S(2)}) async-start(), calls=%async_computation.22 | async-start | bytes 2654208 | tf_op jit(solution)/shard_map/reduce_scatter | solution.py:311
  709.2 375.4 %reduce-scatter.16.cloned.1.call-start = ((), (), s32[]{:S(2)}) async-start(), calls=%async_computation.21 | async-start | bytes 2654208 | tf_op jit(solution)/shard_map/reduce_scatter | solution.py:310
  709.7 447.5 %reduce-scatter.14.cloned.1.call-start = ((), (), s32[]{:S(2)}) async-start(), calls=%async_computation.20 | async-start | bytes 2654208 | tf_op jit(solution)/shard_map/reduce_scatter | solution.py:309
  710.3 519.6 %reduce-scatter.12.cloned.1.call-start = ((), (), s32[]{:S(2)}) async-start(), calls=%async_computation.19 | async-start | bytes 2654208 | tf_op jit(solution)/shard_map/reduce_scatter | solution.py:308
  710.9 640.4 %reduce-scatter.24.cloned.1.call-start = ((), (), s32[]{:S(2)}) async-start(), calls=%async_computation.25 | async-start | bytes 7077888 | tf_op jit(solution)/shard_map/reduce_scatter | solution.py:317
  719.7 753.1 %reduce-scatter.22.cloned.1.call-start = ((), (), s32[]{:S(2)}) async-start(), calls=%async_computation.24 | async-start | bytes 7077888 | tf_op jit(solution)/shard_map/reduce_scatter | solution.py:316
  728.6 865.5 %reduce-scatter.26.cloned.1.call-start = ((), (), s32[]{:S(2)}) async-start(), calls=%async_computation.26 | async-start | bytes 7077888 | tf_op jit(solution)/shard_map/reduce_scatter | solution.py:318
  737.3 131.1 %copy-start.35 = (f32[1536]{0:T(1024)S(1)}, f32[1536]{0:T(1024)}, u32[]{:S(2)}) copy-start(f32[1536]{0:T(1024)} %get-tuple-element.68) | copy-start | bytes 18436
  (36 other events, 188.8 us)
Sparse Core Ops, SparseCore 0:
  10.2 44.0 all-gather.9
  56.4 39.6 all-gather.11
  98.3 39.7 all-gather.13
  140.2 39.7 all-gather.15
  182.1 39.8 all-gather.17
  239.8 67.2 all-reduce.11
  309.2 60.1 all-gather.19
  371.5 58.6 all-gather.21
  432.4 58.6 all-gather.23
  511.4 67.0 all-reduce.13
  679.7 63.4 reduce-scatter.27
  746.0 118.6 all-reduce.15
  868.7 70.2 reduce-scatter.19
  942.9 68.8 reduce-scatter.17
  1015.7 68.8 reduce-scatter.15
  1088.5 68.7 reduce-scatter.13
  1161.1 68.7 reduce-scatter.11
  1234.0 117.2 reduce-scatter.23
  1355.4 117.2 reduce-scatter.21
  1476.8 117.2 reduce-scatter.25
where the time goes:
time: 1610 us; the launch traced here: 1600 us
  waiting for transfers between devices  1190 us (74%)
  matrix products  196 us (12%)
  blocking collectives  92.3 us (6%)
  other arithmetic  55.1 us (3%)
  local copies, waits for them, and re-layouts  52.6 us (3%)
  between operations  16.7 us (1%)
    reduce_scatter x1, waiting for transfers between devices, on_device(): lax.psum_scatter(grad_gate_w, 'dp', scatter_dimension=0, tiled=True)  121 us
    reduce_scatter x1, waiting for transfers between devices, on_device(): lax.psum_scatter(grad_down_w, 'dp', scatter_dimension=1, tiled=True)  121 us
    reduce_scatter x1, waiting for transfers between devices, on_device(): lax.psum_scatter(grad_up_w, 'dp', scatter_dimension=0, tiled=True)  121 us
    psum x1, waiting for transfers between devices, on_device(): lax.psum(project(inner, ffn_set[3]).astype(jnp.bfloat16), 'tensor')  120 us
    reduce_scatter x1, waiting for transfers between devices, on_device(): lax.psum_scatter(grad_outgate_w, 'dp', scatter_dimension=0, tiled=True)  72.8 us
    reduce_scatter x1, waiting for transfers between devices, on_device(): lax.psum_scatter(grad_value_w, 'dp', scatter_dimension=0, tiled=True)  72.8 us
    reduce_scatter x1, waiting for transfers between devices, on_device(): lax.psum_scatter(grad_query_w, 'dp', scatter_dimension=0, tiled=True)  72.7 us
    reduce_scatter x1, waiting for transfers between devices, on_device(): lax.psum_scatter(grad_key_w, 'dp', scatter_dimension=0, tiled=True)  72.7 us
  transfers between devices with their start and end apart: 20, of which 18 were waited for; matrix products, arithmetic and copies ran while one was open for 11% of the time, Pallas kernels for 0%

commit v1 on v0

--- a/solution.py
+++ b/solution.py
@@ -159,31 +159,36 @@
     share_width = w_query.shape[1]
     head_size = share_width // heads_here
     row_count = sequences * length
-    dp_count = lax.axis_size("dp")
+    block = w_query.shape[0]
+    units = w_gate.shape[1]
 
     def head_view(values):
         return values.reshape(sequences, length, heads_here, head_size)
 
-    attn_set = (
-        lax.all_gather(attn_gain, "dp", axis=0, tiled=True),
-        lax.all_gather(w_query, "dp", axis=0, tiled=True),
-        lax.all_gather(w_key, "dp", axis=0, tiled=True),
-        lax.all_gather(w_value, "dp", axis=0, tiled=True),
-        lax.all_gather(w_outgate, "dp", axis=0, tiled=True),
-        lax.all_gather(w_forget, "dp", axis=0, tiled=True),
-        lax.all_gather(w_output, "dp", axis=1, tiled=True),
-    )
+    attn_local = jnp.concatenate(
+        [w_query, w_key, w_value, w_outgate, w_output.T, w_forget, attn_gain[:, None]], axis=1
+    )
+    attn_full = lax.all_gather(attn_local, "dp", axis=0, tiled=True)
+    joined = attn_full[:, : 4 * share_width]
+    output_t = attn_full[:, 4 * share_width : 5 * share_width]
+    forget_w = attn_full[:, 5 * share_width : 5 * share_width + heads_here]
+    gain_one = attn_full[:, 5 * share_width + heads_here].astype(jnp.float32)
+    ffn_local = jnp.concatenate([w_gate, w_up, w_down.T, ffn_gain[:, None]], axis=1)
+    ffn_full = lax.all_gather(ffn_local, "dp", axis=0, tiled=True)
+    gate_up_w = ffn_full[:, : 2 * units]
+    down_t = ffn_full[:, 2 * units : 3 * units]
+    gain_two = ffn_full[:, 3 * units].astype(jnp.float32)
+
     inputs = tokens.reshape(row_count, width).astype(jnp.float32)
     scale_one = lax.rsqrt(jnp.mean(inputs * inputs, axis=-1, keepdims=True) + epsilon)
     unit_one = inputs * scale_one
-    normed = (unit_one * attn_set[0].astype(jnp.float32)).astype(jnp.bfloat16)
-    joined = jnp.concatenate(attn_set[1:5], axis=1)
+    normed = (unit_one * gain_one).astype(jnp.bfloat16)
     projected = project(normed, joined)
     query_all = head_view(projected[:, :share_width].astype(jnp.bfloat16))
     key_all = head_view(projected[:, share_width : 2 * share_width].astype(jnp.bfloat16))
     value_all = head_view(projected[:, 2 * share_width : 3 * share_width].astype(jnp.bfloat16))
     gate_pre = projected[:, 3 * share_width :]
-    forget_pre = project(normed, attn_set[5]) + forget_bias[None, :]
+    forget_pre = project(normed, forget_w) + forget_bias[None, :]
     log_forget = jax.nn.log_sigmoid(forget_pre).reshape(sequences, length, heads_here)
     attended, normalizer = lax.map(
         attend_forward, (query_all, key_all, value_all, log_forget, piece_starts)
@@ -191,69 +196,51 @@
     attended_flat = attended.reshape(row_count, share_width)
     gate_open = jax.nn.sigmoid(gate_pre)
     gated = (attended_flat * gate_open).astype(jnp.bfloat16)
-    attention = lax.psum(project(gated, attn_set[6]).astype(jnp.bfloat16), "tensor").astype(
+    attention = lax.psum(contract_cols(gated, output_t).astype(jnp.bfloat16), "tensor").astype(
         jnp.float32
     )
     hidden = inputs + attention
-    ffn_set = (
-        lax.all_gather(ffn_gain, "dp", axis=0, tiled=True),
-        lax.all_gather(w_gate, "dp", axis=0, tiled=True),
-        lax.all_gather(w_up, "dp", axis=0, tiled=True),
-        lax.all_gather(w_down, "dp", axis=1, tiled=True),
-    )
     scale_two = lax.rsqrt(jnp.mean(hidden * hidden, axis=-1, keepdims=True) + epsilon)
     unit_two = hidden * scale_two
-    normed_two = (unit_two * ffn_set[0].astype(jnp.float32)).astype(jnp.bfloat16)
-    units = ffn_set[1].shape[1]
-    inner_pre = project(normed_two, jnp.concatenate(ffn_set[1:3], axis=1))
+    normed_two = (unit_two * gain_two).astype(jnp.bfloat16)
+    inner_pre = project(normed_two, gate_up_w)
     gate_part = inner_pre[:, :units]
     up_part = inner_pre[:, units:]
     inner = (jax.nn.silu(gate_part) * up_part).astype(jnp.bfloat16)
-    ffn_out = lax.psum(project(inner, ffn_set[3]).astype(jnp.bfloat16), "tensor").astype(
+    ffn_out = lax.psum(contract_cols(inner, down_t).astype(jnp.bfloat16), "tensor").astype(
         jnp.float32
     )
     output = (hidden + ffn_out).astype(jnp.bfloat16).reshape(tokens.shape)
     upstream_low = cotangent.reshape(row_count, width)
     upstream = upstream_low.astype(jnp.float32)
-    ffn_set = (
-        lax.all_gather(ffn_gain, "dp", axis=0, tiled=True),
-        lax.all_gather(w_gate, "dp", axis=0, tiled=True),
-        lax.all_gather(w_up, "dp", axis=0, tiled=True),
-        lax.all_gather(w_down, "dp", axis=1, tiled=True),
-    )
-    grad_down_w = contract_rows(inner, upstream_low)
-    grad_inner = contract_cols(upstream_low, ffn_set[3])
+    grad_down_t = contract_rows(upstream_low, inner)
+    grad_inner = project(upstream_low, down_t)
     sigma = jax.nn.sigmoid(gate_part)
     grad_gate = (grad_inner * up_part * sigma * (1.0 + gate_part * (1.0 - sigma))).astype(
         jnp.bfloat16
     )
     grad_up = (grad_inner * gate_part * sigma).astype(jnp.bfloat16)
-    grad_gate_w = contract_rows(normed_two, grad_gate)
-    grad_up_w = contract_rows(normed_two, grad_up)
+    grad_gate_up = jnp.concatenate([grad_gate, grad_up], axis=1)
+    grad_gate_up_w = contract_rows(normed_two, grad_gate_up)
     grad_normed_two = lax.psum(
-        (contract_cols(grad_gate, ffn_set[1]) + contract_cols(grad_up, ffn_set[2])).astype(
-            jnp.bfloat16
-        ),
-        "tensor",
+        contract_cols(grad_gate_up, gate_up_w).astype(jnp.bfloat16), "tensor"
     ).astype(jnp.float32)
     grad_ffn_gain = jnp.sum(grad_normed_two * unit_two, axis=0)
-    grad_unit_two = grad_normed_two * ffn_set[0].astype(jnp.float32)
+    ffn_sums = lax.psum_scatter(
+        jnp.concatenate(
+            [grad_gate_up_w, grad_down_t, grad_ffn_gain[:, None]], axis=1
+        ).astype(jnp.bfloat16),
+        "dp",
+        scatter_dimension=0,
+        tiled=True,
+    ).astype(jnp.float32)
+    grad_unit_two = grad_normed_two * gain_two
     grad_hidden = upstream + scale_two * (
         grad_unit_two - unit_two * jnp.mean(grad_unit_two * unit_two, axis=-1, keepdims=True)
     )
     hidden_low = grad_hidden.astype(jnp.bfloat16)
-    attn_set = (
-        lax.all_gather(attn_gain, "dp", axis=0, tiled=True),
-        lax.all_gather(w_query, "dp", axis=0, tiled=True),
-        lax.all_gather(w_key, "dp", axis=0, tiled=True),
-        lax.all_gather(w_value, "dp", axis=0, tiled=True),
-        lax.all_gather(w_outgate, "dp", axis=0, tiled=True),
-        lax.all_gather(w_forget, "dp", axis=0, tiled=True),
-        lax.all_gather(w_output, "dp", axis=1, tiled=True),
-    )
-    joined = jnp.concatenate(attn_set[1:5], axis=1)
-    grad_output_w = contract_rows(gated, hidden_low)
-    grad_gated = contract_cols(hidden_low, attn_set[6])
+    grad_output_t = contract_rows(hidden_low, gated)
+    grad_gated = project(hidden_low, output_t)
     grad_attended = (grad_gated * gate_open).astype(jnp.bfloat16)
     grad_gate_pre = (grad_gated * attended_flat * gate_open * (1.0 - gate_open)).astype(
         jnp.bfloat16
@@ -286,54 +273,47 @@
     grad_joined = contract_rows(normed, grad_four)
     grad_forget_w = contract_rows(normed, grad_forget)
     grad_bias = jnp.sum(grad_forget.astype(jnp.float32), axis=0)
-    bias_rows = jnp.broadcast_to(grad_bias[None, :], (dp_count, heads_here))
     grad_normed = lax.psum(
-        (contract_cols(grad_four, joined) + contract_cols(grad_forget, attn_set[5])).astype(
+        (contract_cols(grad_four, joined) + contract_cols(grad_forget, forget_w)).astype(
             jnp.bfloat16
         ),
         "tensor",
     ).astype(jnp.float32)
     grad_attn_gain = jnp.sum(grad_normed * unit_one, axis=0)
-    grad_unit_one = grad_normed * attn_set[0].astype(jnp.float32)
+    grad_unit_one = grad_normed * gain_one
     grad_inputs = grad_hidden + scale_one * (
         grad_unit_one - unit_one * jnp.mean(grad_unit_one * unit_one, axis=-1, keepdims=True)
     )
     tokens_grad = grad_inputs.astype(jnp.bfloat16).reshape(tokens.shape)
-    grad_query_w = grad_joined[:, :share_width]
-    grad_key_w = grad_joined[:, share_width : 2 * share_width]
-    grad_value_w = grad_joined[:, 2 * share_width : 3 * share_width]
-    grad_outgate_w = grad_joined[:, 3 * share_width :]
-    combined = (
-        lax.psum_scatter(grad_attn_gain, "dp", scatter_dimension=0, tiled=True),
-        lax.psum_scatter(grad_query_w, "dp", scatter_dimension=0, tiled=True),
-        lax.psum_scatter(grad_key_w, "dp", scatter_dimension=0, tiled=True),
-        lax.psum_scatter(grad_value_w, "dp", scatter_dimension=0, tiled=True),
-        lax.psum_scatter(grad_outgate_w, "dp", scatter_dimension=0, tiled=True),
-        lax.psum_scatter(grad_forget_w, "dp", scatter_dimension=0, tiled=True),
-        lax.psum_scatter(bias_rows, "dp", scatter_dimension=0, tiled=True),
-        lax.psum_scatter(grad_output_w, "dp", scatter_dimension=1, tiled=True),
-        lax.psum_scatter(grad_ffn_gain, "dp", scatter_dimension=0, tiled=True),
-        lax.psum_scatter(grad_gate_w, "dp", scatter_dimension=0, tiled=True),
-        lax.psum_scatter(grad_up_w, "dp", scatter_dimension=0, tiled=True),
-        lax.psum_scatter(grad_down_w, "dp", scatter_dimension=1, tiled=True),
-    )
-    attn_sums = combined[:8]
-    ffn_sums = combined[8:]
+    place = jnp.arange(width, dtype=jnp.int32) % block
+    bias_col = jnp.where(
+        place < heads_here, jnp.take(grad_bias, jnp.minimum(place, heads_here - 1)), 0.0
+    )
+    attn_sums = lax.psum_scatter(
+        jnp.concatenate(
+            [grad_joined, grad_output_t, grad_forget_w, grad_attn_gain[:, None], bias_col[:, None]],
+            axis=1,
+        ).astype(jnp.bfloat16),
+        "dp",
+        scatter_dimension=0,
+        tiled=True,
+    ).astype(jnp.float32)
+    forget_at = 5 * share_width
     return (
         output,
         tokens_grad,
-        attn_sums[0],
-        attn_sums[1],
-        attn_sums[2],
-        attn_sums[3],
-        attn_sums[4],
-        attn_sums[5],
-        attn_sums[6].reshape(heads_here),
-        attn_sums[7],
-        ffn_sums[0],
-        ffn_sums[1],
-        ffn_sums[2],
-        ffn_sums[3],
+        attn_sums[:, forget_at + heads_here],
+        attn_sums[:, :share_width],
+        attn_sums[:, share_width : 2 * share_width],
+        attn_sums[:, 2 * share_width : 3 * share_width],
+        attn_sums[:, 3 * share_width : 4 * share_width],
+        attn_sums[:, forget_at : forget_at + heads_here],
+        attn_sums[:heads_here, forget_at + heads_here + 1],
+        attn_sums[:, 4 * share_width : 5 * share_width].T,
+        ffn_sums[:, 3 * units],
+        ffn_sums[:, :units],
+        ffn_sums[:, units : 2 * units],
+        ffn_sums[:, 2 * units : 3 * units].T,
     )
 
 

time: 1610 us -> 1080 us (0.67)
  waiting for transfers between devices: 1190 us -> 706 us
  blocking collectives: 92.3 us -> 0 us
  local copies, waits for them, and re-layouts: 52.6 us -> 99 us
  matrix products: 196 us -> 177 us
    reduce_scatter x8 -> x1, waiting for transfers between devices: 677 us -> 161 us  [on_device(): lax.psum_scatter(jnp.concatenate([grad_gate_up_w, grad_down_t, grad_ffn_g...]
    unnamed x21 -> x8, waiting for transfers between devices: 12.1 us -> 90 us
    unnamed x2 -> x0, blocking collectives: 61.5 us -> none
    all_gather x1 -> x0, blocking collectives: 30.8 us -> none  [on_device(): lax.all_gather(w_forget, 'dp', axis=0, tiled=True)]
    concatenate x1 -> x2, local copies, waits for them, and re-layouts: 2.44 us -> 28.6 us  [the longest x1 26.6 us: on_device(): jnp.concatenate([grad_joined, grad_output_t, grad_forget_w, grad_attn_gai...]
    psum x3, waiting for transfers between devices: 244 us -> 219 us  [the longest x1 96.9 us: on_device(): lax.psum(contract_cols(inner, down_t).astype(jnp.bfloat16), 'tensor')]
    all_gather x8 -> x2, waiting for transfers between devices: 255 us -> 236 us  [the longest x1 142 us: on_device(): ffn_full = lax.all_gather(ffn_local, 'dp', axis=0, tiled=True)]
    dot_general x6 -> x5, matrix products: 37.4 us -> 33.2 us  [contract_cols(): lax.dot_general(left, right, (((1,), (1,)), ((), ())), preferred_element_...]
  transfers between devices with their start and end apart: 20 -> 7, of which waited for: 18 -> 7; matrix products, arithmetic and copies ran while one was open for 11% -> 8% of each run, Pallas kernels for 0% -> 0%
where the time goes in v1:
time: 1080 us; the launch traced here: 1070 us
  waiting for transfers between devices  706 us (65%)
  matrix products  177 us (16%)
  local copies, waits for them, and re-layouts  99 us (9%)
  other arithmetic  69.7 us (6%)
  between operations  15.4 us (1%)
    reduce_scatter x1, waiting for transfers between devices, on_device(): lax.psum_scatter(jnp.concatenate([grad_gate_up_w, grad_down_t, grad_ffn_g...  161 us
    all_gather x1, waiting for transfers between devices, on_device(): ffn_full = lax.all_gather(ffn_local, 'dp', axis=0, tiled=True)  142 us
    psum x1, waiting for transfers between devices, on_device(): lax.psum(contract_cols(inner, down_t).astype(jnp.bfloat16), 'tensor')  96.9 us
    all_gather x1, waiting for transfers between devices, on_device(): attn_full = lax.all_gather(attn_local, 'dp', axis=0, tiled=True)  94.3 us
    unnamed x8, waiting for transfers between devices  90 us
    psum x1, waiting for transfers between devices, on_device(): lax.psum(contract_cols(gated, output_t).astype(jnp.bfloat16), 'tensor')  63.6 us
    psum x1, waiting for transfers between devices, on_device(): lax.psum(contract_cols(grad_gate_up, gate_up_w).astype(jnp.bfloat16), 'te...  58.4 us
    dot_general x5, matrix products, project(): return jnp.dot(left, right, preferred_element_type=jnp.float32)  39 us
  transfers between devices with their start and end apart: 7, of which 7 were waited for; matrix products, arithmetic and copies ran while one was open for 8% of the time, Pallas kernels for 0%

profile of v1, /device:TPU:0, one launch (start us, length us, event | category | flops | bytes accessed | tf_op | source)
XLA Modules:
  0.0 1067.6 jit_solution(12600640613263816599)
XLA Ops:
  18.3 94.3 %all-gather.3.cloned.1.call-done = bf16[1536,1927]{1,0:T(8,128)(2,1)} async-done(((bf16[192,1927]{1,0:T(8,128)(2,1)}), bf16[1536,1927]{1,0:T(8,128)(2,1)}) %all-gather.3.cloned.1.call-update) | async-done | bytes 5919760 | tf_op jit(solution)/shard_map/all_gather | solution.py:171
  113.9 9.4 fusion.126
  138.9 5.2 fusion.127
  172.9 4.8 convolution_convert_fusion.2
  180.8 63.6 %all-reduce.5.cloned.1.call-done = bf16[1024,1536]{1,0:T(8,128)(2,1)} async-done(((bf16[1024,1536]{1,0:T(8,128)(2,1)}), bf16[1024,1536]{1,0:T(8,128)(2,1)}) %all-reduce.5.cloned.1.call-update) | async-done | bytes 3145744 | tf_op jit(solution)/shard_map/psum | solution.py:199
  247.5 142.1 %all-gather.5.cloned.1.call-done = bf16[1536,3073]{1,0:T(8,128)(2,1)} async-done(((bf16[192,3073]{1,0:T(8,128)(2,1)}), bf16[1536,3073]{1,0:T(8,128)(2,1)}) %all-gather.5.cloned.1.call-update) | async-done | bytes 9440272 | tf_op jit(solution)/shard_map/all_gather | solution.py:177
  390.8 12.2 %fusion.43 = f32[1024,2048]{1,0:T(8,128)} fusion(bf16[1536,3073]{1,0:T(8,128)(2,1)} %all-gather.5.cloned.1.call-done, bf16[1024,1536]{1,0:T(8,128)(2,1)} %all-reduce.5.cloned.1.call-done, bf16[1,1024,1536]{2,1,0:T(8,128)(2,1)S(1)} %copy-done.1, f32[1536]{0:T(1024)S(1)} %convert_reduce_fusion, f32[1024]{0:T(1024)S(1)} %add_rsqrt_fusion), kind=kOutput, calls=%fused_computation.66 | convolution fusion | flops 6451888128 | bytes 20981760 | tf_op jit(solution)/shard_map/dot_general | solution.py:14
  403.0 8.5 fusion.47
  413.5 8.0 fusion.55
  422.2 7.6 convolution_convert_fusion.4
  429.9 58.4 %all-reduce.7.cloned.1.call-done = bf16[1024,1536]{1,0:T(8,128)(2,1)} async-done(((bf16[1024,1536]{1,0:T(8,128)(2,1)}), bf16[1024,1536]{1,0:T(8,128)(2,1)}) %all-reduce.7.cloned.1.call-update) | async-done | bytes 3145744 | tf_op jit(solution)/shard_map/psum | solution.py:225
  488.3 6.3 fusion.27
  497.2 6.9 multiply_convert_fusion.4
  508.3 6.9 fusion.32
  517.7 9.2 subtract_multiply_fusion.1
  527.0 16.8 %fusion.11 = (f32[6,1024]{1,0:T(8,128)}, f32[6,512]{1,0:T(8,128)}, f32[6,512]{1,0:T(8,128)}, f32[6,1024]{1,0:T(8,128)}, bf16[6,512,1024]{2,1,0:T(8,128)(2,1)S(1)}) fusion(f32[6,512]{1,0:T(8,128)} %get-tuple-element.169, f32[6,1024]{1,0:T(8,128)S(1)} %bitcast.188, f32[6,512,1024]{2,1,0:T(8,128)} %subtract_multiply_fusion.1, ...), kind=kOutput, calls=%fused_computation.23 | convolution fusion | flops 446674944 | bytes 32784384 | tf_op jit(solution)/shard_map/while/body/eval_jaxpr/qhd,khd->hqk/dot_general | solution.py:101
  548.9 7.5 fusion.95
  561.9 7.2 multiply_convert_fusion.3
  575.7 4.2 rev.9
  593.0 9.0 fusion.51
  606.7 4.5 fusion.110
  613.5 5.4 convolution_convert_fusion.5
  618.9 9.9 convolution_convert_fusion
  628.8 96.9 %all-reduce.9.cloned.1.call-done = (bf16[1024,1536]{1,0:T(8,128)(2,1)}, bf16[1024,1536]{1,0:T(8,128)(2,1)}) async-done(((bf16[1024,1536]{1,0:T(8,128)(2,1)}, bf16[1024,1536]{1,0:T(8,128)(2,1)}), (bf16[1024,1536]{1,0:T(8,128)(2,1)}, bf16[1024,1536]{1,0:T(8,128)(2,1)})) %all-reduce.9.cloned.1.call-update) | async-done | bytes 6291472 | tf_op jit(solution)/shard_map/psum | solution.py:210
  729.5 26.6 %concatenate.49 = bf16[1536,1928]{0,1:T(8,128)(2,1)} concatenate(bf16[1536,1536]{0,1:T(8,128)(2,1)} %convolution_convert_fusion, bf16[1536,384]{0,1:T(8,128)(2,1)} %convolution_convert_fusion.5, bf16[1536,6]{0,1:T(8,128)(2,1)S(1)} %copy-done.51, bf16[1536,1]{0,1:T(2,128)(2,1)S(1)} %broadcast_in_dim.195, bf16[1536,1]{0,1:T(2,128)(2,1)S(1)} %copy-done.52), dimensions={1} | concatenate | bytes 11845632 | tf_op jit(solution)/shard_map/concatenate | solution.py:293
  756.1 8.7 copy.140
  765.1 6.1 fusion.58
  771.3 7.9 convolution_convert_fusion.1
  779.5 4.9 pad_maximum_fusion
  784.4 8.8 fusion.60
  793.2 89.9 %reduce-scatter.7.cloned.1.call-done = bf16[192,1928]{1,0:T(8,128)(2,1)} async-done(((bf16[1536,1928]{1,0:T(8,128)(2,1)}), bf16[192,1928]{1,0:T(8,128)(2,1)}) %reduce-scatter.7.cloned.1.call-update) | async-done | bytes 740368
  895.1 160.7 %reduce-scatter.5.cloned.1.call-done = bf16[192,3073]{1,0:T(8,128)(2,1)} async-done(((bf16[1536,3073]{1,0:T(8,128)(2,1)}), bf16[192,3073]{1,0:T(8,128)(2,1)}) %reduce-scatter.5.cloned.1.call-update) | async-done | bytes 1180048 | tf_op jit(solution)/shard_map/reduce_scatter | solution.py:229
  (237 shorter events, 133.5 us)
Async XLA Ops:
  7.2 106.8 %copy-start.1 = (bf16[1,1024,1536]{2,1,0:T(8,128)(2,1)S(1)}, bf16[1,1024,1536]{2,1,0:T(8,128)(2,1)}, u32[]{:S(2)}) copy-start(bf16[1,1024,1536]{2,1,0:T(8,128)(2,1)} %param.15) | copy-start | bytes 9437188
  7.2 105.4 %all-gather.3.cloned.1.call-start = ((), (), s32[]{:S(2)}) async-start(), calls=%async_computation.2 | async-start | bytes 7077888 | tf_op jit(solution)/shard_map/all_gather | solution.py:171
  11.1 233.4 %all-reduce.5.cloned.1.call-start = ((), (), s32[]{:S(2)}) async-start(), calls=%async_computation.3 | async-start | bytes 6291456 | tf_op jit(solution)/shard_map/psum | solution.py:199
  15.8 112.2 %copy-start.49 = (f32[1024]{0:T(1024)}, f32[1024]{0:T(1024)S(1)}, u32[]{:S(2)}) copy-start(f32[1024]{0:T(1024)S(1)} %add_rsqrt_fusion.1) | copy-start | bytes 12292
  113.9 14.0 %copy-start.35 = (f32[1536]{0:T(1024)}, f32[1536]{0:T(1024)S(1)}, u32[]{:S(2)}) copy-start(f32[1536]{0:T(1024)S(1)} %convert_reduce_fusion.1) | copy-start | bytes 18436
  134.5 9.5 copy-start.22
  152.6 12.6 %copy-start.16 = (f32[512,6,64]{0,2,1:T(8,128)}, f32[512,6,64]{0,2,1:T(8,128)S(1)}, u32[]{:S(2)}) copy-start(f32[512,6,64]{0,2,1:T(8,128)S(1)} %fusion.84) | copy-start | bytes 2359300
  177.7 211.9 %all-gather.5.cloned.1.call-start = ((), (), s32[]{:S(2)}) async-start(), calls=%async_computation.4 | async-start | bytes 11059200 | tf_op jit(solution)/shard_map/all_gather | solution.py:177
  180.8 307.5 %all-reduce.7.cloned.1.call-start = ((), (), s32[]{:S(2)}) async-start(), calls=%async_computation.5 | async-start | bytes 6291456 | tf_op jit(solution)/shard_map/psum | solution.py:225
  247.5 247.1 %copy-start.47 = (f32[1024]{0:T(1024)}, f32[1024]{0:T(1024)S(1)}, u32[]{:S(2)}) copy-start(f32[1024]{0:T(1024)S(1)} %add_rsqrt_fusion) | copy-start | bytes 12292
  390.8 103.8 %copy-start.37 = (f32[1536]{0:T(1024)}, f32[1536]{0:T(1024)S(1)}, u32[]{:S(2)}) copy-start(f32[1536]{0:T(1024)S(1)} %convert_reduce_fusion) | copy-start | bytes 18436
  390.8 12.2 %copy-start.20 = (bf16[1,1024,1536]{2,1,0:T(8,128)(2,1)S(1)}, bf16[1,1024,1536]{2,1,0:T(8,128)(2,1)}, u32[]{:S(2)}) copy-start(bf16[1,1024,1536]{2,1,0:T(8,128)(2,1)} %param.29) | copy-start | bytes 9437188
  390.8 12.2 %copy-start.56 = (bf16[1536,3073]{1,0:T(8,128)(2,1)S(1)}, bf16[1536,3073]{1,0:T(8,128)(2,1)}, u32[]{:S(2)}) copy-start(bf16[1536,3073]{1,0:T(8,128)(2,1)} %all-gather.5.cloned.1.call-done) | copy-start | bytes 28320772
  413.5 8.8 copy-start.44
  421.5 304.2 %all-reduce.9.cloned.1.call-start = ((), (), s32[]{:S(2)}) async-start(), calls=%async_computation.8 | async-start | bytes 12582912 | tf_op jit(solution)/shard_map/psum | solution.py:210
  506.3 9.0 copy-start.12
  517.7 9.3 copy-start.13
  517.7 9.3 copy-start.15
  517.7 9.3 copy-start.33
  517.7 9.3 copy-start.46
  527.0 16.8 %copy-start.23 = (bf16[512,384]{0,1:T(8,128)(2,1)S(1)}, bf16[512,384]{0,1:T(8,128)(2,1)}, u32[]{:S(2)}) copy-start(bf16[512,384]{0,1:T(8,128)(2,1)} %copy-done.22) | copy-start | bytes 1179652
  543.8 12.7 %slice-start = ((s8[12582912]{0:T(1024)(128)(4,1)}), s8[4194304]{0:T(1024)(128)(4,1)S(1)}, s32[]{:S(2)}) async-start(s8[12582912]{0:T(1024)(128)(4,1)} %bitcast.158), calls=%async_computation.9 | async-start | bytes 8388608
  543.8 12.7 %slice-start.1 = ((s8[12582912]{0:T(1024)(128)(4,1)}), s8[4194304]{0:T(1024)(128)(4,1)S(1)}, s32[]{:S(2)}) async-start(s8[12582912]{0:T(1024)(128)(4,1)} %bitcast.158), calls=%async_computation.10 | async-start | bytes 8388608
  561.9 9.6 copy-start.24
  561.9 12.4 %copy-start.54 = (f32[6,512]{1,0:T(8,128)S(1)}, f32[6,512]{1,0:T(8,128)}, u32[]{:S(2)}) copy-start(f32[6,512]{1,0:T(8,128)} %get-tuple-element.141) | copy-start | bytes 36868
  593.0 9.0 copy-start.45
  602.1 9.2 copy-start.36
  602.1 9.1 copy-start.50
  605.8 277.3 %reduce-scatter.7.cloned.1.call-start = ((), (), s32[]{:S(2)}) async-start(), calls=%async_computation.7 | async-start | bytes 7077888
  628.8 100.7 %copy-start.51 = (bf16[1536,6]{0,1:T(8,128)(2,1)S(1)}, bf16[1536,6]{0,1:T(8,128)(2,1)}, u32[]{:S(2)}) copy-start(bf16[1536,6]{0,1:T(8,128)(2,1)} %convolution_convert_fusion.6) | copy-start | bytes 55300
  628.8 100.7 %copy-start.52 = (bf16[1536,1]{0,1:T(2,128)(2,1)S(1)}, bf16[1536,1]{0,1:T(2,128)(2,1)}, u32[]{:S(2)}) copy-start(bf16[1536,1]{0,1:T(2,128)(2,1)} %fusion.110) | copy-start | bytes 9220
  764.8 291.0 %reduce-scatter.5.cloned.1.call-start = ((), (), s32[]{:S(2)}) async-start(), calls=%async_computation.6 | async-start | bytes 11059200 | tf_op jit(solution)/shard_map/reduce_scatter | solution.py:229
  (41 other events, 199.6 us)
Sparse Core Ops, SparseCore 0:
  11.2 101.4 all-gather.2
  177.8 66.6 all-reduce.4
  247.2 142.3 all-gather.4
  421.7 66.5 all-reduce.6
  605.9 119.6 all-reduce.8
  764.9 118.2 reduce-scatter.6
  886.8 168.9 reduce-scatter.4

commit v2 on v1

--- a/solution.py
+++ b/solution.py
@@ -135,6 +135,100 @@
         grad_value.astype(jnp.bfloat16),
         grad_log,
     )
+
+
+def ring_order(n):
+    inner = 2 if n % 2 == 0 else 1
+    outer = n // inner
+    order = [o * inner for o in range(outer)]
+    if inner == 2:
+        order += [o * inner + 1 for o in reversed(range(outer))]
+    return order
+
+
+def ring_tables(n):
+    order = ring_order(n)
+    where = [0] * n
+    for p, d in enumerate(order):
+        where[d] = p
+    to_next = [(order[p], order[(p + 1) % n]) for p in range(n)]
+    to_prev = [(order[p], order[(p - 1) % n]) for p in range(n)]
+    return order, where, to_next, to_prev
+
+
+def ring_gather(local, axis):
+    n = lax.axis_size(axis)
+    rows = local.shape[0]
+    if n > 16:
+        return lax.all_gather(local, axis, axis=0, tiled=True)
+    order, where, to_next, to_prev = ring_tables(n)
+    me = lax.axis_index(axis)
+    out = jnp.zeros((n, rows) + local.shape[1:], local.dtype)
+    out = lax.dynamic_update_index_in_dim(out, local, me, axis=0)
+    ahead = n // 2
+    behind = n - 1 - ahead
+    moving_next = local
+    moving_prev = local
+    for step in range(1, ahead + 1):
+        moving_next = lax.ppermute(moving_next, axis, to_next)
+        source = jnp.asarray([order[(where[d] - step) % n] for d in range(n)], jnp.int32)[me]
+        out = lax.dynamic_update_index_in_dim(out, moving_next, source, axis=0)
+        if step <= behind:
+            moving_prev = lax.ppermute(moving_prev, axis, to_prev)
+            source = jnp.asarray([order[(where[d] + step) % n] for d in range(n)], jnp.int32)[me]
+            out = lax.dynamic_update_index_in_dim(out, moving_prev, source, axis=0)
+    return out.reshape((n * rows,) + local.shape[1:])
+
+
+def ring_reduce_scatter(full, axis):
+    n = lax.axis_size(axis)
+    rows = full.shape[0] // n
+    if n > 16:
+        return lax.psum_scatter(
+            full.astype(jnp.bfloat16), axis, scatter_dimension=0, tiled=True
+        ).astype(jnp.float32)
+    order, where, to_next, to_prev = ring_tables(n)
+    me = lax.axis_index(axis)
+
+    def chunk(shift):
+        index = jnp.asarray([order[(where[d] + shift) % n] for d in range(n)], jnp.int32)[me]
+        return lax.dynamic_slice_in_dim(full, index * rows, rows, axis=0)
+
+    ahead = n // 2
+    behind = n - 1 - ahead
+    part_next = None
+    part_prev = None
+    for step in range(ahead):
+        mine = chunk(ahead - step)
+        part_next = mine if part_next is None else part_next.astype(jnp.float32) + mine
+        part_next = lax.ppermute(part_next.astype(jnp.bfloat16), axis, to_next)
+        if step < behind:
+            mine = chunk(step - behind)
+            part_prev = mine if part_prev is None else part_prev.astype(jnp.float32) + mine
+            part_prev = lax.ppermute(part_prev.astype(jnp.bfloat16), axis, to_prev)
+    total = lax.dynamic_slice_in_dim(full, me * rows, rows, axis=0) + part_next.astype(jnp.float32)
+    if part_prev is not None:
+        total = total + part_prev.astype(jnp.float32)
+    return total
+
+
+def tensor_sum(term, axis):
+    n = lax.axis_size(axis)
+    if n != 4:
+        return lax.psum(term, axis).astype(jnp.float32)
+    half = term.shape[0] // 2
+    me = lax.axis_index(axis)
+    core = me % 2
+    keep = lax.dynamic_slice_in_dim(term, core * half, half, axis=0)
+    give = lax.dynamic_slice_in_dim(term, (1 - core) * half, half, axis=0)
+    on_chip = [(i, i ^ 1) for i in range(n)]
+    across = [(i, i ^ 2) for i in range(n)]
+    mine = keep.astype(jnp.float32) + lax.ppermute(give, axis, on_chip).astype(jnp.float32)
+    total = mine + lax.ppermute(mine.astype(term.dtype), axis, across).astype(jnp.float32)
+    back = lax.ppermute(total.astype(term.dtype), axis, on_chip).astype(jnp.float32)
+    first = jnp.where(core == 0, total, back)
+    second = jnp.where(core == 0, back, total)
+    return jnp.concatenate([first, second], axis=0)
 
 
 def on_device(
@@ -166,14 +260,16 @@
         return values.reshape(sequences, length, heads_here, head_size)
 
     attn_local = jnp.concatenate(
-        [w_query, w_key, w_value, w_outgate, w_output.T, w_forget, attn_gain[:, None]], axis=1
+        [w_output.T, w_query, w_key, w_value, w_outgate, w_forget, attn_gain[:, None]], axis=1
     )
     attn_full = lax.all_gather(attn_local, "dp", axis=0, tiled=True)
-    joined = attn_full[:, : 4 * share_width]
-    output_t = attn_full[:, 4 * share_width : 5 * share_width]
+    ffn_local = jnp.concatenate([w_gate, w_up, w_down.T, ffn_gain[:, None]], axis=1)
+    ffn_local, attn_full = lax.optimization_barrier((ffn_local, attn_full))
+    output_t = attn_full[:, :share_width]
+    joined = attn_full[:, share_width : 5 * share_width]
+    joined_five = attn_full[:, share_width : 5 * share_width + heads_here]
     forget_w = attn_full[:, 5 * share_width : 5 * share_width + heads_here]
     gain_one = attn_full[:, 5 * share_width + heads_here].astype(jnp.float32)
-    ffn_local = jnp.concatenate([w_gate, w_up, w_down.T, ffn_gain[:, None]], axis=1)
     ffn_full = lax.all_gather(ffn_local, "dp", axis=0, tiled=True)
     gate_up_w = ffn_full[:, : 2 * units]
     down_t = ffn_full[:, 2 * units : 3 * units]
@@ -196,9 +292,7 @@
     attended_flat = attended.reshape(row_count, share_width)
     gate_open = jax.nn.sigmoid(gate_pre)
     gated = (attended_flat * gate_open).astype(jnp.bfloat16)
-    attention = lax.psum(contract_cols(gated, output_t).astype(jnp.bfloat16), "tensor").astype(
-        jnp.float32
-    )
+    attention = tensor_sum(contract_cols(gated, output_t).astype(jnp.bfloat16), "tensor")
     hidden = inputs + attention
     scale_two = lax.rsqrt(jnp.mean(hidden * hidden, axis=-1, keepdims=True) + epsilon)
     unit_two = hidden * scale_two
@@ -207,13 +301,9 @@
     gate_part = inner_pre[:, :units]
     up_part = inner_pre[:, units:]
     inner = (jax.nn.silu(gate_part) * up_part).astype(jnp.bfloat16)
-    ffn_out = lax.psum(contract_cols(inner, down_t).astype(jnp.bfloat16), "tensor").astype(
-        jnp.float32
-    )
-    output = (hidden + ffn_out).astype(jnp.bfloat16).reshape(tokens.shape)
+    ffn_term = contract_cols(inner, down_t).astype(jnp.bfloat16)
     upstream_low = cotangent.reshape(row_count, width)
     upstream = upstream_low.astype(jnp.float32)
-    grad_down_t = contract_rows(upstream_low, inner)
     grad_inner = project(upstream_low, down_t)
     sigma = jax.nn.sigmoid(gate_part)
     grad_gate = (grad_inner * up_part * sigma * (1.0 + gate_part * (1.0 - sigma))).astype(
@@ -221,25 +311,27 @@
     )
     grad_up = (grad_inner * gate_part * sigma).astype(jnp.bfloat16)
     grad_gate_up = jnp.concatenate([grad_gate, grad_up], axis=1)
+    grad_normed_two = tensor_sum(
+        contract_cols(grad_gate_up, gate_up_w).astype(jnp.bfloat16), "tensor"
+    )
+    ffn_term, grad_normed_two = lax.optimization_barrier((ffn_term, grad_normed_two))
+    ffn_out = tensor_sum(ffn_term, "tensor")
+    grad_down_t = contract_rows(upstream_low, inner)
     grad_gate_up_w = contract_rows(normed_two, grad_gate_up)
-    grad_normed_two = lax.psum(
-        contract_cols(grad_gate_up, gate_up_w).astype(jnp.bfloat16), "tensor"
-    ).astype(jnp.float32)
     grad_ffn_gain = jnp.sum(grad_normed_two * unit_two, axis=0)
-    ffn_sums = lax.psum_scatter(
-        jnp.concatenate(
-            [grad_gate_up_w, grad_down_t, grad_ffn_gain[:, None]], axis=1
-        ).astype(jnp.bfloat16),
-        "dp",
-        scatter_dimension=0,
-        tiled=True,
-    ).astype(jnp.float32)
     grad_unit_two = grad_normed_two * gain_two
     grad_hidden = upstream + scale_two * (
         grad_unit_two - unit_two * jnp.mean(grad_unit_two * unit_two, axis=-1, keepdims=True)
     )
     hidden_low = grad_hidden.astype(jnp.bfloat16)
     grad_output_t = contract_rows(hidden_low, gated)
+    early_grads = jnp.concatenate(
+        [grad_gate_up_w, grad_down_t, grad_output_t, grad_ffn_gain[:, None]], axis=1
+    )
+    early_grads, hidden_low = lax.optimization_barrier((early_grads, hidden_low))
+    early_sums = lax.psum_scatter(
+        early_grads.astype(jnp.bfloat16), "dp", scatter_dimension=0, tiled=True
+    ).astype(jnp.float32)
     grad_gated = project(hidden_low, output_t)
     grad_attended = (grad_gated * gate_open).astype(jnp.bfloat16)
     grad_gate_pre = (grad_gated * attended_flat * gate_open * (1.0 - gate_open)).astype(
@@ -261,59 +353,50 @@
     grad_forget = (grad_log.reshape(row_count, heads_here) * jax.nn.sigmoid(-forget_pre)).astype(
         jnp.bfloat16
     )
-    grad_four = jnp.concatenate(
+    grad_five = jnp.concatenate(
         [
             grad_query.reshape(row_count, share_width),
             grad_key.reshape(row_count, share_width),
             grad_value.reshape(row_count, share_width),
             grad_gate_pre,
+            grad_forget,
         ],
         axis=1,
     )
-    grad_joined = contract_rows(normed, grad_four)
-    grad_forget_w = contract_rows(normed, grad_forget)
+    ffn_out, grad_five = lax.optimization_barrier((ffn_out, grad_five))
+    output = (hidden + ffn_out).astype(jnp.bfloat16).reshape(tokens.shape)
     grad_bias = jnp.sum(grad_forget.astype(jnp.float32), axis=0)
-    grad_normed = lax.psum(
-        (contract_cols(grad_four, joined) + contract_cols(grad_forget, forget_w)).astype(
-            jnp.bfloat16
-        ),
-        "tensor",
-    ).astype(jnp.float32)
+    place = jnp.arange(width, dtype=jnp.int32) % block
+    bias_col = jnp.where(
+        place < heads_here, jnp.take(grad_bias, jnp.minimum(place, heads_here - 1)), 0.0
+    )
+    late_grads = contract_rows(normed, grad_five)
+    grad_normed = tensor_sum(contract_cols(grad_five, joined_five).astype(jnp.bfloat16), "tensor")
     grad_attn_gain = jnp.sum(grad_normed * unit_one, axis=0)
+    late_sums = ring_reduce_scatter(
+        jnp.concatenate([late_grads, bias_col[:, None], grad_attn_gain[:, None]], axis=1), "dp"
+    )
     grad_unit_one = grad_normed * gain_one
     grad_inputs = grad_hidden + scale_one * (
         grad_unit_one - unit_one * jnp.mean(grad_unit_one * unit_one, axis=-1, keepdims=True)
     )
     tokens_grad = grad_inputs.astype(jnp.bfloat16).reshape(tokens.shape)
-    place = jnp.arange(width, dtype=jnp.int32) % block
-    bias_col = jnp.where(
-        place < heads_here, jnp.take(grad_bias, jnp.minimum(place, heads_here - 1)), 0.0
-    )
-    attn_sums = lax.psum_scatter(
-        jnp.concatenate(
-            [grad_joined, grad_output_t, grad_forget_w, grad_attn_gain[:, None], bias_col[:, None]],
-            axis=1,
-        ).astype(jnp.bfloat16),
-        "dp",
-        scatter_dimension=0,
-        tiled=True,
-    ).astype(jnp.float32)
-    forget_at = 5 * share_width
+    forget_at = 4 * share_width
     return (
         output,
         tokens_grad,
-        attn_sums[:, forget_at + heads_here],
-        attn_sums[:, :share_width],
-        attn_sums[:, share_width : 2 * share_width],
-        attn_sums[:, 2 * share_width : 3 * share_width],
-        attn_sums[:, 3 * share_width : 4 * share_width],
-        attn_sums[:, forget_at : forget_at + heads_here],
-        attn_sums[:heads_here, forget_at + heads_here + 1],
-        attn_sums[:, 4 * share_width : 5 * share_width].T,
-        ffn_sums[:, 3 * units],
-        ffn_sums[:, :units],
-        ffn_sums[:, units : 2 * units],
-        ffn_sums[:, 2 * units : 3 * units].T,
+        late_sums[:, forget_at + heads_here + 1],
+        late_sums[:, :share_width],
+        late_sums[:, share_width : 2 * share_width],
+        late_sums[:, 2 * share_width : 3 * share_width],
+        late_sums[:, 3 * share_width : 4 * share_width],
+        late_sums[:, forget_at : forget_at + heads_here],
+        late_sums[:heads_here, forget_at + heads_here],
+        early_sums[:, 3 * units : 3 * units + share_width].T,
+        early_sums[:, 3 * units + share_width],
+        early_sums[:, :units],
+        early_sums[:, units : 2 * units],
+        early_sums[:, 2 * units : 3 * units].T,
     )
 
 

time: 1080 us -> 658 us (0.61)
  waiting for transfers between devices: 706 us -> 291 us
  other arithmetic: 69.7 us -> 101 us
  local copies, waits for them, and re-layouts: 99 us -> 71.1 us
  matrix products: 177 us -> 156 us
  starting transfers between devices: 0.75 us -> 14.3 us
    psum x3 -> x0, waiting for transfers between devices: 219 us -> none  [the longest x1 96.9 us: on_device(): lax.psum(contract_cols(inner, down_t).astype(jnp.bfloat16), 'tensor')]
    ppermute x0 -> x19, waiting for transfers between devices: none -> 180 us  [the longest x4 127 us: tensor_sum(): lax.ppermute(mine.astype(term.dtype), axis, across).astype(jnp.float32)]
    reduce_scatter x1, waiting for transfers between devices: 161 us -> 0.01 us  [on_device(): lax.psum_scatter(early_grads.astype(jnp.bfloat16), 'dp', scatter_dimensio...]
    all_gather x1, waiting for transfers between devices: 142 us -> 19.4 us  [on_device(): ffn_full = lax.all_gather(ffn_local, 'dp', axis=0, tiled=True)]
    unnamed x8 -> x3, waiting for transfers between devices: 90 us -> 0.05 us
    convert_element_type x2 -> x13, other arithmetic: 1.69 us -> 24.4 us  [the longest x3 7.99 us: ring_reduce_scatter(): part_next = lax.ppermute(part_next.astype(jnp.bfloat16), axis, to_next)]
    select_n x0 -> x5, other arithmetic: none -> 15.8 us  [the longest x4 10.2 us: tensor_sum(): first = jnp.where(core == 0, total, back)]
    unnamed x144 -> x204, local copies, waits for them, and re-layouts: 28 us -> 12.3 us
  transfers between devices with their start and end apart: 7 -> 22, of which waited for: 7 -> 15; matrix products, arithmetic and copies ran while one was open for 8% -> 42% of each run, Pallas kernels for 0% -> 0%
where the time goes in v2:
time: 658 us; the launch traced here: 653 us
  waiting for transfers between devices  291 us (44%)
  matrix products  156 us (24%)
  other arithmetic  101 us (15%)
  local copies, waits for them, and re-layouts  71.1 us (11%)
  between operations  20 us (3%)
  starting transfers between devices  14.3 us (2%)
    ppermute x4, waiting for transfers between devices, tensor_sum(): lax.ppermute(mine.astype(term.dtype), axis, across).astype(jnp.float32)  127 us
    all_gather x1, waiting for transfers between devices, on_device(): attn_full = lax.all_gather(attn_local, 'dp', axis=0, tiled=True)  92.2 us
    dot_general x5, matrix products, project(): return jnp.dot(left, right, preferred_element_type=jnp.float32)  38.2 us
    ppermute x4, waiting for transfers between devices, ring_reduce_scatter(): part_next = lax.ppermute(part_next.astype(jnp.bfloat16), axis, to_next)  37.8 us
    dot_general x4, matrix products, contract_rows(): lax.dot_general(left, right, (((0,), (0,)), ((), ())), preferred_element_...  27.1 us
    dot_general x2, matrix products, attend_backward(): jnp.einsum('qhd,khd->hqk', out_rows, value_all, preferred_element_type=jn...  23.6 us
    dot_general x4, matrix products, contract_cols(): lax.dot_general(left, right, (((1,), (1,)), ((), ())), preferred_element_...  23.2 us
    all_gather x1, waiting for transfers between devices, on_device(): ffn_full = lax.all_gather(ffn_local, 'dp', axis=0, tiled=True)  19.4 us
  transfers between devices with their start and end apart: 22, of which 15 were waited for; matrix products, arithmetic and copies ran while one was open for 42% of the time, Pallas kernels for 0%

profile of v2, /device:TPU:0, one launch (start us, length us, event | category | flops | bytes accessed | tf_op | source)
XLA Modules:
  0.0 653.3 jit_solution(13070169394413438276)
XLA Ops:
  20.2 92.2 %all-gather.3.cloned.1.call-done = bf16[1536,1927]{1,0:T(8,128)(2,1)} async-done(((bf16[192,1927]{1,0:T(8,128)(2,1)}), bf16[1536,1927]{1,0:T(8,128)(2,1)}) %all-gather.3.cloned.1.call-update) | async-done | bytes 5919760 | tf_op jit(solution)/shard_map/all_gather | solution.py:265
  119.4 10.1 %fusion.137 = (bf16[1024,1536]{1,0:T(8,128)(2,1)S(1)}, f32[1024,1536]{1,0:T(8,128)}) fusion(bf16[1536,1927]{1,0:T(8,128)(2,1)} %all-gather.3.cloned.1.call-done, bf16[1,1024,1536]{2,1,0:T(8,128)(2,1)S(1)} %copy-done.4, f32[1536]{0:T(1024)S(1)} %convert_reduce_fusion.1, f32[1024]{0:T(1024)S(1)} %add_rsqrt_fusion.1), kind=kOutput, calls=%fused_computation.228 | convolution fusion | flops 4839702528 | bytes 17311744 | tf_op jit(solution)/shard_map/dot_general | solution.py:14
  142.0 5.2 fusion.138
  150.1 3.9 fusion.139
  186.0 35.2 %collective-permute-done.1 = bf16[512,1536]{1,0:T(8,128)(2,1)S(1)} collective-permute-done((bf16[512,1536]{1,0:T(8,128)(2,1)S(1)}, bf16[512,1536]{1,0:T(8,128)(2,1)S(1)}, u32[]{:S(2)}, u32[]{:S(2)}) %collective-permute-start.1) | collective-permute-done | bytes 1572896 | tf_op jit(solution)/shard_map/ppermute | solution.py:227
  228.7 3.8 convert_select_fusion.7
  235.7 19.4 %all-gather.5.cloned.1.call-done = bf16[1536,3073]{1,0:T(8,128)(2,1)} async-done(((bf16[192,3073]{1,0:T(8,128)(2,1)}), bf16[1536,3073]{1,0:T(8,128)(2,1)}) %all-gather.5.cloned.1.call-update) | async-done | bytes 9440272 | tf_op jit(solution)/shard_map/all_gather | solution.py:273
  256.3 12.9 %fusion.36 = f32[1024,2048]{1,0:T(8,128)} fusion(bf16[1536,3073]{1,0:T(8,128)(2,1)} %all-gather.5.cloned.1.call-done, f32[1024,1536]{1,0:T(8,128)} %get-tuple-element.190, f32[1536]{0:T(1024)S(1)} %convert_reduce_fusion, f32[1024]{0:T(1024)S(1)} %add_rsqrt_fusion), kind=kOutput, calls=%fused_computation.59 | convolution fusion | flops 6447169536 | bytes 20981760 | tf_op jit(solution)/shard_map/dot_general | solution.py:14
  269.2 7.4 %fusion.44 = (bf16[1024,1024]{1,0:T(8,128)(2,1)S(1)}, bf16[1024,1024]{1,0:T(8,128)(2,1)S(1)}, bf16[1024,1024]{1,0:T(8,128)(2,1)S(1)}) fusion(f32[1024,2048]{1,0:T(8,128)} %fusion.36, bf16[1536,3073]{1,0:T(8,128)(2,1)S(1)} %copy-done.74, bf16[1,1024,1536]{2,1,0:T(8,128)(2,1)S(1)} %copy-done.19), kind=kOutput, calls=%fused_computation.71 | convolution fusion | flops 3238002688 | bytes 20971520 | tf_op jit(solution)/shard_map/dot_general | solution.py:14
  278.0 7.3 %fusion.51 = bf16[1024,1536]{1,0:T(8,128)(2,1)S(1)} fusion(bf16[1536,3073]{1,0:T(8,128)(2,1)S(1)} %copy-done.74, bf16[1024,1024]{1,0:T(8,128)(2,1)S(1)} %get-tuple-element.192, bf16[1024,1024]{1,0:T(8,128)(2,1)S(1)} %get-tuple-element.191), kind=kOutput, calls=%fused_computation.87 | convolution fusion | flops 6452412416 | bytes 13631488 | tf_op jit(solution)/shard_map/dot_general | solution.py:24
  291.5 4.9 convolution_bitcast_fusion
  296.4 29.4 %collective-permute-done.4 = bf16[512,1536]{1,0:T(8,128)(2,1)S(1)} collective-permute-done((bf16[512,1536]{1,0:T(8,128)(2,1)S(1)}, bf16[512,1536]{1,0:T(8,128)(2,1)S(1)}, u32[]{:S(2)}, u32[]{:S(2)}) %collective-permute-start.4) | collective-permute-done | bytes 1572896 | tf_op jit(solution)/shard_map/ppermute | solution.py:227
  326.5 5.9 convolution_convert_fusion.1
  332.6 9.6 %fusion.73 = bf16[1536,2048]{1,0:T(8,128)(2,1)} fusion(bf16[1024,1024]{1,0:T(8,128)(2,1)S(1)} %copy-done.86, bf16[1024,1024]{1,0:T(8,128)(2,1)S(1)} %copy-done.84, f32[1024,1536]{1,0:T(8,128)S(1)} %bitcast.165, f32[1536]{0:T(1024)S(1)} %convert_reduce_fusion, f32[1024]{0:T(1024)S(1)} %add_rsqrt_fusion), kind=kOutput, calls=%fused_computation.117 | convolution fusion | flops 6455558144 | bytes 16787456 | tf_op jit(solution)/shard_map/dot_general | solution.py:18
  353.1 4.7 pad_maximum_fusion
  357.8 5.7 multiply_convert_fusion.4
  365.9 6.0 fusion.26
  371.9 7.7 %add_convert_fusion.1 = bf16[6,64,1024]{2,1,0:T(8,128)(2,1)} fusion(f32[6,64,1024]{2,1,0:T(8,128)S(1)} %fusion.26, bf16[512,6,64]{0,2,1:T(8,128)(2,1)S(1)} %bitcast.174, f32[6,512,1024]{2,1,0:T(8,128)} %copy-done, f32[6,512]{1,0:T(8,128)S(1)} %log_add_fusion.1), kind=kOutput, calls=%fused_computation.125 | convolution fusion | flops 409731072 | bytes 15347712 | tf_op jit(solution)/shard_map/while/body/eval_jaxpr/hqk,qhd->khd/dot_general | solution.py:109
  379.7 6.2 subtract_multiply_fusion.1
  388.3 17.3 %fusion.11 = (f32[6,1024]{1,0:T(8,128)S(1)}, f32[6,512]{1,0:T(8,128)S(1)}, f32[6,512]{1,0:T(8,128)S(1)}, f32[6,1024]{1,0:T(8,128)S(1)}, bf16[6,512,1024]{2,1,0:T(8,128)(2,1)}) fusion(f32[6,512]{1,0:T(8,128)S(1)} %copy-done.73, f32[6,1024]{1,0:T(8,128)S(1)} %bitcast.196, f32[6,512,1024]{2,1,0:T(8,128)} %subtract_multiply_fusion.1, ...), kind=kOutput, calls=%fused_computation.24 | convolution fusion | flops 446674944 | bytes 32784384 | tf_op jit(solution)/shard_map/while/body/eval_jaxpr/qhd,khd->hqk/dot_general | solution.py:101
  414.6 5.1 fusion.58
  423.0 27.1 %collective-permute-done.7 = bf16[512,1536]{1,0:T(8,128)(2,1)S(1)} collective-permute-done((bf16[512,1536]{1,0:T(8,128)(2,1)S(1)}, bf16[512,1536]{1,0:T(8,128)(2,1)S(1)}, u32[]{:S(2)}, u32[]{:S(2)}) %collective-permute-start.7) | collective-permute-done | bytes 1572896 | tf_op jit(solution)/shard_map/ppermute | solution.py:227
  455.9 5.0 fusion.89
  473.6 6.6 %fusion.48 = bf16[1024,1536]{1,0:T(8,128)(2,1)S(1)} fusion(bf16[1024,1542]{1,0:T(8,128)(2,1)S(1)} %constant_dynamic-update-slice_fusion, bf16[1536,1927]{1,0:T(8,128)(2,1)S(1)} %bitcast.203), kind=kOutput, calls=%fused_computation.86 | convolution fusion | flops 4852285440 | bytes 11665408 | tf_op jit(solution)/shard_map/dot_general | solution.py:24
  485.8 35.0 %collective-permute-done.10 = bf16[512,1536]{1,0:T(8,128)(2,1)S(1)} collective-permute-done((bf16[512,1536]{1,0:T(8,128)(2,1)S(1)}, bf16[512,1536]{1,0:T(8,128)(2,1)S(1)}, u32[]{:S(2)}, u32[]{:S(2)}) %collective-permute-start.10) | collective-permute-done | bytes 1572896 | tf_op jit(solution)/shard_map/ppermute | solution.py:227
  525.7 5.6 fusion.99
  531.3 10.8 %fusion.123 = f32[1536,1542]{1,0:T(8,128)} fusion(bf16[1024,1542]{1,0:T(8,128)(2,1)} %copy-done.51, bf16[1,1024,1536]{2,1,0:T(8,128)(2,1)S(1)} %copy-done.5, f32[1536]{0:T(1024)S(1)} %copy-done.60, f32[1024]{0:T(1024)S(1)} %copy-done.66), kind=kOutput, calls=%fused_computation.218 | convolution fusion | flops 4857004032 | bytes 15788032 | tf_op jit(solution)/shard_map/dot_general | solution.py:18
  548.5 12.2 %concatenate.64 = f32[1536,1544]{1,0:T(8,128)} concatenate(f32[1536,1542]{1,0:T(8,128)} %fusion.123, f32[1536,1]{1,0:T(8,128)} %fusion.99, f32[1536,1]{1,0:T(8,128)} %broadcast_in_dim.200), dimensions={1} | concatenate | bytes 18972672 | tf_op jit(solution)/shard_map/concatenate | solution.py:377
  566.9 13.8 %collective-permute-done.12 = bf16[192,1544]{1,0:T(8,128)(2,1)} collective-permute-done((bf16[192,1544]{1,0:T(8,128)(2,1)}, bf16[192,1544]{1,0:T(8,128)(2,1)}, u32[]{:S(2)}, u32[]{:S(2)}) %collective-permute-start.12) | collective-permute-done | bytes 592928 | tf_op jit(solution)/shard_map/ppermute | solution.py:204
  585.9 13.4 %collective-permute-done.13 = bf16[192,1544]{1,0:T(8,128)(2,1)} collective-permute-done((bf16[192,1544]{1,0:T(8,128)(2,1)}, bf16[192,1544]{1,0:T(8,128)(2,1)}, u32[]{:S(2)}, u32[]{:S(2)}) %collective-permute-start.13) | collective-permute-done | bytes 592928 | tf_op jit(solution)/shard_map/ppermute | solution.py:204
  607.4 10.7 %collective-permute-done.14 = bf16[192,1544]{1,0:T(8,128)(2,1)} collective-permute-done((bf16[192,1544]{1,0:T(8,128)(2,1)}, bf16[192,1544]{1,0:T(8,128)(2,1)}, u32[]{:S(2)}, u32[]{:S(2)}) %collective-permute-start.14) | collective-permute-done | bytes 592928 | tf_op jit(solution)/shard_map/ppermute | solution.py:204
  623.1 13.2 %fusion.66 = (bf16[1,1024,1536]{2,1,0:T(8,128)(2,1)}, bf16[1,1024,1536]{2,1,0:T(8,128)(2,1)}) fusion(f32[1024]{0:T(1024)S(1)} %broadcast_multiply_fusion, bf16[1,1024,1536]{2,1,0:T(8,128)(2,1)S(1)} %copy-done.5, f32[1536]{0:T(1024)S(1)} %copy-done.60, f32[512,1536]{1,0:T(8,128)} %copy-done.8, f32[512,1536]{1,0:T(8,128)S(1)} %copy-done.7, ...), kind=kLoop, calls=%fused_computation.110 | loop fusion | flops 28311552 | bytes 37777408 | tf_op jit(solution)/shard_map/reshape | solution.py:383
  (357 shorter events, 180.0 us)
Async XLA Ops:
  7.2 105.3 %all-gather.3.cloned.1.call-start = ((), (), s32[]{:S(2)}) async-start(), calls=%async_computation.1 | async-start | bytes 7077888 | tf_op jit(solution)/shard_map/all_gather | solution.py:265
  10.9 244.2 %all-gather.5.cloned.1.call-start = ((), (), s32[]{:S(2)}) async-start(), calls=%async_computation.2 | async-start | bytes 11059200 | tf_op jit(solution)/shard_map/all_gather | solution.py:273
  16.5 102.9 %copy-start.65 = (f32[1024]{0:T(1024)}, f32[1024]{0:T(1024)S(1)}, u32[]{:S(2)}) copy-start(f32[1024]{0:T(1024)S(1)} %add_rsqrt_fusion.1) | copy-start | bytes 12292
  18.0 95.8 %copy-start.4 = (bf16[1,1024,1536]{2,1,0:T(8,128)(2,1)S(1)}, bf16[1,1024,1536]{2,1,0:T(8,128)(2,1)}, u32[]{:S(2)}) copy-start(bf16[1,1024,1536]{2,1,0:T(8,128)(2,1)} %param.22) | copy-start | bytes 9437188
  18.0 95.8 %copy-start.75 = (f32[6]{0:T(128)S(1)}, f32[6]{0:T(128)}, u32[]{:S(2)}) copy-start(f32[6]{0:T(128)} %param.30) | copy-start | bytes 76
  112.5 528.7 %reduce-scatter.2.cloned.1.call-start = ((), (), s32[]{:S(2)}) async-start(), calls=%async_computation.3 | async-start | bytes 12386304 | tf_op jit(solution)/shard_map/reduce_scatter | solution.py:332
  178.7 3.8 collective-permute-start
  178.7 42.5 %copy-start.18 = (bf16[1024,1536]{1,0:T(8,128)(2,1)S(1)}, bf16[1024,1536]{1,0:T(8,128)(2,1)}, u32[]{:S(2)}) copy-start(bf16[1024,1536]{1,0:T(8,128)(2,1)} %copy-done.17) | copy-start | bytes 9437188
  184.7 36.5 %collective-permute-start.1 = (bf16[512,1536]{1,0:T(8,128)(2,1)S(1)}, bf16[512,1536]{1,0:T(8,128)(2,1)S(1)}, u32[]{:S(2)}, u32[]{:S(2)}) collective-permute-start(bf16[512,1536]{1,0:T(8,128)(2,1)S(1)} %fusion.67), channel_id=1, source_target_pairs={{0,2},{1,3},{2,0},{3,1},{4,6},{5,7},{6,4},{7,5},{8,10},{9,11},{10,... | collective-permute-start | bytes 4718600 | tf_op jit(solution)/shard_map/ppermute | solution.py:227
  224.9 3.8 collective-permute-start.2
  235.7 112.2 %copy-start.63 = (f32[1024]{0:T(1024)}, f32[1024]{0:T(1024)S(1)}, u32[]{:S(2)}) copy-start(f32[1024]{0:T(1024)S(1)} %add_rsqrt_fusion) | copy-start | bytes 12292
  256.3 91.7 %copy-start.57 = (f32[1536]{0:T(1024)}, f32[1536]{0:T(1024)S(1)}, u32[]{:S(2)}) copy-start(f32[1536]{0:T(1024)S(1)} %convert_reduce_fusion) | copy-start | bytes 18436
  285.4 3.5 collective-permute-start.3
  289.3 36.5 %collective-permute-start.4 = (bf16[512,1536]{1,0:T(8,128)(2,1)S(1)}, bf16[512,1536]{1,0:T(8,128)(2,1)S(1)}, u32[]{:S(2)}, u32[]{:S(2)}) collective-permute-start(bf16[512,1536]{1,0:T(8,128)(2,1)S(1)} %fusion.68), channel_id=1, source_target_pairs={{0,2},{1,3},{2,0},{3,1},{4,6},{5,7},{6,4},{7,5},{8,10},{9,11},{10,... | collective-permute-start | bytes 4718600 | tf_op jit(solution)/shard_map/ppermute | solution.py:227
  326.4 15.7 %collective-permute-start.5 = (bf16[512,1536]{1,0:T(8,128)(2,1)S(1)}, bf16[512,1536]{1,0:T(8,128)(2,1)S(1)}, u32[]{:S(2)}, u32[]{:S(2)}) collective-permute-start(bf16[512,1536]{1,0:T(8,128)(2,1)S(1)} %fusion.109), channel_id=1, source_target_pairs={{0,1},{1,0},{2,3},{3,2},{4,5},{5,4},{6,7},{7,6},{8,9},{9,8},{10,11... | collective-permute-start | bytes 4718600 | tf_op jit(solution)/shard_map/ppermute | solution.py:228
  347.1 64.0 %collective-permute-start.6 = (bf16[512,1536]{1,0:T(8,128)(2,1)}, bf16[512,1536]{1,0:T(8,128)(2,1)S(1)}, u32[]{:S(2)}, u32[]{:S(2)}) collective-permute-start(bf16[512,1536]{1,0:T(8,128)(2,1)} %constant_dynamic-slice_fusion.1), channel_id=1, source_target_pairs={{0,1},{1,0},{2,3},{3,2},{4,5},{5,4},{6,7},{7,6},{8,9},{9,8},{10,11... | collective-permute-start | bytes 4718600 | tf_op jit(solution)/shard_map/ppermute | solution.py:226
  413.0 37.1 %collective-permute-start.7 = (bf16[512,1536]{1,0:T(8,128)(2,1)S(1)}, bf16[512,1536]{1,0:T(8,128)(2,1)S(1)}, u32[]{:S(2)}, u32[]{:S(2)}) collective-permute-start(bf16[512,1536]{1,0:T(8,128)(2,1)S(1)} %fusion.69), channel_id=1, source_target_pairs={{0,2},{1,3},{2,0},{3,1},{4,6},{5,7},{6,4},{7,5},{8,10},{9,11},{10,... | collective-permute-start | bytes 4718600 | tf_op jit(solution)/shard_map/ppermute | solution.py:227
  451.8 15.1 %collective-permute-start.8 = (bf16[512,1536]{1,0:T(8,128)(2,1)}, bf16[512,1536]{1,0:T(8,128)(2,1)}, u32[]{:S(2)}, u32[]{:S(2)}) collective-permute-start(bf16[512,1536]{1,0:T(8,128)(2,1)} %fusion.110), channel_id=1, source_target_pairs={{0,1},{1,0},{2,3},{3,2},{4,5},{5,4},{6,7},{7,6},{8,9},{9,8},{10,11... | collective-permute-start | bytes 4718600 | tf_op jit(solution)/shard_map/ppermute | solution.py:228
  480.3 3.5 collective-permute-start.9
  484.2 40.8 %copy-start.69 = (f32[6]{0:T(128)S(1)}, f32[6]{0:T(128)}, u32[]{:S(2)}) copy-start(f32[6]{0:T(128)} %get-tuple-element.187) | copy-start | bytes 76
  484.3 47.0 %copy-start.5 = (bf16[1,1024,1536]{2,1,0:T(8,128)(2,1)S(1)}, bf16[1,1024,1536]{2,1,0:T(8,128)(2,1)}, u32[]{:S(2)}) copy-start(bf16[1,1024,1536]{2,1,0:T(8,128)(2,1)} %param.22) | copy-start | bytes 9437188
  484.3 47.0 %copy-start.60 = (f32[1536]{0:T(1024)S(1)}, f32[1536]{0:T(1024)}, u32[]{:S(2)}) copy-start(f32[1536]{0:T(1024)} %copy-done.59) | copy-start | bytes 18436
  484.3 47.0 %copy-start.66 = (f32[1024]{0:T(1024)S(1)}, f32[1024]{0:T(1024)}, u32[]{:S(2)}) copy-start(f32[1024]{0:T(1024)} %copy-done.65) | copy-start | bytes 12292
  484.3 36.5 %collective-permute-start.10 = (bf16[512,1536]{1,0:T(8,128)(2,1)S(1)}, bf16[512,1536]{1,0:T(8,128)(2,1)S(1)}, u32[]{:S(2)}, u32[]{:S(2)}) collective-permute-start(bf16[512,1536]{1,0:T(8,128)(2,1)S(1)} %fusion.70), channel_id=1, source_target_pairs={{0,2},{1,3},{2,0},{3,1},{4,6},{5,7},{6,4},{7,5},{8,10},{9,11},{10,... | collective-permute-start | bytes 4718600 | tf_op jit(solution)/shard_map/ppermute | solution.py:227
  522.6 19.5 %collective-permute-start.11 = (bf16[512,1536]{1,0:T(8,128)(2,1)}, bf16[512,1536]{1,0:T(8,128)(2,1)}, u32[]{:S(2)}, u32[]{:S(2)}) collective-permute-start(bf16[512,1536]{1,0:T(8,128)(2,1)} %fusion.111), channel_id=1, source_target_pairs={{0,1},{1,0},{2,3},{3,2},{4,5},{5,4},{6,7},{7,6},{8,9},{9,8},{10,11... | collective-permute-start | bytes 4718600 | tf_op jit(solution)/shard_map/ppermute | solution.py:228
  563.6 17.1 %collective-permute-start.12 = (bf16[192,1544]{1,0:T(8,128)(2,1)}, bf16[192,1544]{1,0:T(8,128)(2,1)}, u32[]{:S(2)}, u32[]{:S(2)}) collective-permute-start(bf16[192,1544]{1,0:T(8,128)(2,1)} %get-tuple-element.197), channel_id=1, source_target_pairs={{0,8},{8,16},{16,24},{24,28},{28,20},{20,12},{12,4},{4,0},{1,9},{9... | collective-permute-start | bytes 1778696 | tf_op jit(solution)/shard_map/ppermute | solution.py:204
  564.8 21.0 %collective-permute-start.16 = (bf16[192,1544]{1,0:T(8,128)(2,1)}, bf16[192,1544]{1,0:T(8,128)(2,1)}, u32[]{:S(2)}, u32[]{:S(2)}) collective-permute-start(bf16[192,1544]{1,0:T(8,128)(2,1)} %get-tuple-element.198), channel_id=1, source_target_pairs={{0,4},{8,0},{16,8},{24,16},{28,24},{20,28},{12,20},{4,12},{1,5},{9... | collective-permute-start | bytes 1778696 | tf_op jit(solution)/shard_map/ppermute | solution.py:208
  583.1 16.2 %collective-permute-start.13 = (bf16[192,1544]{1,0:T(8,128)(2,1)}, bf16[192,1544]{1,0:T(8,128)(2,1)}, u32[]{:S(2)}, u32[]{:S(2)}) collective-permute-start(bf16[192,1544]{1,0:T(8,128)(2,1)} %add_convert_fusion.6), channel_id=1, source_target_pairs={{0,8},{8,16},{16,24},{24,28},{28,20},{20,12},{12,4},{4,0},{1,9},{9... | collective-permute-start | bytes 1778696 | tf_op jit(solution)/shard_map/ppermute | solution.py:204
  602.6 15.4 %collective-permute-start.14 = (bf16[192,1544]{1,0:T(8,128)(2,1)}, bf16[192,1544]{1,0:T(8,128)(2,1)}, u32[]{:S(2)}, u32[]{:S(2)}) collective-permute-start(bf16[192,1544]{1,0:T(8,128)(2,1)} %get-tuple-element.195), channel_id=1, source_target_pairs={{0,8},{8,16},{16,24},{24,28},{28,20},{20,12},{12,4},{4,0},{1,9},{9... | collective-permute-start | bytes 1778696 | tf_op jit(solution)/shard_map/ppermute | solution.py:204
  603.2 15.5 %collective-permute-start.17 = (bf16[192,1544]{1,0:T(8,128)(2,1)}, bf16[192,1544]{1,0:T(8,128)(2,1)}, u32[]{:S(2)}, u32[]{:S(2)}) collective-permute-start(bf16[192,1544]{1,0:T(8,128)(2,1)} %get-tuple-element.196), channel_id=1, source_target_pairs={{0,4},{8,0},{16,8},{24,16},{28,24},{20,28},{12,20},{4,12},{1,5},{9... | collective-permute-start | bytes 1778696 | tf_op jit(solution)/shard_map/ppermute | solution.py:208
  621.0 15.3 %collective-permute-start.15 = (bf16[192,1544]{1,0:T(8,128)(2,1)S(1)}, bf16[192,1544]{1,0:T(8,128)(2,1)S(1)}, u32[]{:S(2)}, u32[]{:S(2)}) collective-permute-start(bf16[192,1544]{1,0:T(8,128)(2,1)S(1)} %get-tuple-element.193), channel_id=1, source_target_pairs={{0,8},{8,16},{16,24},{24,28},{28,20},{20,12},{12,4},{4,0},{1,9},{9... | collective-permute-start | bytes 1778696 | tf_op jit(solution)/shard_map/ppermute | solution.py:204
  622.8 13.7 %collective-permute-start.18 = (bf16[192,1544]{1,0:T(8,128)(2,1)S(1)}, bf16[192,1544]{1,0:T(8,128)(2,1)S(1)}, u32[]{:S(2)}, u32[]{:S(2)}) collective-permute-start(bf16[192,1544]{1,0:T(8,128)(2,1)S(1)} %get-tuple-element.194), channel_id=1, source_target_pairs={{0,4},{8,0},{16,8},{24,16},{28,24},{20,28},{12,20},{4,12},{1,5},{9... | collective-permute-start | bytes 1778696 | tf_op jit(solution)/shard_map/ppermute | solution.py:208
  (88 other events, 873.1 us)
Sparse Core Ops, SparseCore 0:
  11.0 101.4 all-gather.2
  114.6 140.4 all-gather.4
  364.7 184.2 reduce-scatter.1

commit v3 on v2

--- a/solution.py
+++ b/solution.py
@@ -40,14 +40,20 @@
     return (places[None, :] <= places[:, None]) | same
 
 
+def key_reach(first_row, block_rows, length, slots):
+    width = length // slots
+    return min(length, -(-(first_row + block_rows) // width) * width)
+
+
 def block_scores(query_rows, key_all, decay, allowed_rows, first_row):
     count = query_rows.shape[0]
+    reach = key_all.shape[0]
     raw = jnp.einsum(
         "qhd,khd->hqk", query_rows, key_all, preferred_element_type=jnp.float32
     ) * query_rows.shape[-1] ** (-0.5)
     apart = (
         lax.slice_in_dim(decay, first_row, first_row + count, axis=1)[:, :, None]
-        - decay[:, None, :]
+        - decay[:, None, :reach]
     )
     return (jnp.where(allowed_rows[None], raw - jnp.abs(apart), masked_value), apart)
 
@@ -61,11 +67,12 @@
     results = []
     normalizers = []
     for first_row in range(0, length, block_rows):
+        reach = key_reach(first_row, block_rows, length, starts.shape[0])
         scores, apart = block_scores(
             query_all[first_row : first_row + block_rows],
-            key_all,
+            key_all[:reach],
             decay,
-            allowed[first_row : first_row + block_rows],
+            allowed[first_row : first_row + block_rows, :reach],
             first_row,
         )
         largest = jnp.max(scores, axis=-1, keepdims=True)
@@ -73,7 +80,9 @@
         denominator = jnp.sum(weights, axis=-1, keepdims=True)
         chances = (weights / denominator).astype(jnp.bfloat16)
         results.append(
-            jnp.einsum("hqk,khd->qhd", chances, value_all, preferred_element_type=jnp.float32)
+            jnp.einsum(
+                "hqk,khd->qhd", chances, value_all[:reach], preferred_element_type=jnp.float32
+            )
         )
         normalizers.append(largest + jnp.log(denominator))
     return (jnp.concatenate(results, axis=0), jnp.concatenate(normalizers, axis=1))
@@ -92,39 +101,44 @@
     query_parts = []
     row_parts = []
     for first_row in range(0, length, block_rows):
+        reach = key_reach(first_row, block_rows, length, starts.shape[0])
+        key_rows = key_all[:reach]
+        value_rows = value_all[:reach]
         query_rows = query_all[first_row : first_row + block_rows]
         out_rows = grad_out[first_row : first_row + block_rows]
         scores, apart = block_scores(
-            query_rows, key_all, decay, allowed[first_row : first_row + block_rows], first_row
+            query_rows, key_rows, decay, allowed[first_row : first_row + block_rows, :reach],
+            first_row,
         )
         chances = jnp.exp(scores - normalizer[:, first_row : first_row + block_rows])
         grad_chance = jnp.einsum(
-            "qhd,khd->hqk", out_rows, value_all, preferred_element_type=jnp.float32
+            "qhd,khd->hqk", out_rows, value_rows, preferred_element_type=jnp.float32
         )
         offset = jnp.sum(
             out_rows.astype(jnp.float32) * attended[first_row : first_row + block_rows], axis=-1
         ).T[:, :, None]
         grad_score = chances * (grad_chance - offset)
         grad_rounded = grad_score.astype(jnp.bfloat16)
-        grad_value = grad_value + jnp.einsum(
-            "hqk,qhd->khd",
-            chances.astype(jnp.bfloat16),
-            out_rows,
-            preferred_element_type=jnp.float32,
-        )
-        grad_key = (
-            grad_key
-            + jnp.einsum(
+        grad_value = grad_value.at[:reach].add(
+            jnp.einsum(
+                "hqk,qhd->khd",
+                chances.astype(jnp.bfloat16),
+                out_rows,
+                preferred_element_type=jnp.float32,
+            )
+        )
+        grad_key = grad_key.at[:reach].add(
+            jnp.einsum(
                 "hqk,qhd->khd", grad_rounded, query_rows, preferred_element_type=jnp.float32
             )
             * scale
         )
         query_parts.append(
-            jnp.einsum("hqk,khd->qhd", grad_rounded, key_all, preferred_element_type=jnp.float32)
+            jnp.einsum("hqk,khd->qhd", grad_rounded, key_rows, preferred_element_type=jnp.float32)
             * scale
         )
         signed = grad_score * jnp.sign(apart)
-        grad_decay = grad_decay + jnp.sum(signed, axis=1)
+        grad_decay = grad_decay.at[:, :reach].add(jnp.sum(signed, axis=1))
         row_parts.append(-jnp.sum(signed, axis=-1))
     grad_decay = grad_decay + jnp.concatenate(row_parts, axis=1)
     grad_log = jnp.flip(jnp.cumsum(jnp.flip(grad_decay, axis=1), axis=1), axis=1).T
@@ -311,13 +325,18 @@
     )
     grad_up = (grad_inner * gate_part * sigma).astype(jnp.bfloat16)
     grad_gate_up = jnp.concatenate([grad_gate, grad_up], axis=1)
+    grad_down_t = contract_rows(upstream_low, inner)
+    grad_gate_up_w = contract_rows(normed_two, grad_gate_up)
+    ffn_grads = jnp.concatenate([grad_gate_up_w, grad_down_t], axis=1).astype(jnp.bfloat16)
     grad_normed_two = tensor_sum(
         contract_cols(grad_gate_up, gate_up_w).astype(jnp.bfloat16), "tensor"
     )
+    ffn_grads, grad_normed_two = lax.optimization_barrier((ffn_grads, grad_normed_two))
+    ffn_sums = lax.psum_scatter(ffn_grads, "dp", scatter_dimension=0, tiled=True).astype(
+        jnp.float32
+    )
     ffn_term, grad_normed_two = lax.optimization_barrier((ffn_term, grad_normed_two))
     ffn_out = tensor_sum(ffn_term, "tensor")
-    grad_down_t = contract_rows(upstream_low, inner)
-    grad_gate_up_w = contract_rows(normed_two, grad_gate_up)
     grad_ffn_gain = jnp.sum(grad_normed_two * unit_two, axis=0)
     grad_unit_two = grad_normed_two * gain_two
     grad_hidden = upstream + scale_two * (
@@ -325,13 +344,6 @@
     )
     hidden_low = grad_hidden.astype(jnp.bfloat16)
     grad_output_t = contract_rows(hidden_low, gated)
-    early_grads = jnp.concatenate(
-        [grad_gate_up_w, grad_down_t, grad_output_t, grad_ffn_gain[:, None]], axis=1
-    )
-    early_grads, hidden_low = lax.optimization_barrier((early_grads, hidden_low))
-    early_sums = lax.psum_scatter(
-        early_grads.astype(jnp.bfloat16), "dp", scatter_dimension=0, tiled=True
-    ).astype(jnp.float32)
     grad_gated = project(hidden_low, output_t)
     grad_attended = (grad_gated * gate_open).astype(jnp.bfloat16)
     grad_gate_pre = (grad_gated * attended_flat * gate_open * (1.0 - gate_open)).astype(
@@ -374,8 +386,19 @@
     grad_normed = tensor_sum(contract_cols(grad_five, joined_five).astype(jnp.bfloat16), "tensor")
     grad_attn_gain = jnp.sum(grad_normed * unit_one, axis=0)
     late_sums = ring_reduce_scatter(
-        jnp.concatenate([late_grads, bias_col[:, None], grad_attn_gain[:, None]], axis=1), "dp"
-    )
+        jnp.concatenate(
+            [
+                late_grads,
+                bias_col[:, None],
+                grad_attn_gain[:, None],
+                grad_ffn_gain[:, None],
+                grad_output_t,
+            ],
+            axis=1,
+        ),
+        "dp",
+    )
+    out_at = 4 * share_width + heads_here + 3
     grad_unit_one = grad_normed * gain_one
     grad_inputs = grad_hidden + scale_one * (
         grad_unit_one - unit_one * jnp.mean(grad_unit_one * unit_one, axis=-1, keepdims=True)
@@ -392,11 +415,11 @@
         late_sums[:, 3 * share_width : 4 * share_width],
         late_sums[:, forget_at : forget_at + heads_here],
         late_sums[:heads_here, forget_at + heads_here],
-        early_sums[:, 3 * units : 3 * units + share_width].T,
-        early_sums[:, 3 * units + share_width],
-        early_sums[:, :units],
-        early_sums[:, units : 2 * units],
-        early_sums[:, 2 * units : 3 * units].T,
+        late_sums[:, out_at : out_at + share_width].T,
+        late_sums[:, out_at - 1],
+        ffn_sums[:, :units],
+        ffn_sums[:, units : 2 * units],
+        ffn_sums[:, 2 * units : 3 * units].T,
     )
 
 

time: 658 us -> 655 us (level)
  matrix products: 156 us -> 134 us
  local copies, waits for them, and re-layouts: 71.1 us -> 89.6 us
  other arithmetic: 101 us -> 116 us
  waiting for transfers between devices: 291 us -> 276 us
    ppermute x4, waiting for transfers between devices: 127 us -> 101 us  [tensor_sum(): lax.ppermute(mine.astype(term.dtype), axis, across).astype(jnp.float32)]
    ppermute x4, waiting for transfers between devices: 37.8 us -> 51 us  [ring_reduce_scatter(): part_next = lax.ppermute(part_next.astype(jnp.bfloat16), axis, to_next)]
    dot_general x6, matrix products: 38.3 us -> 26.4 us  [the longest x2 17.5 us: attend_backward(): jnp.einsum('qhd,khd->hqk', out_rows, value_rows, preferred_element_type=j...]
    reshape x1, other arithmetic: 13.2 us -> 3.72 us  [on_device(): tokens_grad = grad_inputs.astype(jnp.bfloat16).reshape(tokens.shape)]
    reshape x0 -> x1, other arithmetic: none -> 7.7 us  [on_device(): output = (hidden + ffn_out).astype(jnp.bfloat16).reshape(tokens.shape)]
    unnamed x204 -> x220, local copies, waits for them, and re-layouts: 12.3 us -> 16.6 us
  transfers between devices with their start and end apart: 22 -> 22, of which waited for: 15 -> 16; matrix products, arithmetic and copies ran while one was open for 42% -> 44% of each run, Pallas kernels for 0% -> 0%
where the time goes in v3:
time: 655 us; the launch traced here: 649 us
  waiting for transfers between devices  276 us (42%)
  matrix products  134 us (20%)
  other arithmetic  116 us (18%)
  local copies, waits for them, and re-layouts  89.6 us (14%)
  between operations  20 us (3%)
  starting transfers between devices  14 us (2%)
    ppermute x4, waiting for transfers between devices, tensor_sum(): lax.ppermute(mine.astype(term.dtype), axis, across).astype(jnp.float32)  101 us
    all_gather x1, waiting for transfers between devices, on_device(): attn_full = lax.all_gather(attn_local, 'dp', axis=0, tiled=True)  91.1 us
    ppermute x4, waiting for transfers between devices, ring_reduce_scatter(): part_next = lax.ppermute(part_next.astype(jnp.bfloat16), axis, to_next)  51 us
    dot_general x5, matrix products, project(): return jnp.dot(left, right, preferred_element_type=jnp.float32)  35 us
    dot_general x4, matrix products, contract_rows(): lax.dot_general(left, right, (((0,), (0,)), ((), ())), preferred_element_...  25.5 us
    dot_general x4, matrix products, contract_cols(): lax.dot_general(left, right, (((1,), (1,)), ((), ())), preferred_element_...  24 us
    all_gather x1, waiting for transfers between devices, on_device(): ffn_full = lax.all_gather(ffn_local, 'dp', axis=0, tiled=True)  19 us
    dot_general x2, matrix products, attend_backward(): jnp.einsum('qhd,khd->hqk', out_rows, value_rows, preferred_element_type=j...  17.5 us
  transfers between devices with their start and end apart: 22, of which 16 were waited for; matrix products, arithmetic and copies ran while one was open for 44% of the time, Pallas kernels for 0%

profile of v3, /device:TPU:0, one launch (start us, length us, event | category | flops | bytes accessed | tf_op | source)
XLA Modules:
  0.0 649.4 jit_solution(2534613210706926436)
XLA Ops:
  21.6 91.1 %all-gather.3.cloned.1.call-done = bf16[1536,1927]{1,0:T(8,128)(2,1)} async-done(((bf16[192,1927]{1,0:T(8,128)(2,1)}), bf16[1536,1927]{1,0:T(8,128)(2,1)}) %all-gather.3.cloned.1.call-update) | async-done | bytes 5919760 | tf_op jit(solution)/shard_map/all_gather | solution.py:279
  119.6 10.1 %fusion.148 = (bf16[1024,1536]{1,0:T(8,128)(2,1)S(1)}, f32[1024,1536]{1,0:T(8,128)}) fusion(bf16[1536,1927]{1,0:T(8,128)(2,1)} %all-gather.3.cloned.1.call-done, bf16[1,1024,1536]{2,1,0:T(8,128)(2,1)S(1)} %copy-done.3, f32[1536]{0:T(1024)S(1)} %convert_reduce_fusion.1, f32[1024]{0:T(1024)S(1)} %add_rsqrt_fusion.1), kind=kOutput, calls=%fused_computation.236 | convolution fusion | flops 4839702528 | bytes 17311744 | tf_op jit(solution)/shard_map/dot_general | solution.py:14
  152.1 3.9 fusion.149
  160.8 4.0 fusion.100
  187.0 34.8 %collective-permute-done.1 = bf16[512,1536]{1,0:T(8,128)(2,1)S(1)} collective-permute-done((bf16[512,1536]{1,0:T(8,128)(2,1)S(1)}, bf16[512,1536]{1,0:T(8,128)(2,1)S(1)}, u32[]{:S(2)}, u32[]{:S(2)}) %collective-permute-start.1) | collective-permute-done | bytes 1572896 | tf_op jit(solution)/shard_map/ppermute | solution.py:241
  236.3 19.0 %all-gather.5.cloned.1.call-done = bf16[1536,3073]{1,0:T(8,128)(2,1)} async-done(((bf16[192,3073]{1,0:T(8,128)(2,1)}), bf16[1536,3073]{1,0:T(8,128)(2,1)}) %all-gather.5.cloned.1.call-update) | async-done | bytes 9440272 | tf_op jit(solution)/shard_map/all_gather | solution.py:287
  256.5 10.8 %fusion.30 = f32[1024,2048]{1,0:T(8,128)S(1)} fusion(bf16[1536,3073]{1,0:T(8,128)(2,1)} %all-gather.5.cloned.1.call-done, f32[1024,1536]{1,0:T(8,128)} %get-tuple-element.316, f32[1536]{0:T(1024)S(1)} %convert_reduce_fusion, f32[1024]{0:T(1024)S(1)} %add_rsqrt_fusion), kind=kOutput, calls=%fused_computation.55 | convolution fusion | flops 6447169536 | bytes 20981760 | tf_op jit(solution)/shard_map/dot_general | solution.py:14
  267.3 6.2 fusion.40
  273.6 7.3 %fusion.47 = bf16[1024,1536]{1,0:T(8,128)(2,1)S(1)} fusion(bf16[1536,3073]{1,0:T(8,128)(2,1)S(1)} %copy-done.75, bf16[1024,1024]{1,0:T(8,128)(2,1)S(1)} %get-tuple-element.324, bf16[1024,1024]{1,0:T(8,128)(2,1)S(1)} %get-tuple-element.323), kind=kOutput, calls=%fused_computation.84 | convolution fusion | flops 6452412416 | bytes 13631488 | tf_op jit(solution)/shard_map/dot_general | solution.py:24
  290.3 9.6 %convolution_convert_fusion = bf16[1536,2048]{1,0:T(8,128)(2,1)S(1)} fusion(bf16[1024,1024]{1,0:T(8,128)(2,1)} %copy-done.86, bf16[1024,1024]{1,0:T(8,128)(2,1)} %copy-done.85, f32[1024,1536]{1,0:T(8,128)S(1)} %bitcast.169, f32[1536]{0:T(1024)S(1)} %convert_reduce_fusion, f32[1024]{0:T(1024)S(1)} %add_rsqrt_fusion), kind=kOutput, calls=%fused_computation.23 | convolution fusion | flops 6458703872 | bytes 16787456 | tf_op jit(solution)/shard_map/dot_general | solution.py:18
  299.9 21.5 %collective-permute-done.4 = bf16[512,1536]{1,0:T(8,128)(2,1)S(1)} collective-permute-done((bf16[512,1536]{1,0:T(8,128)(2,1)S(1)}, bf16[512,1536]{1,0:T(8,128)(2,1)S(1)}, u32[]{:S(2)}, u32[]{:S(2)}) %collective-permute-start.4) | collective-permute-done | bytes 1572896 | tf_op jit(solution)/shard_map/ppermute | solution.py:241
  323.2 6.7 %convolution_convert_fusion.3 = bf16[1024,1536]{1,0:T(8,128)(2,1)} fusion(bf16[1024,1024]{1,0:T(8,128)(2,1)S(1)} %copy-done.88, bf16[1536,3073]{1,0:T(8,128)(2,1)} %all-gather.5.cloned.1.call-done), kind=kOutput, calls=%fused_computation.87 | convolution fusion | flops 3222798336 | bytes 8388608 | tf_op jit(solution)/shard_map/dot_general | solution.py:24
  329.9 4.8 pad_maximum_fusion
  340.6 6.2 multiply_reduce_fusion
  355.2 5.9 multiply_convert_fusion.3
  366.0 12.5 %fusion.6 = (f32[6,1024]{1,0:T(8,128)S(1)}, f32[6,512]{1,0:T(8,128)S(1)}, bf16[6,512,1024]{2,1,0:T(8,128)(2,1)}) fusion(f32[6,1024]{1,0:T(8,128)S(1)} %bitcast.209, f32[6,512]{1,0:T(8,128)S(1)} %copy-done.73, f32[6,512]{1,0:T(8,128)S(1)} %bitcast.217, bf16[512,6,64]{0,2,1:T(8,128)(2,1)S(1)} %bitcast.188, bf16[1024,6,64]{0,2,1:T(8,128)(2,1)} %bitcast.201, ...), kind=kOutput, calls=%fused_computation.12 | convolution fusion | flops 430955520 | bytes 20152320 | tf_op jit(solution)/shard_map/while/body/eval_jaxpr/qhd,khd->hqk/dot_general | solution.py:114
  378.5 5.1 fusion.33
  387.7 4.4 fusion.93
  392.1 4.3 fusion.97
  417.0 19.2 %collective-permute-done.7 = bf16[512,1536]{1,0:T(8,128)(2,1)} collective-permute-done((bf16[512,1536]{1,0:T(8,128)(2,1)}, bf16[512,1536]{1,0:T(8,128)(2,1)}, u32[]{:S(2)}, u32[]{:S(2)}) %collective-permute-start.7) | collective-permute-done | bytes 1572896 | tf_op jit(solution)/shard_map/ppermute | solution.py:241
  441.0 4.2 fusion.74
  451.8 4.3 convert_select_fusion.3
  459.6 6.6 %fusion.44 = bf16[1024,1536]{1,0:T(8,128)(2,1)S(1)} fusion(bf16[1024,1542]{1,0:T(8,128)(2,1)S(1)} %constant_dynamic-update-slice_fusion, bf16[1536,1927]{1,0:T(8,128)(2,1)S(1)} %bitcast.215), kind=kOutput, calls=%fused_computation.83 | convolution fusion | flops 4852285440 | bytes 11665408 | tf_op jit(solution)/shard_map/dot_general | solution.py:24
  478.3 5.6 fusion.113
  483.9 25.8 %collective-permute-done.10 = bf16[512,1536]{1,0:T(8,128)(2,1)} collective-permute-done((bf16[512,1536]{1,0:T(8,128)(2,1)}, bf16[512,1536]{1,0:T(8,128)(2,1)}, u32[]{:S(2)}, u32[]{:S(2)}) %collective-permute-start.10) | collective-permute-done | bytes 1572896 | tf_op jit(solution)/shard_map/ppermute | solution.py:241
  516.1 8.9 %fusion.137 = f32[1536,1542]{1,0:T(8,128)} fusion(bf16[1024,1542]{1,0:T(8,128)(2,1)S(1)} %copy-done.51, bf16[1,1024,1536]{2,1,0:T(8,128)(2,1)S(1)} %copy-done.4, f32[1536]{0:T(1024)S(1)} %copy-done.58, f32[1024]{0:T(1024)S(1)} %copy-done.68), kind=kOutput, calls=%fused_computation.229 | convolution fusion | flops 4857004032 | bytes 15788032 | tf_op jit(solution)/shard_map/dot_general | solution.py:18
  531.3 15.0 %concatenate.81 = f32[1536,1929]{1,0:T(8,128)} concatenate(f32[1536,1542]{1,0:T(8,128)} %fusion.137, f32[1536,1]{1,0:T(8,128)} %fusion.113, f32[1536,1]{1,0:T(8,128)} %broadcast_in_dim.210, f32[1536,1]{1,0:T(8,128)} %broadcast_in_dim.211, f32[1536,384]{1,0:T(8,128)} %fusion.79), dimensions={1} | concatenate | bytes 23703552 | tf_op jit(solution)/shard_map/concatenate | solution.py:389
  553.0 16.9 %collective-permute-done.12 = bf16[192,1929]{1,0:T(8,128)(2,1)} collective-permute-done((bf16[192,1929]{1,0:T(8,128)(2,1)}, bf16[192,1929]{1,0:T(8,128)(2,1)}, u32[]{:S(2)}, u32[]{:S(2)}) %collective-permute-start.12) | collective-permute-done | bytes 740768 | tf_op jit(solution)/shard_map/ppermute | solution.py:218
  577.9 14.1 %collective-permute-done.13 = bf16[192,1929]{1,0:T(8,128)(2,1)} collective-permute-done((bf16[192,1929]{1,0:T(8,128)(2,1)}, bf16[192,1929]{1,0:T(8,128)(2,1)}, u32[]{:S(2)}, u32[]{:S(2)}) %collective-permute-start.13) | collective-permute-done | bytes 740768 | tf_op jit(solution)/shard_map/ppermute | solution.py:218
  596.8 7.7 %fusion.53 = bf16[1,1024,1536]{2,1,0:T(8,128)(2,1)} fusion(f32[1024,1536]{1,0:T(8,128)} %get-tuple-element.316, f32[1024,1536]{1,0:T(8,128)} %pad_maximum_fusion.2), kind=kLoop, calls=%fused_computation.90 | loop fusion | flops 3145728 | bytes 15728640 | tf_op jit(solution)/shard_map/reshape | solution.py:379
  604.5 8.5 %collective-permute-done.14 = bf16[192,1929]{1,0:T(8,128)(2,1)S(1)} collective-permute-done((bf16[192,1929]{1,0:T(8,128)(2,1)S(1)}, bf16[192,1929]{1,0:T(8,128)(2,1)S(1)}, u32[]{:S(2)}, u32[]{:S(2)}) %collective-permute-start.14) | collective-permute-done | bytes 740768 | tf_op jit(solution)/shard_map/ppermute | solution.py:218
  621.8 11.6 %collective-permute-done.15 = bf16[192,1929]{1,0:T(8,128)(2,1)S(1)} collective-permute-done((bf16[192,1929]{1,0:T(8,128)(2,1)S(1)}, bf16[192,1929]{1,0:T(8,128)(2,1)S(1)}, u32[]{:S(2)}, u32[]{:S(2)}) %collective-permute-start.15) | collective-permute-done | bytes 740768 | tf_op jit(solution)/shard_map/ppermute | solution.py:218
  (381 shorter events, 213.0 us)
Async XLA Ops:
  7.2 105.4 %all-gather.3.cloned.1.call-start = ((), (), s32[]{:S(2)}) async-start(), calls=%async_computation.1 | async-start | bytes 7077888 | tf_op jit(solution)/shard_map/all_gather | solution.py:279
  11.1 244.2 %all-gather.5.cloned.1.call-start = ((), (), s32[]{:S(2)}) async-start(), calls=%async_computation.2 | async-start | bytes 11059200 | tf_op jit(solution)/shard_map/all_gather | solution.py:287
  19.4 94.7 %copy-start.77 = (f32[6]{0:T(128)S(1)}, f32[6]{0:T(128)}, u32[]{:S(2)}) copy-start(f32[6]{0:T(128)} %param.48) | copy-start | bytes 76
  112.7 526.1 %reduce-scatter.2.cloned.1.call-start = ((), (), s32[]{:S(2)}) async-start(), calls=%async_computation.3 | async-start | bytes 10616832 | tf_op jit(solution)/shard_map/reduce_scatter | solution.py:335
  179.3 3.8 collective-permute-start
  179.3 42.5 %copy-start.19 = (bf16[1024,1536]{1,0:T(8,128)(2,1)S(1)}, bf16[1024,1536]{1,0:T(8,128)(2,1)}, u32[]{:S(2)}) copy-start(bf16[1024,1536]{1,0:T(8,128)(2,1)} %copy-done.18) | copy-start | bytes 9437188
  185.3 36.5 %collective-permute-start.1 = (bf16[512,1536]{1,0:T(8,128)(2,1)S(1)}, bf16[512,1536]{1,0:T(8,128)(2,1)S(1)}, u32[]{:S(2)}, u32[]{:S(2)}) collective-permute-start(bf16[512,1536]{1,0:T(8,128)(2,1)S(1)} %fusion.64), channel_id=1, source_target_pairs={{0,2},{1,3},{2,0},{3,1},{4,6},{5,7},{6,4},{7,5},{8,10},{9,11},{10,... | collective-permute-start | bytes 4718600 | tf_op jit(solution)/shard_map/ppermute | solution.py:241
  225.5 3.8 collective-permute-start.2
  280.9 40.6 %copy-start.17 = (bf16[1024,1536]{1,0:T(8,128)(2,1)}, bf16[1024,1536]{1,0:T(8,128)(2,1)S(1)}, u32[]{:S(2)}) copy-start(bf16[1024,1536]{1,0:T(8,128)(2,1)S(1)} %fusion.47) | copy-start | bytes 9437188
  281.1 3.5 collective-permute-start.3
  284.9 36.5 %collective-permute-start.4 = (bf16[512,1536]{1,0:T(8,128)(2,1)S(1)}, bf16[512,1536]{1,0:T(8,128)(2,1)S(1)}, u32[]{:S(2)}, u32[]{:S(2)}) collective-permute-start(bf16[512,1536]{1,0:T(8,128)(2,1)S(1)} %fusion.65), channel_id=1, source_target_pairs={{0,2},{1,3},{2,0},{3,1},{4,6},{5,7},{6,4},{7,5},{8,10},{9,11},{10,... | collective-permute-start | bytes 4718600 | tf_op jit(solution)/shard_map/ppermute | solution.py:241
  323.2 11.5 %collective-permute-start.5 = (bf16[512,1536]{1,0:T(8,128)(2,1)}, bf16[512,1536]{1,0:T(8,128)(2,1)}, u32[]{:S(2)}, u32[]{:S(2)}) collective-permute-start(bf16[512,1536]{1,0:T(8,128)(2,1)} %fusion.123), channel_id=1, source_target_pairs={{0,1},{1,0},{2,3},{3,2},{4,5},{5,4},{6,7},{7,6},{8,9},{9,8},{10,11... | collective-permute-start | bytes 4718600 | tf_op jit(solution)/shard_map/ppermute | solution.py:242
  354.6 41.8 %collective-permute-start.6 = (bf16[512,1536]{1,0:T(8,128)(2,1)}, bf16[512,1536]{1,0:T(8,128)(2,1)}, u32[]{:S(2)}, u32[]{:S(2)}) collective-permute-start(bf16[512,1536]{1,0:T(8,128)(2,1)} %constant_dynamic-slice_fusion.1), channel_id=1, source_target_pairs={{0,1},{1,0},{2,3},{3,2},{4,5},{5,4},{6,7},{7,6},{8,9},{9,8},{10,11... | collective-permute-start | bytes 4718600 | tf_op jit(solution)/shard_map/ppermute | solution.py:240
  399.5 36.7 %collective-permute-start.7 = (bf16[512,1536]{1,0:T(8,128)(2,1)}, bf16[512,1536]{1,0:T(8,128)(2,1)}, u32[]{:S(2)}, u32[]{:S(2)}) collective-permute-start(bf16[512,1536]{1,0:T(8,128)(2,1)} %fusion.66), channel_id=1, source_target_pairs={{0,2},{1,3},{2,0},{3,1},{4,6},{5,7},{6,4},{7,5},{8,10},{9,11},{10,... | collective-permute-start | bytes 4718600 | tf_op jit(solution)/shard_map/ppermute | solution.py:241
  440.0 11.5 %collective-permute-start.8 = (bf16[512,1536]{1,0:T(8,128)(2,1)}, bf16[512,1536]{1,0:T(8,128)(2,1)}, u32[]{:S(2)}, u32[]{:S(2)}) collective-permute-start(bf16[512,1536]{1,0:T(8,128)(2,1)} %fusion.124), channel_id=1, source_target_pairs={{0,1},{1,0},{2,3},{3,2},{4,5},{5,4},{6,7},{7,6},{8,9},{9,8},{10,11... | collective-permute-start | bytes 4718600 | tf_op jit(solution)/shard_map/ppermute | solution.py:242
  466.2 46.5 %slice-start.4 = ((s8[6291456]{0:T(1024)(128)(4,1)}), s8[2097152]{0:T(1024)(128)(4,1)S(1)}, s32[]{:S(2)}) async-start(s8[6291456]{0:T(1024)(128)(4,1)} %bitcast.172), calls=%async_computation.8 | async-start | bytes 4194304
  466.4 3.6 collective-permute-start.9
  472.7 37.0 %collective-permute-start.10 = (bf16[512,1536]{1,0:T(8,128)(2,1)}, bf16[512,1536]{1,0:T(8,128)(2,1)}, u32[]{:S(2)}, u32[]{:S(2)}) collective-permute-start(bf16[512,1536]{1,0:T(8,128)(2,1)} %fusion.67), channel_id=1, source_target_pairs={{0,2},{1,3},{2,0},{3,1},{4,6},{5,7},{6,4},{7,5},{8,10},{9,11},{10,... | collective-permute-start | bytes 4718600 | tf_op jit(solution)/shard_map/ppermute | solution.py:241
  476.5 36.2 %slice-start.5 = ((s8[6291456]{0:T(1024)(128)(4,1)}), s8[4194304]{0:T(1024)(128)(4,1)S(1)}, s32[]{:S(2)}) async-start(s8[6291456]{0:T(1024)(128)(4,1)} %bitcast.172), calls=%async_computation.9 | async-start | bytes 8388608
  483.9 28.9 %copy-start.34 = (bf16[1024,384]{1,0:T(8,128)(2,1)S(1)}, bf16[1024,384]{1,0:T(8,128)(2,1)}, u32[]{:S(2)}) copy-start(bf16[1024,384]{1,0:T(8,128)(2,1)} %copy-done.33) | copy-start | bytes 2359300
  512.6 12.3 %collective-permute-start.11 = (bf16[512,1536]{1,0:T(8,128)(2,1)S(1)}, bf16[512,1536]{1,0:T(8,128)(2,1)S(1)}, u32[]{:S(2)}, u32[]{:S(2)}) collective-permute-start(bf16[512,1536]{1,0:T(8,128)(2,1)S(1)} %fusion.125), channel_id=1, source_target_pairs={{0,1},{1,0},{2,3},{3,2},{4,5},{5,4},{6,7},{7,6},{8,9},{9,8},{10,11... | collective-permute-start | bytes 4718600 | tf_op jit(solution)/shard_map/ppermute | solution.py:242
  546.3 26.5 %copy-start.81 = (s32[8]{0:T(128)S(1)}, s32[8]{0:T(128)}, u32[]{:S(2)}) copy-start(s32[8]{0:T(128)} %constant.382.clone) | copy-start | bytes 100
  546.3 27.8 %copy-start.80 = (s32[8]{0:T(128)S(1)}, s32[8]{0:T(128)}, u32[]{:S(2)}) copy-start(s32[8]{0:T(128)} %constant.381.clone) | copy-start | bytes 100
  546.3 29.0 %copy-start.79 = (s32[8]{0:T(128)S(1)}, s32[8]{0:T(128)}, u32[]{:S(2)}) copy-start(s32[8]{0:T(128)} %constant.380.clone) | copy-start | bytes 100
  546.3 30.2 %copy-start.78 = (s32[8]{0:T(128)S(1)}, s32[8]{0:T(128)}, u32[]{:S(2)}) copy-start(s32[8]{0:T(128)} %constant.379.clone) | copy-start | bytes 100
  549.6 20.2 %collective-permute-start.12 = (bf16[192,1929]{1,0:T(8,128)(2,1)}, bf16[192,1929]{1,0:T(8,128)(2,1)}, u32[]{:S(2)}, u32[]{:S(2)}) collective-permute-start(bf16[192,1929]{1,0:T(8,128)(2,1)} %get-tuple-element.321), channel_id=1, source_target_pairs={{0,8},{8,16},{16,24},{24,28},{28,20},{20,12},{12,4},{4,0},{1,9},{9... | collective-permute-start | bytes 2222216 | tf_op jit(solution)/shard_map/ppermute | solution.py:218
  550.9 27.0 %collective-permute-start.16 = (bf16[192,1929]{1,0:T(8,128)(2,1)}, bf16[192,1929]{1,0:T(8,128)(2,1)}, u32[]{:S(2)}, u32[]{:S(2)}) collective-permute-start(bf16[192,1929]{1,0:T(8,128)(2,1)} %get-tuple-element.322), channel_id=1, source_target_pairs={{0,4},{8,0},{16,8},{24,16},{28,24},{20,28},{12,20},{4,12},{1,5},{9... | collective-permute-start | bytes 2222216 | tf_op jit(solution)/shard_map/ppermute | solution.py:222
  572.5 19.4 %collective-permute-start.13 = (bf16[192,1929]{1,0:T(8,128)(2,1)}, bf16[192,1929]{1,0:T(8,128)(2,1)}, u32[]{:S(2)}, u32[]{:S(2)}) collective-permute-start(bf16[192,1929]{1,0:T(8,128)(2,1)} %add_convert_fusion.5), channel_id=1, source_target_pairs={{0,8},{8,16},{16,24},{24,28},{28,20},{20,12},{12,4},{4,0},{1,9},{9... | collective-permute-start | bytes 2222216 | tf_op jit(solution)/shard_map/ppermute | solution.py:218
  594.7 18.3 %collective-permute-start.14 = (bf16[192,1929]{1,0:T(8,128)(2,1)S(1)}, bf16[192,1929]{1,0:T(8,128)(2,1)S(1)}, u32[]{:S(2)}, u32[]{:S(2)}) collective-permute-start(bf16[192,1929]{1,0:T(8,128)(2,1)S(1)} %get-tuple-element.319), channel_id=1, source_target_pairs={{0,8},{8,16},{16,24},{24,28},{28,20},{20,12},{12,4},{4,0},{1,9},{9... | collective-permute-start | bytes 2222216 | tf_op jit(solution)/shard_map/ppermute | solution.py:218
  595.3 18.2 %collective-permute-start.17 = (bf16[192,1929]{1,0:T(8,128)(2,1)S(1)}, bf16[192,1929]{1,0:T(8,128)(2,1)S(1)}, u32[]{:S(2)}, u32[]{:S(2)}) collective-permute-start(bf16[192,1929]{1,0:T(8,128)(2,1)S(1)} %get-tuple-element.320), channel_id=1, source_target_pairs={{0,4},{8,0},{16,8},{24,16},{28,24},{20,28},{12,20},{4,12},{1,5},{9... | collective-permute-start | bytes 2222216 | tf_op jit(solution)/shard_map/ppermute | solution.py:222
  616.0 17.4 %collective-permute-start.15 = (bf16[192,1929]{1,0:T(8,128)(2,1)S(1)}, bf16[192,1929]{1,0:T(8,128)(2,1)S(1)}, u32[]{:S(2)}, u32[]{:S(2)}) collective-permute-start(bf16[192,1929]{1,0:T(8,128)(2,1)S(1)} %get-tuple-element.317), channel_id=1, source_target_pairs={{0,8},{8,16},{16,24},{24,28},{28,20},{20,12},{12,4},{4,0},{1,9},{9... | collective-permute-start | bytes 2222216 | tf_op jit(solution)/shard_map/ppermute | solution.py:218
  616.8 16.8 %collective-permute-start.18 = (bf16[192,1929]{1,0:T(8,128)(2,1)S(1)}, bf16[192,1929]{1,0:T(8,128)(2,1)S(1)}, u32[]{:S(2)}, u32[]{:S(2)}) collective-permute-start(bf16[192,1929]{1,0:T(8,128)(2,1)S(1)} %get-tuple-element.318), channel_id=1, source_target_pairs={{0,4},{8,0},{16,8},{24,16},{28,24},{20,28},{12,20},{4,12},{1,5},{9... | collective-permute-start | bytes 2222216 | tf_op jit(solution)/shard_map/ppermute | solution.py:222
  (96 other events, 697.1 us)
Sparse Core Ops, SparseCore 0:
  11.2 101.4 all-gather.2
  114.8 140.4 all-gather.4
  340.7 160.4 reduce-scatter.1

commit v4 on v3

--- a/solution.py
+++ b/solution.py
@@ -375,14 +375,15 @@
         ],
         axis=1,
     )
-    ffn_out, grad_five = lax.optimization_barrier((ffn_out, grad_five))
     output = (hidden + ffn_out).astype(jnp.bfloat16).reshape(tokens.shape)
     grad_bias = jnp.sum(grad_forget.astype(jnp.float32), axis=0)
     place = jnp.arange(width, dtype=jnp.int32) % block
     bias_col = jnp.where(
         place < heads_here, jnp.take(grad_bias, jnp.minimum(place, heads_here - 1)), 0.0
     )
-    late_grads = contract_rows(normed, grad_five)
+    late_grads = lax.dot_general(
+        grad_five, normed, (((0,), (0,)), ((), ())), preferred_element_type=jnp.float32
+    ).T
     grad_normed = tensor_sum(contract_cols(grad_five, joined_five).astype(jnp.bfloat16), "tensor")
     grad_attn_gain = jnp.sum(grad_normed * unit_one, axis=0)
     late_sums = ring_reduce_scatter(

time: 655 us -> 632 us (0.965)
  waiting for transfers between devices: 276 us -> 247 us
  matrix products: 134 us -> 144 us
  other arithmetic: 116 us -> 108 us
    ppermute x4, waiting for transfers between devices: 101 us -> 75.5 us  [tensor_sum(): lax.ppermute(mine.astype(term.dtype), axis, across).astype(jnp.float32)]
    dot_general x0 -> x1, matrix products: none -> 8.82 us  [on_device(): lax.dot_general(grad_five, normed, (((0,), (0,)), ((), ())), preferred_el...]
    reshape x1 -> x0, other arithmetic: 7.7 us -> none  [on_device(): output = (hidden + ffn_out).astype(jnp.bfloat16).reshape(tokens.shape)]
    dot_general x4 -> x3, matrix products: 25.5 us -> 19.6 us  [contract_rows(): lax.dot_general(left, right, (((0,), (0,)), ((), ())), preferred_element_...]
    select_n x4 -> x3, other arithmetic: 13.2 us -> 9.13 us  [tensor_sum(): first = jnp.where(core == 0, total, back)]
    unnamed x220 -> x212, local copies, waits for them, and re-layouts: 16.6 us -> 19.2 us
  transfers between devices with their start and end apart: 22 -> 22, of which waited for: 16 -> 16; matrix products, arithmetic and copies ran while one was open for 44% -> 46% of each run, Pallas kernels for 0% -> 0%
where the time goes in v4:
time: 632 us; the launch traced here: 626 us
  waiting for transfers between devices  247 us (39%)
  matrix products  144 us (23%)
  other arithmetic  108 us (17%)
  local copies, waits for them, and re-layouts  93.9 us (15%)
  between operations  19.9 us (3%)
  starting transfers between devices  13.9 us (2%)
    all_gather x1, waiting for transfers between devices, on_device(): attn_full = lax.all_gather(attn_local, 'dp', axis=0, tiled=True)  91.1 us
    ppermute x4, waiting for transfers between devices, tensor_sum(): lax.ppermute(mine.astype(term.dtype), axis, across).astype(jnp.float32)  75.5 us
    ppermute x4, waiting for transfers between devices, ring_reduce_scatter(): part_next = lax.ppermute(part_next.astype(jnp.bfloat16), axis, to_next)  47.4 us
    dot_general x5, matrix products, project(): return jnp.dot(left, right, preferred_element_type=jnp.float32)  36.1 us
    dot_general x4, matrix products, contract_cols(): lax.dot_general(left, right, (((1,), (1,)), ((), ())), preferred_element_...  27 us
    dot_general x3, matrix products, contract_rows(): lax.dot_general(left, right, (((0,), (0,)), ((), ())), preferred_element_...  19.6 us
    unnamed x212, local copies, waits for them, and re-layouts  19.2 us
    dot_general x2, matrix products, attend_backward(): jnp.einsum('qhd,khd->hqk', out_rows, value_rows, preferred_element_type=j...  17.6 us
  transfers between devices with their start and end apart: 22, of which 16 were waited for; matrix products, arithmetic and copies ran while one was open for 46% of the time, Pallas kernels for 0%

profile of v4, /device:TPU:0, one launch (start us, length us, event | category | flops | bytes accessed | tf_op | source)
XLA Modules:
  0.0 625.6 jit_solution(812888359612878098)
XLA Ops:
  21.6 91.1 %all-gather.3.cloned.1.call-done = bf16[1536,1927]{1,0:T(8,128)(2,1)} async-done(((bf16[192,1927]{1,0:T(8,128)(2,1)}), bf16[1536,1927]{1,0:T(8,128)(2,1)}) %all-gather.3.cloned.1.call-update) | async-done | bytes 5919760 | tf_op jit(solution)/shard_map/all_gather | solution.py:279
  119.6 10.0 %fusion.155 = (bf16[1024,1536]{1,0:T(8,128)(2,1)S(1)}, f32[1024,1536]{1,0:T(8,128)}) fusion(bf16[1536,1927]{1,0:T(8,128)(2,1)} %all-gather.3.cloned.1.call-done, bf16[1,1024,1536]{2,1,0:T(8,128)(2,1)S(1)} %copy-done, f32[1536]{0:T(1024)S(1)} %convert_reduce_fusion.1, f32[1024]{0:T(1024)S(1)} %add_rsqrt_fusion.1), kind=kOutput, calls=%fused_computation.239 | convolution fusion | flops 4839702528 | bytes 17311744 | tf_op jit(solution)/shard_map/dot_general | solution.py:14
  160.7 4.0 fusion.106
  187.0 34.8 %collective-permute-done.1 = bf16[512,1536]{1,0:T(8,128)(2,1)S(1)} collective-permute-done((bf16[512,1536]{1,0:T(8,128)(2,1)S(1)}, bf16[512,1536]{1,0:T(8,128)(2,1)S(1)}, u32[]{:S(2)}, u32[]{:S(2)}) %collective-permute-start.1) | collective-permute-done | bytes 1572896 | tf_op jit(solution)/shard_map/ppermute | solution.py:241
  237.7 17.6 %all-gather.5.cloned.1.call-done = bf16[1536,3073]{1,0:T(8,128)(2,1)} async-done(((bf16[192,3073]{1,0:T(8,128)(2,1)}), bf16[1536,3073]{1,0:T(8,128)(2,1)}) %all-gather.5.cloned.1.call-update) | async-done | bytes 9440272 | tf_op jit(solution)/shard_map/all_gather | solution.py:287
  256.5 10.8 %fusion.35 = f32[1024,2048]{1,0:T(8,128)S(1)} fusion(bf16[1536,3073]{1,0:T(8,128)(2,1)} %all-gather.5.cloned.1.call-done, f32[1024,1536]{1,0:T(8,128)} %get-tuple-element.312, f32[1536]{0:T(1024)S(1)} %convert_reduce_fusion, f32[1024]{0:T(1024)S(1)} %add_rsqrt_fusion), kind=kOutput, calls=%fused_computation.57 | convolution fusion | flops 6447169536 | bytes 20981760 | tf_op jit(solution)/shard_map/dot_general | solution.py:14
  267.3 6.3 fusion.45
  273.6 7.3 %fusion.52 = bf16[1024,1536]{1,0:T(8,128)(2,1)S(1)} fusion(bf16[1536,3073]{1,0:T(8,128)(2,1)S(1)} %copy-done.82, bf16[1024,1024]{1,0:T(8,128)(2,1)S(1)} %get-tuple-element.320, bf16[1024,1024]{1,0:T(8,128)(2,1)S(1)} %get-tuple-element.319), kind=kOutput, calls=%fused_computation.86 | convolution fusion | flops 6452412416 | bytes 13631488 | tf_op jit(solution)/shard_map/dot_general | solution.py:24
  290.4 9.6 %convolution_convert_fusion = bf16[1536,2048]{1,0:T(8,128)(2,1)S(1)} fusion(bf16[1024,1024]{1,0:T(8,128)(2,1)} %copy-done.93, bf16[1024,1024]{1,0:T(8,128)(2,1)} %copy-done.92, f32[1024,1536]{1,0:T(8,128)S(1)} %bitcast.199, f32[1536]{0:T(1024)S(1)} %convert_reduce_fusion, f32[1024]{0:T(1024)S(1)} %add_rsqrt_fusion), kind=kOutput, calls=%fused_computation.25 | convolution fusion | flops 6458703872 | bytes 16787456 | tf_op jit(solution)/shard_map/dot_general | solution.py:18
  300.0 21.5 %collective-permute-done.4 = bf16[512,1536]{1,0:T(8,128)(2,1)S(1)} collective-permute-done((bf16[512,1536]{1,0:T(8,128)(2,1)S(1)}, bf16[512,1536]{1,0:T(8,128)(2,1)S(1)}, u32[]{:S(2)}, u32[]{:S(2)}) %collective-permute-start.4) | collective-permute-done | bytes 1572896 | tf_op jit(solution)/shard_map/ppermute | solution.py:241
  323.3 6.7 %convolution_convert_fusion.3 = bf16[1024,1536]{1,0:T(8,128)(2,1)} fusion(bf16[1024,1024]{1,0:T(8,128)(2,1)S(1)} %copy-done.95, bf16[1536,3073]{1,0:T(8,128)(2,1)} %all-gather.5.cloned.1.call-done), kind=kOutput, calls=%fused_computation.89 | convolution fusion | flops 3222798336 | bytes 8388608 | tf_op jit(solution)/shard_map/dot_general | solution.py:24
  330.0 4.8 pad_maximum_fusion
  340.8 6.2 multiply_reduce_fusion
  353.2 6.9 %multiply_convert_fusion.3 = (bf16[1024,384]{1,0:T(8,128)(2,1)S(1)}, f32[1024,384]{1,0:T(8,128)}) fusion(f32[1024,1536]{1,0:T(8,128)} %get-tuple-element.354, bf16[1536,1927]{1,0:T(8,128)(2,1)} %all-gather.3.cloned.1.call-done, f32[1024,1536]{1,0:T(8,128)S(1)} %multiply_add_fusion), kind=kOutput, calls=%fused_computation.141 | convolution fusion | flops 1211498496 | bytes 11403264 | tf_op jit(solution)/shard_map/dot_general | solution.py:14
  362.2 4.9 fusion.103
  367.1 6.6 %fusion.38 = (f32[6,512]{1,0:T(8,128)}, f32[6,512]{1,0:T(8,128)}, bf16[6,512,512]{1,2,0:T(8,128)(2,1)S(1)}) fusion(f32[6,512]{1,0:T(8,128)S(1)} %copy-done.81, f32[6,512]{1,0:T(8,128)S(1)} %bitcast.237, bf16[512,6,64]{0,2,1:T(8,128)(2,1)S(1)} %bitcast.208, bf16[512,6,64]{0,2,1:T(8,128)(2,1)S(1)} %bitcast.227, f32[6,512,512]{1,2,0:T(8,128)} %copy-done.14, ...), kind=kOutput, calls=%fused_computation.60 | convolution fusion | flops 215476224 | bytes 10285056 | tf_op jit(solution)/shard_map/while/body/eval_jaxpr/qhd,khd->hqk/dot_general | solution.py:114
  377.0 7.3 %fusion.79 = bf16[1024,6,64]{0,2,1:T(8,128)(2,1)} fusion(f32[512,6,64]{0,2,1:T(8,128)} %fusion.103, bf16[512,6,64]{0,2,1:T(8,128)(2,1)S(1)} %bitcast.210, f32[6,512,1024]{2,1,0:T(8,128)} %copy-done.4, f32[6,512]{1,0:T(8,128)S(1)} %copy-done.70), kind=kOutput, calls=%fused_computation.125 | convolution fusion | flops 409731072 | bytes 14561280 | tf_op jit(solution)/shard_map/while/body/eval_jaxpr/hqk,qhd->khd/dot_general | solution.py:123
  384.4 11.0 %fusion.6 = (f32[6,1024]{1,0:T(8,128)}, f32[6,512]{1,0:T(8,128)}, bf16[6,512,1024]{2,1,0:T(8,128)(2,1)S(1)}) fusion(f32[6,1024]{1,0:T(8,128)S(1)} %bitcast.231, f32[6,512]{1,0:T(8,128)S(1)} %copy-done.79, f32[6,512]{1,0:T(8,128)S(1)} %bitcast.236, bf16[512,6,64]{0,2,1:T(8,128)(2,1)S(1)} %bitcast.211, bf16[1024,6,64]{0,2,1:T(8,128)(2,1)S(1)} %bitcast.224, ...), kind=kOutput, calls=%fused_computation.12 | convolution fusion | flops 430955520 | bytes 20152320 | tf_op jit(solution)/shard_map/while/body/eval_jaxpr/qhd,khd->hqk/dot_general | solution.py:114
  404.8 4.2 rev.9
  410.3 4.1 reduce-window.16
  416.9 4.2 rev.10
  425.5 4.2 fusion.80
  435.9 9.6 %fusion.49 = bf16[1024,1536]{1,0:T(8,128)(2,1)S(1)} fusion(bf16[1024,1542]{1,0:T(8,128)(2,1)S(1)} %constant_dynamic-update-slice_fusion, bf16[1536,1927]{1,0:T(8,128)(2,1)} %all-gather.3.cloned.1.call-done), kind=kOutput, calls=%fused_computation.85 | convolution fusion | flops 4852285440 | bytes 11415552 | tf_op jit(solution)/shard_map/dot_general | solution.py:24
  457.9 5.6 fusion.119
  463.5 6.2 fusion.85
  469.7 19.1 %collective-permute-done.10 = bf16[512,1536]{1,0:T(8,128)(2,1)} collective-permute-done((bf16[512,1536]{1,0:T(8,128)(2,1)}, bf16[512,1536]{1,0:T(8,128)(2,1)}, u32[]{:S(2)}, u32[]{:S(2)}) %collective-permute-start.10) | collective-permute-done | bytes 1572896 | tf_op jit(solution)/shard_map/ppermute | solution.py:241
  491.0 8.8 %fusion.143 = f32[1536,1542]{1,0:T(8,128)} fusion(bf16[1024,1542]{1,0:T(8,128)(2,1)S(1)} %copy-done.58, bf16[1,1024,1536]{2,1,0:T(8,128)(2,1)S(1)} %copy-done.1, f32[1536]{0:T(1024)S(1)} %copy-done.63, f32[1024]{0:T(1024)S(1)} %copy-done.72), kind=kOutput, calls=%fused_computation.232 | convolution fusion | flops 4857004032 | bytes 15788032 | tf_op jit(solution)/shard_map/dot_general | solution.py:384
  509.4 15.0 %concatenate.98 = f32[1536,1929]{1,0:T(8,128)} concatenate(f32[1536,1542]{1,0:T(8,128)} %fusion.143, f32[1536,1]{1,0:T(8,128)} %fusion.119, f32[1536,1]{1,0:T(8,128)} %broadcast_in_dim.210, f32[1536,1]{1,0:T(8,128)} %broadcast_in_dim.211, f32[1536,384]{1,0:T(8,128)} %fusion.85), dimensions={1} | concatenate | bytes 23703552 | tf_op jit(solution)/shard_map/concatenate | solution.py:390
  536.1 11.6 %collective-permute-done.12 = bf16[192,1929]{1,0:T(8,128)(2,1)} collective-permute-done((bf16[192,1929]{1,0:T(8,128)(2,1)}, bf16[192,1929]{1,0:T(8,128)(2,1)}, u32[]{:S(2)}, u32[]{:S(2)}) %collective-permute-start.12) | collective-permute-done | bytes 740768 | tf_op jit(solution)/shard_map/ppermute | solution.py:218
  554.0 14.7 %collective-permute-done.13 = bf16[192,1929]{1,0:T(8,128)(2,1)S(1)} collective-permute-done((bf16[192,1929]{1,0:T(8,128)(2,1)S(1)}, bf16[192,1929]{1,0:T(8,128)(2,1)S(1)}, u32[]{:S(2)}, u32[]{:S(2)}) %collective-permute-start.13) | collective-permute-done | bytes 740768 | tf_op jit(solution)/shard_map/ppermute | solution.py:218
  576.9 12.1 %collective-permute-done.14 = bf16[192,1929]{1,0:T(8,128)(2,1)S(1)} collective-permute-done((bf16[192,1929]{1,0:T(8,128)(2,1)S(1)}, bf16[192,1929]{1,0:T(8,128)(2,1)S(1)}, u32[]{:S(2)}, u32[]{:S(2)}) %collective-permute-start.14) | collective-permute-done | bytes 740768 | tf_op jit(solution)/shard_map/ppermute | solution.py:218
  600.1 9.1 %collective-permute-done.15 = bf16[192,1929]{1,0:T(8,128)(2,1)S(1)} collective-permute-done((bf16[192,1929]{1,0:T(8,128)(2,1)S(1)}, bf16[192,1929]{1,0:T(8,128)(2,1)S(1)}, u32[]{:S(2)}, u32[]{:S(2)}) %collective-permute-start.15) | collective-permute-done | bytes 740768 | tf_op jit(solution)/shard_map/ppermute | solution.py:218
  (367 shorter events, 209.7 us)
Async XLA Ops:
  7.2 105.4 %all-gather.3.cloned.1.call-start = ((), (), s32[]{:S(2)}) async-start(), calls=%async_computation.1 | async-start | bytes 7077888 | tf_op jit(solution)/shard_map/all_gather | solution.py:279
  11.1 244.2 %all-gather.5.cloned.1.call-start = ((), (), s32[]{:S(2)}) async-start(), calls=%async_computation.2 | async-start | bytes 11059200 | tf_op jit(solution)/shard_map/all_gather | solution.py:287
  19.4 94.7 %copy-start.84 = (f32[6]{0:T(128)S(1)}, f32[6]{0:T(128)}, u32[]{:S(2)}) copy-start(f32[6]{0:T(128)} %param.48) | copy-start | bytes 76
  112.7 502.3 %reduce-scatter.2.cloned.1.call-start = ((), (), s32[]{:S(2)}) async-start(), calls=%async_computation.3 | async-start | bytes 10616832 | tf_op jit(solution)/shard_map/reduce_scatter | solution.py:335
  179.2 3.8 collective-permute-start
  179.2 42.5 %copy-start.27 = (bf16[1024,1536]{1,0:T(8,128)(2,1)S(1)}, bf16[1024,1536]{1,0:T(8,128)(2,1)}, u32[]{:S(2)}) copy-start(bf16[1024,1536]{1,0:T(8,128)(2,1)} %copy-done.26) | copy-start | bytes 9437188
  185.3 36.5 %collective-permute-start.1 = (bf16[512,1536]{1,0:T(8,128)(2,1)S(1)}, bf16[512,1536]{1,0:T(8,128)(2,1)S(1)}, u32[]{:S(2)}, u32[]{:S(2)}) collective-permute-start(bf16[512,1536]{1,0:T(8,128)(2,1)S(1)} %fusion.70), channel_id=1, source_target_pairs={{0,2},{1,3},{2,0},{3,1},{4,6},{5,7},{6,4},{7,5},{8,10},{9,11},{10,... | collective-permute-start | bytes 4718600 | tf_op jit(solution)/shard_map/ppermute | solution.py:241
  225.5 3.8 collective-permute-start.2
  280.9 40.6 %copy-start.25 = (bf16[1024,1536]{1,0:T(8,128)(2,1)}, bf16[1024,1536]{1,0:T(8,128)(2,1)S(1)}, u32[]{:S(2)}) copy-start(bf16[1024,1536]{1,0:T(8,128)(2,1)S(1)} %fusion.52) | copy-start | bytes 9437188
  281.1 3.5 collective-permute-start.3
  285.0 36.5 %collective-permute-start.4 = (bf16[512,1536]{1,0:T(8,128)(2,1)S(1)}, bf16[512,1536]{1,0:T(8,128)(2,1)S(1)}, u32[]{:S(2)}, u32[]{:S(2)}) collective-permute-start(bf16[512,1536]{1,0:T(8,128)(2,1)S(1)} %fusion.71), channel_id=1, source_target_pairs={{0,2},{1,3},{2,0},{3,1},{4,6},{5,7},{6,4},{7,5},{8,10},{9,11},{10,... | collective-permute-start | bytes 4718600 | tf_op jit(solution)/shard_map/ppermute | solution.py:241
  300.0 23.3 %copy-start.95 = (bf16[1024,1024]{1,0:T(8,128)(2,1)S(1)}, bf16[1024,1024]{1,0:T(8,128)(2,1)}, u32[]{:S(2)}) copy-start(bf16[1024,1024]{1,0:T(8,128)(2,1)} %get-tuple-element.321) | copy-start | bytes 6291460
  323.3 11.6 %collective-permute-start.5 = (bf16[512,1536]{1,0:T(8,128)(2,1)}, bf16[512,1536]{1,0:T(8,128)(2,1)}, u32[]{:S(2)}, u32[]{:S(2)}) collective-permute-start(bf16[512,1536]{1,0:T(8,128)(2,1)} %fusion.129), channel_id=1, source_target_pairs={{0,1},{1,0},{2,3},{3,2},{4,5},{5,4},{6,7},{7,6},{8,9},{9,8},{10,11... | collective-permute-start | bytes 4718600 | tf_op jit(solution)/shard_map/ppermute | solution.py:242
  398.9 26.6 %copy-start.44 = (bf16[512,384]{0,1:T(8,128)(2,1)S(1)}, bf16[512,384]{0,1:T(8,128)(2,1)}, u32[]{:S(2)}) copy-start(bf16[512,384]{0,1:T(8,128)(2,1)} %copy-done.43) | copy-start | bytes 1179652
  445.6 3.5 collective-permute-start.9
  451.9 37.0 %collective-permute-start.10 = (bf16[512,1536]{1,0:T(8,128)(2,1)}, bf16[512,1536]{1,0:T(8,128)(2,1)}, u32[]{:S(2)}, u32[]{:S(2)}) collective-permute-start(bf16[512,1536]{1,0:T(8,128)(2,1)} %fusion.73), channel_id=1, source_target_pairs={{0,2},{1,3},{2,0},{3,1},{4,6},{5,7},{6,4},{7,5},{8,10},{9,11},{10,... | collective-permute-start | bytes 4718600 | tf_op jit(solution)/shard_map/ppermute | solution.py:241
  457.1 42.7 %collective-permute-start.6 = (bf16[512,1536]{1,0:T(8,128)(2,1)S(1)}, bf16[512,1536]{1,0:T(8,128)(2,1)S(1)}, u32[]{:S(2)}, u32[]{:S(2)}) collective-permute-start(bf16[512,1536]{1,0:T(8,128)(2,1)S(1)} %constant_dynamic-slice_fusion.1), channel_id=1, source_target_pairs={{0,1},{1,0},{2,3},{3,2},{4,5},{5,4},{6,7},{7,6},{8,9},{9,8},{10,11... | collective-permute-start | bytes 4718600 | tf_op jit(solution)/shard_map/ppermute | solution.py:240
  463.5 25.4 %copy-start.18 = (bf16[512,1536]{1,0:T(8,128)(2,1)S(1)}, bf16[512,1536]{1,0:T(8,128)(2,1)}, u32[]{:S(2)}) copy-start(bf16[512,1536]{1,0:T(8,128)(2,1)} %copy-done.17) | copy-start | bytes 4718596
  463.5 25.4 %copy-start.24 = (bf16[1024,1536]{1,0:T(8,128)(2,1)S(1)}, bf16[1024,1536]{1,0:T(8,128)(2,1)}, u32[]{:S(2)}) copy-start(bf16[1024,1536]{1,0:T(8,128)(2,1)} %copy-done.23) | copy-start | bytes 9437188
  463.5 27.5 %copy-start.58 = (bf16[1024,1542]{1,0:T(8,128)(2,1)S(1)}, bf16[1024,1542]{1,0:T(8,128)(2,1)}, u32[]{:S(2)}) copy-start(bf16[1024,1542]{1,0:T(8,128)(2,1)} %copy-done.57) | copy-start | bytes 9474052
  490.9 12.1 %collective-permute-start.11 = (bf16[512,1536]{1,0:T(8,128)(2,1)S(1)}, bf16[512,1536]{1,0:T(8,128)(2,1)S(1)}, u32[]{:S(2)}, u32[]{:S(2)}) collective-permute-start(bf16[512,1536]{1,0:T(8,128)(2,1)S(1)} %fusion.131), channel_id=1, source_target_pairs={{0,1},{1,0},{2,3},{3,2},{4,5},{5,4},{6,7},{7,6},{8,9},{9,8},{10,11... | collective-permute-start | bytes 4718600 | tf_op jit(solution)/shard_map/ppermute | solution.py:242
  501.5 48.7 %collective-permute-start.7 = (bf16[512,1536]{1,0:T(8,128)(2,1)}, bf16[512,1536]{1,0:T(8,128)(2,1)}, u32[]{:S(2)}, u32[]{:S(2)}) collective-permute-start(bf16[512,1536]{1,0:T(8,128)(2,1)} %fusion.72), channel_id=1, source_target_pairs={{0,2},{1,3},{2,0},{3,1},{4,6},{5,7},{6,4},{7,5},{8,10},{9,11},{10,... | collective-permute-start | bytes 4718600 | tf_op jit(solution)/shard_map/ppermute | solution.py:241
  527.7 19.9 %collective-permute-start.12 = (bf16[192,1929]{1,0:T(8,128)(2,1)}, bf16[192,1929]{1,0:T(8,128)(2,1)}, u32[]{:S(2)}, u32[]{:S(2)}) collective-permute-start(bf16[192,1929]{1,0:T(8,128)(2,1)} %get-tuple-element.317), channel_id=1, source_target_pairs={{0,8},{8,16},{16,24},{24,28},{28,20},{20,12},{12,4},{4,0},{1,9},{9... | collective-permute-start | bytes 2222216 | tf_op jit(solution)/shard_map/ppermute | solution.py:218
  534.0 20.0 %collective-permute-start.16 = (bf16[192,1929]{1,0:T(8,128)(2,1)}, bf16[192,1929]{1,0:T(8,128)(2,1)S(1)}, u32[]{:S(2)}, u32[]{:S(2)}) collective-permute-start(bf16[192,1929]{1,0:T(8,128)(2,1)} %get-tuple-element.318), channel_id=1, source_target_pairs={{0,4},{8,0},{16,8},{24,16},{28,24},{20,28},{12,20},{4,12},{1,5},{9... | collective-permute-start | bytes 2222216 | tf_op jit(solution)/shard_map/ppermute | solution.py:222
  547.7 25.5 %slice-start = ((s8[6291456]{0:T(1024)(128)(4,1)}), s8[4194304]{0:T(1024)(128)(4,1)S(1)}, s32[]{:S(2)}) async-start(s8[6291456]{0:T(1024)(128)(4,1)} %bitcast.196), calls=%async_computation.4 | async-start | bytes 8388608
  549.6 23.5 %slice-start.1 = ((s8[6291456]{0:T(1024)(128)(4,1)}), s8[2097152]{0:T(1024)(128)(4,1)S(1)}, s32[]{:S(2)}) async-start(s8[6291456]{0:T(1024)(128)(4,1)} %bitcast.196), calls=%async_computation.5 | async-start | bytes 4194304
  549.7 19.0 %collective-permute-start.13 = (bf16[192,1929]{1,0:T(8,128)(2,1)S(1)}, bf16[192,1929]{1,0:T(8,128)(2,1)S(1)}, u32[]{:S(2)}, u32[]{:S(2)}) collective-permute-start(bf16[192,1929]{1,0:T(8,128)(2,1)S(1)} %add_convert_fusion.4), channel_id=1, source_target_pairs={{0,8},{8,16},{16,24},{24,28},{28,20},{20,12},{12,4},{4,0},{1,9},{9... | collective-permute-start | bytes 2222216 | tf_op jit(solution)/shard_map/ppermute | solution.py:218
  552.7 41.4 %collective-permute-start.8 = (bf16[512,1536]{1,0:T(8,128)(2,1)S(1)}, bf16[512,1536]{1,0:T(8,128)(2,1)S(1)}, u32[]{:S(2)}, u32[]{:S(2)}) collective-permute-start(bf16[512,1536]{1,0:T(8,128)(2,1)S(1)} %fusion.130), channel_id=1, source_target_pairs={{0,1},{1,0},{2,3},{3,2},{4,5},{5,4},{6,7},{7,6},{8,9},{9,8},{10,11... | collective-permute-start | bytes 4718600 | tf_op jit(solution)/shard_map/ppermute | solution.py:242
  571.1 18.0 %collective-permute-start.14 = (bf16[192,1929]{1,0:T(8,128)(2,1)S(1)}, bf16[192,1929]{1,0:T(8,128)(2,1)S(1)}, u32[]{:S(2)}, u32[]{:S(2)}) collective-permute-start(bf16[192,1929]{1,0:T(8,128)(2,1)S(1)} %get-tuple-element.315), channel_id=1, source_target_pairs={{0,8},{8,16},{16,24},{24,28},{28,20},{20,12},{12,4},{4,0},{1,9},{9... | collective-permute-start | bytes 2222216 | tf_op jit(solution)/shard_map/ppermute | solution.py:218
  571.7 17.9 %collective-permute-start.17 = (bf16[192,1929]{1,0:T(8,128)(2,1)S(1)}, bf16[192,1929]{1,0:T(8,128)(2,1)S(1)}, u32[]{:S(2)}, u32[]{:S(2)}) collective-permute-start(bf16[192,1929]{1,0:T(8,128)(2,1)S(1)} %get-tuple-element.316), channel_id=1, source_target_pairs={{0,4},{8,0},{16,8},{24,16},{28,24},{20,28},{12,20},{4,12},{1,5},{9... | collective-permute-start | bytes 2222216 | tf_op jit(solution)/shard_map/ppermute | solution.py:222
  592.0 17.1 %collective-permute-start.15 = (bf16[192,1929]{1,0:T(8,128)(2,1)S(1)}, bf16[192,1929]{1,0:T(8,128)(2,1)S(1)}, u32[]{:S(2)}, u32[]{:S(2)}) collective-permute-start(bf16[192,1929]{1,0:T(8,128)(2,1)S(1)} %get-tuple-element.313), channel_id=1, source_target_pairs={{0,8},{8,16},{16,24},{24,28},{28,20},{20,12},{12,4},{4,0},{1,9},{9... | collective-permute-start | bytes 2222216 | tf_op jit(solution)/shard_map/ppermute | solution.py:218
  593.4 16.5 %collective-permute-start.18 = (bf16[192,1929]{1,0:T(8,128)(2,1)S(1)}, bf16[192,1929]{1,0:T(8,128)(2,1)S(1)}, u32[]{:S(2)}, u32[]{:S(2)}) collective-permute-start(bf16[192,1929]{1,0:T(8,128)(2,1)S(1)} %get-tuple-element.314), channel_id=1, source_target_pairs={{0,4},{8,0},{16,8},{24,16},{28,24},{20,28},{12,20},{4,12},{1,5},{9... | collective-permute-start | bytes 2222216 | tf_op jit(solution)/shard_map/ppermute | solution.py:222
  (92 other events, 593.7 us)
Sparse Core Ops, SparseCore 0:
  11.2 101.4 all-gather.2
  114.8 140.4 all-gather.4
  340.9 160.3 reduce-scatter.1

commit v5 on v4

--- a/solution.py
+++ b/solution.py
@@ -276,7 +276,7 @@
     attn_local = jnp.concatenate(
         [w_output.T, w_query, w_key, w_value, w_outgate, w_forget, attn_gain[:, None]], axis=1
     )
-    attn_full = lax.all_gather(attn_local, "dp", axis=0, tiled=True)
+    attn_full = ring_gather(attn_local, "dp")
     ffn_local = jnp.concatenate([w_gate, w_up, w_down.T, ffn_gain[:, None]], axis=1)
     ffn_local, attn_full = lax.optimization_barrier((ffn_local, attn_full))
     output_t = attn_full[:, :share_width]

time: 632 us -> 628 us (level)
  waiting for transfers between devices: 247 us -> 203 us
  local copies, waits for them, and re-layouts: 93.9 us -> 111 us
  between operations: 19.9 us -> 33.2 us
  starting transfers between devices: 13.9 us -> 21.5 us
    all_gather x1 -> x0, waiting for transfers between devices: 91.1 us -> none  [on_device(): attn_full = lax.all_gather(attn_local, 'dp', axis=0, tiled=True)]
    ppermute x0 -> x7, waiting for transfers between devices: none -> 42.5 us  [the longest x4 29.7 us: ring_gather(): moving_next = lax.ppermute(moving_next, axis, to_next)]
    dynamic_update_slice x0 -> x8, local copies, waits for them, and re-layouts: none -> 11.2 us  [the longest x4 5.02 us: ring_gather(): out = lax.dynamic_update_index_in_dim(out, moving_next, source, axis=0)]
    ppermute x0 -> x7, starting transfers between devices: none -> 7.71 us  [the longest x3 6.6 us: ring_gather(): moving_prev = lax.ppermute(moving_prev, axis, to_prev)]
    unnamed x212 -> x198, local copies, waits for them, and re-layouts: 19.2 us -> 19.2 us
  transfers between devices with their start and end apart: 22 -> 28, of which waited for: 16 -> 17; matrix products, arithmetic and copies ran while one was open for 46% -> 50% of each run, Pallas kernels for 0% -> 0%
where the time goes in v5:
time: 628 us; the launch traced here: 620 us
  waiting for transfers between devices  203 us (32%)
  matrix products  144 us (23%)
  local copies, waits for them, and re-layouts  111 us (18%)
  other arithmetic  108 us (17%)
  between operations  33.2 us (5%)
  starting transfers between devices  21.5 us (3%)
    ppermute x4, waiting for transfers between devices, tensor_sum(): lax.ppermute(mine.astype(term.dtype), axis, across).astype(jnp.float32)  76.8 us
    ppermute x4, waiting for transfers between devices, ring_reduce_scatter(): part_next = lax.ppermute(part_next.astype(jnp.bfloat16), axis, to_next)  51.6 us
    dot_general x5, matrix products, project(): return jnp.dot(left, right, preferred_element_type=jnp.float32)  36.1 us
    ppermute x4, waiting for transfers between devices, ring_gather(): moving_next = lax.ppermute(moving_next, axis, to_next)  29.7 us
    dot_general x4, matrix products, contract_cols(): lax.dot_general(left, right, (((1,), (1,)), ((), ())), preferred_element_...  27 us
    dot_general x3, matrix products, contract_rows(): lax.dot_general(left, right, (((0,), (0,)), ((), ())), preferred_element_...  19.6 us
    unnamed x198, local copies, waits for them, and re-layouts  19.2 us
    dot_general x2, matrix products, attend_backward(): jnp.einsum('qhd,khd->hqk', out_rows, value_rows, preferred_element_type=j...  17.6 us
  transfers between devices with their start and end apart: 28, of which 17 were waited for; matrix products, arithmetic and copies ran while one was open for 50% of the time, Pallas kernels for 0%

profile of v5, /device:TPU:0, one launch (start us, length us, event | category | flops | bytes accessed | tf_op | source)
XLA Modules:
  0.0 619.9 jit_solution(18009588138708893554)
XLA Ops:
  56.8 12.9 %collective-permute-done.3 = bf16[192,1927]{1,0:T(8,128)(2,1)S(1)} collective-permute-done((bf16[192,1927]{1,0:T(8,128)(2,1)}, bf16[192,1927]{1,0:T(8,128)(2,1)S(1)}, u32[]{:S(2)}, u32[]{:S(2)}) %collective-permute-start.3) | collective-permute-done | bytes 740000 | tf_op jit(solution)/shard_map/ppermute | solution.py:191
  73.6 15.4 %collective-permute-done.4 = bf16[192,1927]{1,0:T(8,128)(2,1)S(1)} collective-permute-done((bf16[192,1927]{1,0:T(8,128)(2,1)S(1)}, bf16[192,1927]{1,0:T(8,128)(2,1)S(1)}, u32[]{:S(2)}, u32[]{:S(2)}) %collective-permute-start.4) | collective-permute-done | bytes 740000 | tf_op jit(solution)/shard_map/ppermute | solution.py:187
  91.5 14.3 %collective-permute-done.6 = bf16[192,1927]{1,0:T(8,128)(2,1)S(1)} collective-permute-done((bf16[192,1927]{1,0:T(8,128)(2,1)S(1)}, bf16[192,1927]{1,0:T(8,128)(2,1)S(1)}, u32[]{:S(2)}, u32[]{:S(2)}) %collective-permute-start.6) | collective-permute-done | bytes 740000 | tf_op jit(solution)/shard_map/ppermute | solution.py:187
  113.6 10.1 %fusion.155 = (bf16[1024,1536]{1,0:T(8,128)(2,1)S(1)}, f32[1024,1536]{1,0:T(8,128)}) fusion(bf16[1536,1927]{1,0:T(8,128)(2,1)} %bitcast.18, bf16[1,1024,1536]{2,1,0:T(8,128)(2,1)S(1)} %copy-done, f32[1536]{0:T(1024)S(1)} %convert_reduce_fusion.1, f32[1024]{0:T(1024)S(1)} %add_rsqrt_fusion.1), kind=kOutput, calls=%fused_computation.247 | convolution fusion | flops 4839702528 | bytes 17311744 | tf_op jit(solution)/shard_map/dot_general | solution.py:14
  181.0 34.9 %collective-permute-done.8 = bf16[512,1536]{1,0:T(8,128)(2,1)S(1)} collective-permute-done((bf16[512,1536]{1,0:T(8,128)(2,1)S(1)}, bf16[512,1536]{1,0:T(8,128)(2,1)S(1)}, u32[]{:S(2)}, u32[]{:S(2)}) %collective-permute-start.8) | collective-permute-done | bytes 1572896 | tf_op jit(solution)/shard_map/ppermute | solution.py:241
  231.8 17.6 %all-gather.2.cloned.1.call-done = bf16[1536,3073]{1,0:T(8,128)(2,1)} async-done(((bf16[192,3073]{1,0:T(8,128)(2,1)}), bf16[1536,3073]{1,0:T(8,128)(2,1)}) %all-gather.2.cloned.1.call-update) | async-done | bytes 9440272 | tf_op jit(solution)/shard_map/all_gather | solution.py:287
  250.6 10.8 %fusion.35 = f32[1024,2048]{1,0:T(8,128)S(1)} fusion(bf16[1536,3073]{1,0:T(8,128)(2,1)} %all-gather.2.cloned.1.call-done, f32[1024,1536]{1,0:T(8,128)} %get-tuple-element.326, f32[1536]{0:T(1024)S(1)} %convert_reduce_fusion, f32[1024]{0:T(1024)S(1)} %add_rsqrt_fusion), kind=kOutput, calls=%fused_computation.57 | convolution fusion | flops 6447169536 | bytes 20981760 | tf_op jit(solution)/shard_map/dot_general | solution.py:14
  261.5 6.2 %fusion.45 = (bf16[1024,1024]{1,0:T(8,128)(2,1)S(1)}, bf16[1024,1024]{1,0:T(8,128)(2,1)S(1)}, bf16[1024,1024]{1,0:T(8,128)(2,1)}) fusion(f32[1024,2048]{1,0:T(8,128)S(1)} %fusion.35, bf16[1536,3073]{1,0:T(8,128)(2,1)S(1)} %copy-done.82, bf16[1,1024,1536]{2,1,0:T(8,128)(2,1)S(1)} %copy-done.32), kind=kOutput, calls=%fused_computation.70 | convolution fusion | flops 3238002688 | bytes 20971520 | tf_op jit(solution)/shard_map/dot_general | solution.py:14
  267.7 7.3 %fusion.52 = bf16[1024,1536]{1,0:T(8,128)(2,1)S(1)} fusion(bf16[1536,3073]{1,0:T(8,128)(2,1)S(1)} %copy-done.82, bf16[1024,1024]{1,0:T(8,128)(2,1)S(1)} %get-tuple-element.334, bf16[1024,1024]{1,0:T(8,128)(2,1)S(1)} %get-tuple-element.333), kind=kOutput, calls=%fused_computation.86 | convolution fusion | flops 6452412416 | bytes 13631488 | tf_op jit(solution)/shard_map/dot_general | solution.py:24
  284.5 9.6 %convolution_convert_fusion = bf16[1536,2048]{1,0:T(8,128)(2,1)S(1)} fusion(bf16[1024,1024]{1,0:T(8,128)(2,1)} %copy-done.86, bf16[1024,1024]{1,0:T(8,128)(2,1)} %copy-done.85, f32[1024,1536]{1,0:T(8,128)S(1)} %bitcast.223, f32[1536]{0:T(1024)S(1)} %convert_reduce_fusion, f32[1024]{0:T(1024)S(1)} %add_rsqrt_fusion), kind=kOutput, calls=%fused_computation.25 | convolution fusion | flops 6458703872 | bytes 16787456 | tf_op jit(solution)/shard_map/dot_general | solution.py:18
  294.1 21.5 %collective-permute-done.11 = bf16[512,1536]{1,0:T(8,128)(2,1)S(1)} collective-permute-done((bf16[512,1536]{1,0:T(8,128)(2,1)S(1)}, bf16[512,1536]{1,0:T(8,128)(2,1)S(1)}, u32[]{:S(2)}, u32[]{:S(2)}) %collective-permute-start.11) | collective-permute-done | bytes 1572896 | tf_op jit(solution)/shard_map/ppermute | solution.py:241
  317.4 6.7 %convolution_convert_fusion.3 = bf16[1024,1536]{1,0:T(8,128)(2,1)} fusion(bf16[1024,1024]{1,0:T(8,128)(2,1)S(1)} %copy-done.88, bf16[1536,3073]{1,0:T(8,128)(2,1)} %all-gather.2.cloned.1.call-done), kind=kOutput, calls=%fused_computation.89 | convolution fusion | flops 3222798336 | bytes 8388608 | tf_op jit(solution)/shard_map/dot_general | solution.py:24
  324.1 4.8 pad_maximum_fusion
  334.9 6.2 %multiply_reduce_fusion = (f32[1536]{0:T(1024)}, f32[1024]{0:T(1024)S(1)}) fusion(f32[1024,1536]{1,0:T(8,128)} %pad_maximum_fusion.1, f32[1024,1536]{1,0:T(8,128)} %get-tuple-element.326, f32[1024]{0:T(1024)S(1)} %add_rsqrt_fusion, f32[1536]{0:T(1024)S(1)} %convert_reduce_fusion), kind=kLoop, calls=%fused_computation.42 | loop fusion | flops 9434624 | bytes 12603392 | tf_op jit(solution)/shard_map/reduce_sum | solution.py:340
  347.3 6.9 %multiply_convert_fusion.3 = (bf16[1024,384]{1,0:T(8,128)(2,1)S(1)}, f32[1024,384]{1,0:T(8,128)}) fusion(f32[1024,1536]{1,0:T(8,128)} %get-tuple-element.368, bf16[1536,1927]{1,0:T(8,128)(2,1)} %bitcast.18, f32[1024,1536]{1,0:T(8,128)S(1)} %multiply_add_fusion), kind=kOutput, calls=%fused_computation.141 | convolution fusion | flops 1211498496 | bytes 11403264 | tf_op jit(solution)/shard_map/dot_general | solution.py:14
  356.3 4.9 fusion.103
  361.1 6.6 %fusion.38 = (f32[6,512]{1,0:T(8,128)}, f32[6,512]{1,0:T(8,128)}, bf16[6,512,512]{1,2,0:T(8,128)(2,1)S(1)}) fusion(f32[6,512]{1,0:T(8,128)S(1)} %copy-done.81, f32[6,512]{1,0:T(8,128)S(1)} %bitcast.261, bf16[512,6,64]{0,2,1:T(8,128)(2,1)S(1)} %bitcast.232, bf16[512,6,64]{0,2,1:T(8,128)(2,1)S(1)} %bitcast.251, f32[6,512,512]{1,2,0:T(8,128)} %copy-done.14, ...), kind=kOutput, calls=%fused_computation.60 | convolution fusion | flops 215476224 | bytes 10285056 | tf_op jit(solution)/shard_map/while/body/eval_jaxpr/qhd,khd->hqk/dot_general | solution.py:114
  371.1 7.3 %fusion.79 = bf16[1024,6,64]{0,2,1:T(8,128)(2,1)} fusion(f32[512,6,64]{0,2,1:T(8,128)} %fusion.103, bf16[512,6,64]{0,2,1:T(8,128)(2,1)S(1)} %bitcast.234, f32[6,512,1024]{2,1,0:T(8,128)} %copy-done.4, f32[6,512]{1,0:T(8,128)S(1)} %copy-done.70), kind=kOutput, calls=%fused_computation.125 | convolution fusion | flops 409731072 | bytes 14561280 | tf_op jit(solution)/shard_map/while/body/eval_jaxpr/hqk,qhd->khd/dot_general | solution.py:123
  378.5 11.0 %fusion.6 = (f32[6,1024]{1,0:T(8,128)}, f32[6,512]{1,0:T(8,128)}, bf16[6,512,1024]{2,1,0:T(8,128)(2,1)S(1)}) fusion(f32[6,1024]{1,0:T(8,128)S(1)} %bitcast.255, f32[6,512]{1,0:T(8,128)S(1)} %copy-done.79, f32[6,512]{1,0:T(8,128)S(1)} %bitcast.260, bf16[512,6,64]{0,2,1:T(8,128)(2,1)S(1)} %bitcast.235, bf16[1024,6,64]{0,2,1:T(8,128)(2,1)S(1)} %bitcast.248, ...), kind=kOutput, calls=%fused_computation.12 | convolution fusion | flops 430955520 | bytes 20152320 | tf_op jit(solution)/shard_map/while/body/eval_jaxpr/qhd,khd->hqk/dot_general | solution.py:114
  398.9 4.2 rev.9
  411.1 4.2 rev.10
  419.7 4.2 fusion.80
  430.0 9.6 %fusion.49 = bf16[1024,1536]{1,0:T(8,128)(2,1)S(1)} fusion(bf16[1024,1542]{1,0:T(8,128)(2,1)S(1)} %constant_dynamic-update-slice_fusion, bf16[1536,1927]{1,0:T(8,128)(2,1)} %bitcast.18), kind=kOutput, calls=%fused_computation.85 | convolution fusion | flops 4852285440 | bytes 11415552 | tf_op jit(solution)/shard_map/dot_general | solution.py:24
  450.7 5.6 fusion.119
  456.3 6.2 %fusion.85 = f32[1536,384]{1,0:T(8,128)} fusion(bf16[1024,384]{1,0:T(8,128)(2,1)S(1)} %copy-done.42, f32[1024,1536]{1,0:T(8,128)} %copy-done.2), kind=kOutput, calls=%fused_computation.142 | convolution fusion | flops 1209532416 | bytes 9437184 | tf_op jit(solution)/shard_map/dot_general | solution.py:18
  462.5 20.4 %collective-permute-done.17 = bf16[512,1536]{1,0:T(8,128)(2,1)} collective-permute-done((bf16[512,1536]{1,0:T(8,128)(2,1)}, bf16[512,1536]{1,0:T(8,128)(2,1)}, u32[]{:S(2)}, u32[]{:S(2)}) %collective-permute-start.17) | collective-permute-done | bytes 1572896 | tf_op jit(solution)/shard_map/ppermute | solution.py:241
  485.1 8.8 %fusion.143 = f32[1536,1542]{1,0:T(8,128)} fusion(bf16[1024,1542]{1,0:T(8,128)(2,1)S(1)} %copy-done.58, bf16[1,1024,1536]{2,1,0:T(8,128)(2,1)S(1)} %copy-done.1, f32[1536]{0:T(1024)S(1)} %copy-done.63, f32[1024]{0:T(1024)S(1)} %copy-done.72), kind=kOutput, calls=%fused_computation.240 | convolution fusion | flops 4857004032 | bytes 15788032 | tf_op jit(solution)/shard_map/dot_general | solution.py:384
  503.5 15.0 %concatenate.98 = f32[1536,1929]{1,0:T(8,128)} concatenate(f32[1536,1542]{1,0:T(8,128)} %fusion.143, f32[1536,1]{1,0:T(8,128)} %fusion.119, f32[1536,1]{1,0:T(8,128)} %broadcast_in_dim.247, f32[1536,1]{1,0:T(8,128)} %broadcast_in_dim.248, f32[1536,384]{1,0:T(8,128)} %fusion.85), dimensions={1} | concatenate | bytes 23703552 | tf_op jit(solution)/shard_map/concatenate | solution.py:390
  527.0 14.6 %collective-permute-done.19 = bf16[192,1929]{1,0:T(8,128)(2,1)} collective-permute-done((bf16[192,1929]{1,0:T(8,128)(2,1)}, bf16[192,1929]{1,0:T(8,128)(2,1)}, u32[]{:S(2)}, u32[]{:S(2)}) %collective-permute-start.19) | collective-permute-done | bytes 740768 | tf_op jit(solution)/shard_map/ppermute | solution.py:218
  546.8 15.8 %collective-permute-done.20 = bf16[192,1929]{1,0:T(8,128)(2,1)S(1)} collective-permute-done((bf16[192,1929]{1,0:T(8,128)(2,1)S(1)}, bf16[192,1929]{1,0:T(8,128)(2,1)S(1)}, u32[]{:S(2)}, u32[]{:S(2)}) %collective-permute-start.20) | collective-permute-done | bytes 740768 | tf_op jit(solution)/shard_map/ppermute | solution.py:218
  570.9 12.1 %collective-permute-done.21 = bf16[192,1929]{1,0:T(8,128)(2,1)S(1)} collective-permute-done((bf16[192,1929]{1,0:T(8,128)(2,1)S(1)}, bf16[192,1929]{1,0:T(8,128)(2,1)S(1)}, u32[]{:S(2)}, u32[]{:S(2)}) %collective-permute-start.21) | collective-permute-done | bytes 740768 | tf_op jit(solution)/shard_map/ppermute | solution.py:218
  594.1 9.0 %collective-permute-done.22 = bf16[192,1929]{1,0:T(8,128)(2,1)S(1)} collective-permute-done((bf16[192,1929]{1,0:T(8,128)(2,1)S(1)}, bf16[192,1929]{1,0:T(8,128)(2,1)S(1)}, u32[]{:S(2)}, u32[]{:S(2)}) %collective-permute-start.22) | collective-permute-done | bytes 740768 | tf_op jit(solution)/shard_map/ppermute | solution.py:218
  (373 shorter events, 241.7 us)
Async XLA Ops:
  7.2 28.8 %copy-start.83 = (bf16[192]{0:T(256)(128)(2,1)S(1)}, bf16[192]{0:T(256)(128)(2,1)}, u32[]{:S(2)}) copy-start(bf16[192]{0:T(256)(128)(2,1)} %param.57) | copy-start | bytes 1156
  7.2 242.2 %all-gather.2.cloned.1.call-start = ((), (), s32[]{:S(2)}) async-start(), calls=%async_computation.1 | async-start | bytes 11059200 | tf_op jit(solution)/shard_map/all_gather | solution.py:287
  10.9 39.5 %collective-permute-start.1 = (bf16[192,1927]{1,0:T(8,128)(2,1)}, bf16[192,1927]{1,0:T(8,128)(2,1)}, u32[]{:S(2)}, u32[]{:S(2)}) collective-permute-start(bf16[192,1927]{1,0:T(8,128)(2,1)} %concatenate.80), channel_id=1, source_target_pairs={{0,4},{8,0},{16,8},{24,16},{28,24},{20,28},{12,20},{4,12},{1,5},{9... | collective-permute-start | bytes 2219912 | tf_op jit(solution)/shard_map/ppermute | solution.py:191
  13.9 38.5 %collective-permute-start = (bf16[192,1927]{1,0:T(8,128)(2,1)}, bf16[192,1927]{1,0:T(8,128)(2,1)}, u32[]{:S(2)}, u32[]{:S(2)}) collective-permute-start(bf16[192,1927]{1,0:T(8,128)(2,1)} %concatenate.80), channel_id=1, source_target_pairs={{0,8},{8,16},{16,24},{24,28},{28,20},{20,12},{12,4},{4,0},{1,9},{9... | collective-permute-start | bytes 2219912 | tf_op jit(solution)/shard_map/ppermute | solution.py:187
  50.4 19.2 %collective-permute-start.3 = (bf16[192,1927]{1,0:T(8,128)(2,1)}, bf16[192,1927]{1,0:T(8,128)(2,1)S(1)}, u32[]{:S(2)}, u32[]{:S(2)}) collective-permute-start(bf16[192,1927]{1,0:T(8,128)(2,1)} %collective-permute-done.1), channel_id=1, source_target_pairs={{0,4},{8,0},{16,8},{24,16},{28,24},{20,28},{12,20},{4,12},{1,5},{9... | collective-permute-start | bytes 2219912 | tf_op jit(solution)/shard_map/ppermute | solution.py:191
  52.4 18.9 %collective-permute-start.2 = (bf16[192,1927]{1,0:T(8,128)(2,1)}, bf16[192,1927]{1,0:T(8,128)(2,1)S(1)}, u32[]{:S(2)}, u32[]{:S(2)}) collective-permute-start(bf16[192,1927]{1,0:T(8,128)(2,1)} %collective-permute-done), channel_id=1, source_target_pairs={{0,8},{8,16},{16,24},{24,28},{28,20},{20,12},{12,4},{4,0},{1,9},{9... | collective-permute-start | bytes 2219912 | tf_op jit(solution)/shard_map/ppermute | solution.py:187
  69.6 20.9 %collective-permute-start.5 = (bf16[192,1927]{1,0:T(8,128)(2,1)S(1)}, bf16[192,1927]{1,0:T(8,128)(2,1)S(1)}, u32[]{:S(2)}, u32[]{:S(2)}) collective-permute-start(bf16[192,1927]{1,0:T(8,128)(2,1)S(1)} %collective-permute-done.3), channel_id=1, source_target_pairs={{0,4},{8,0},{16,8},{24,16},{28,24},{20,28},{12,20},{4,12},{1,5},{9... | collective-permute-start | bytes 2219912 | tf_op jit(solution)/shard_map/ppermute | solution.py:191
  71.3 17.7 %collective-permute-start.4 = (bf16[192,1927]{1,0:T(8,128)(2,1)S(1)}, bf16[192,1927]{1,0:T(8,128)(2,1)S(1)}, u32[]{:S(2)}, u32[]{:S(2)}) collective-permute-start(bf16[192,1927]{1,0:T(8,128)(2,1)S(1)} %collective-permute-done.2), channel_id=1, source_target_pairs={{0,8},{8,16},{16,24},{24,28},{28,20},{20,12},{12,4},{4,0},{1,9},{9... | collective-permute-start | bytes 2219912 | tf_op jit(solution)/shard_map/ppermute | solution.py:187
  73.6 34.5 %copy-start.84 = (f32[6]{0:T(128)S(1)}, f32[6]{0:T(128)}, u32[]{:S(2)}) copy-start(f32[6]{0:T(128)} %param.55) | copy-start | bytes 76
  89.0 16.7 %collective-permute-start.6 = (bf16[192,1927]{1,0:T(8,128)(2,1)S(1)}, bf16[192,1927]{1,0:T(8,128)(2,1)S(1)}, u32[]{:S(2)}, u32[]{:S(2)}) collective-permute-start(bf16[192,1927]{1,0:T(8,128)(2,1)S(1)} %collective-permute-done.4), channel_id=1, source_target_pairs={{0,8},{8,16},{16,24},{24,28},{28,20},{20,12},{12,4},{4,0},{1,9},{9... | collective-permute-start | bytes 2219912 | tf_op jit(solution)/shard_map/ppermute | solution.py:187
  106.7 502.2 %reduce-scatter.2.cloned.1.call-start = ((), (), s32[]{:S(2)}) async-start(), calls=%async_computation.2 | async-start | bytes 10616832 | tf_op jit(solution)/shard_map/reduce_scatter | solution.py:335
  173.3 3.8 collective-permute-start.7
  173.3 42.5 %copy-start.27 = (bf16[1024,1536]{1,0:T(8,128)(2,1)S(1)}, bf16[1024,1536]{1,0:T(8,128)(2,1)}, u32[]{:S(2)}) copy-start(bf16[1024,1536]{1,0:T(8,128)(2,1)} %copy-done.26) | copy-start | bytes 9437188
  179.4 36.5 %collective-permute-start.8 = (bf16[512,1536]{1,0:T(8,128)(2,1)S(1)}, bf16[512,1536]{1,0:T(8,128)(2,1)S(1)}, u32[]{:S(2)}, u32[]{:S(2)}) collective-permute-start(bf16[512,1536]{1,0:T(8,128)(2,1)S(1)} %fusion.70), channel_id=1, source_target_pairs={{0,2},{1,3},{2,0},{3,1},{4,6},{5,7},{6,4},{7,5},{8,10},{9,11},{10,... | collective-permute-start | bytes 4718600 | tf_op jit(solution)/shard_map/ppermute | solution.py:241
  219.6 3.8 collective-permute-start.9
  275.0 40.6 %copy-start.25 = (bf16[1024,1536]{1,0:T(8,128)(2,1)}, bf16[1024,1536]{1,0:T(8,128)(2,1)S(1)}, u32[]{:S(2)}) copy-start(bf16[1024,1536]{1,0:T(8,128)(2,1)S(1)} %fusion.52) | copy-start | bytes 9437188
  275.2 3.5 collective-permute-start.10
  279.1 36.5 %collective-permute-start.11 = (bf16[512,1536]{1,0:T(8,128)(2,1)S(1)}, bf16[512,1536]{1,0:T(8,128)(2,1)S(1)}, u32[]{:S(2)}, u32[]{:S(2)}) collective-permute-start(bf16[512,1536]{1,0:T(8,128)(2,1)S(1)} %fusion.71), channel_id=1, source_target_pairs={{0,2},{1,3},{2,0},{3,1},{4,6},{5,7},{6,4},{7,5},{8,10},{9,11},{10,... | collective-permute-start | bytes 4718600 | tf_op jit(solution)/shard_map/ppermute | solution.py:241
  317.3 11.6 %collective-permute-start.12 = (bf16[512,1536]{1,0:T(8,128)(2,1)}, bf16[512,1536]{1,0:T(8,128)(2,1)}, u32[]{:S(2)}, u32[]{:S(2)}) collective-permute-start(bf16[512,1536]{1,0:T(8,128)(2,1)} %fusion.129), channel_id=1, source_target_pairs={{0,1},{1,0},{2,3},{3,2},{4,5},{5,4},{6,7},{7,6},{8,9},{9,8},{10,11... | collective-permute-start | bytes 4718600 | tf_op jit(solution)/shard_map/ppermute | solution.py:242
  439.8 3.5 collective-permute-start.16
  446.0 37.0 %collective-permute-start.17 = (bf16[512,1536]{1,0:T(8,128)(2,1)}, bf16[512,1536]{1,0:T(8,128)(2,1)}, u32[]{:S(2)}, u32[]{:S(2)}) collective-permute-start(bf16[512,1536]{1,0:T(8,128)(2,1)} %fusion.73), channel_id=1, source_target_pairs={{0,2},{1,3},{2,0},{3,1},{4,6},{5,7},{6,4},{7,5},{8,10},{9,11},{10,... | collective-permute-start | bytes 4718600 | tf_op jit(solution)/shard_map/ppermute | solution.py:241
  450.0 44.0 %collective-permute-start.13 = (bf16[512,1536]{1,0:T(8,128)(2,1)S(1)}, bf16[512,1536]{1,0:T(8,128)(2,1)S(1)}, u32[]{:S(2)}, u32[]{:S(2)}) collective-permute-start(bf16[512,1536]{1,0:T(8,128)(2,1)S(1)} %constant_dynamic-slice_fusion.1), channel_id=1, source_target_pairs={{0,1},{1,0},{2,3},{3,2},{4,5},{5,4},{6,7},{7,6},{8,9},{9,8},{10,11... | collective-permute-start | bytes 4718600 | tf_op jit(solution)/shard_map/ppermute | solution.py:240
  485.0 12.1 %collective-permute-start.18 = (bf16[512,1536]{1,0:T(8,128)(2,1)S(1)}, bf16[512,1536]{1,0:T(8,128)(2,1)S(1)}, u32[]{:S(2)}, u32[]{:S(2)}) collective-permute-start(bf16[512,1536]{1,0:T(8,128)(2,1)S(1)} %fusion.131), channel_id=1, source_target_pairs={{0,1},{1,0},{2,3},{3,2},{4,5},{5,4},{6,7},{7,6},{8,9},{9,8},{10,11... | collective-permute-start | bytes 4718600 | tf_op jit(solution)/shard_map/ppermute | solution.py:242
  495.6 48.6 %collective-permute-start.14 = (bf16[512,1536]{1,0:T(8,128)(2,1)}, bf16[512,1536]{1,0:T(8,128)(2,1)}, u32[]{:S(2)}, u32[]{:S(2)}) collective-permute-start(bf16[512,1536]{1,0:T(8,128)(2,1)} %fusion.72), channel_id=1, source_target_pairs={{0,2},{1,3},{2,0},{3,1},{4,6},{5,7},{6,4},{7,5},{8,10},{9,11},{10,... | collective-permute-start | bytes 4718600 | tf_op jit(solution)/shard_map/ppermute | solution.py:241
  521.7 19.9 %collective-permute-start.19 = (bf16[192,1929]{1,0:T(8,128)(2,1)}, bf16[192,1929]{1,0:T(8,128)(2,1)}, u32[]{:S(2)}, u32[]{:S(2)}) collective-permute-start(bf16[192,1929]{1,0:T(8,128)(2,1)} %get-tuple-element.331), channel_id=1, source_target_pairs={{0,8},{8,16},{16,24},{24,28},{28,20},{20,12},{12,4},{4,0},{1,9},{9... | collective-permute-start | bytes 2222216 | tf_op jit(solution)/shard_map/ppermute | solution.py:218
  524.9 21.9 %collective-permute-start.23 = (bf16[192,1929]{1,0:T(8,128)(2,1)}, bf16[192,1929]{1,0:T(8,128)(2,1)S(1)}, u32[]{:S(2)}, u32[]{:S(2)}) collective-permute-start(bf16[192,1929]{1,0:T(8,128)(2,1)} %get-tuple-element.332), channel_id=1, source_target_pairs={{0,4},{8,0},{16,8},{24,16},{28,24},{20,28},{12,20},{4,12},{1,5},{9... | collective-permute-start | bytes 2222216 | tf_op jit(solution)/shard_map/ppermute | solution.py:222
  543.6 19.0 %collective-permute-start.20 = (bf16[192,1929]{1,0:T(8,128)(2,1)S(1)}, bf16[192,1929]{1,0:T(8,128)(2,1)S(1)}, u32[]{:S(2)}, u32[]{:S(2)}) collective-permute-start(bf16[192,1929]{1,0:T(8,128)(2,1)S(1)} %add_convert_fusion.4), channel_id=1, source_target_pairs={{0,8},{8,16},{16,24},{24,28},{28,20},{20,12},{12,4},{4,0},{1,9},{9... | collective-permute-start | bytes 2222216 | tf_op jit(solution)/shard_map/ppermute | solution.py:218
  546.7 41.4 %collective-permute-start.15 = (bf16[512,1536]{1,0:T(8,128)(2,1)S(1)}, bf16[512,1536]{1,0:T(8,128)(2,1)S(1)}, u32[]{:S(2)}, u32[]{:S(2)}) collective-permute-start(bf16[512,1536]{1,0:T(8,128)(2,1)S(1)} %fusion.130), channel_id=1, source_target_pairs={{0,1},{1,0},{2,3},{3,2},{4,5},{5,4},{6,7},{7,6},{8,9},{9,8},{10,11... | collective-permute-start | bytes 4718600 | tf_op jit(solution)/shard_map/ppermute | solution.py:242
  565.1 18.0 %collective-permute-start.21 = (bf16[192,1929]{1,0:T(8,128)(2,1)S(1)}, bf16[192,1929]{1,0:T(8,128)(2,1)S(1)}, u32[]{:S(2)}, u32[]{:S(2)}) collective-permute-start(bf16[192,1929]{1,0:T(8,128)(2,1)S(1)} %get-tuple-element.329), channel_id=1, source_target_pairs={{0,8},{8,16},{16,24},{24,28},{28,20},{20,12},{12,4},{4,0},{1,9},{9... | collective-permute-start | bytes 2222216 | tf_op jit(solution)/shard_map/ppermute | solution.py:218
  565.7 17.9 %collective-permute-start.24 = (bf16[192,1929]{1,0:T(8,128)(2,1)S(1)}, bf16[192,1929]{1,0:T(8,128)(2,1)S(1)}, u32[]{:S(2)}, u32[]{:S(2)}) collective-permute-start(bf16[192,1929]{1,0:T(8,128)(2,1)S(1)} %get-tuple-element.330), channel_id=1, source_target_pairs={{0,4},{8,0},{16,8},{24,16},{28,24},{20,28},{12,20},{4,12},{1,5},{9... | collective-permute-start | bytes 2222216 | tf_op jit(solution)/shard_map/ppermute | solution.py:222
  586.0 17.1 %collective-permute-start.22 = (bf16[192,1929]{1,0:T(8,128)(2,1)S(1)}, bf16[192,1929]{1,0:T(8,128)(2,1)S(1)}, u32[]{:S(2)}, u32[]{:S(2)}) collective-permute-start(bf16[192,1929]{1,0:T(8,128)(2,1)S(1)} %get-tuple-element.327), channel_id=1, source_target_pairs={{0,8},{8,16},{16,24},{24,28},{28,20},{20,12},{12,4},{4,0},{1,9},{9... | collective-permute-start | bytes 2222216 | tf_op jit(solution)/shard_map/ppermute | solution.py:218
  587.3 16.5 %collective-permute-start.25 = (bf16[192,1929]{1,0:T(8,128)(2,1)S(1)}, bf16[192,1929]{1,0:T(8,128)(2,1)S(1)}, u32[]{:S(2)}, u32[]{:S(2)}) collective-permute-start(bf16[192,1929]{1,0:T(8,128)(2,1)S(1)} %get-tuple-element.328), channel_id=1, source_target_pairs={{0,4},{8,0},{16,8},{24,16},{28,24},{20,28},{12,20},{4,12},{1,5},{9... | collective-permute-start | bytes 2222216 | tf_op jit(solution)/shard_map/ppermute | solution.py:222
  (91 other events, 722.4 us)
Sparse Core Ops, SparseCore 0:
  106.8 142.5 all-gather.1
  335.0 160.4 reduce-scatter.1

commit v6 on v5

--- a/solution.py
+++ b/solution.py
@@ -58,11 +58,24 @@
     return (jnp.where(allowed_rows[None], raw - jnp.abs(apart), masked_value), apart)
 
 
+def running_sum(values, reverse=False):
+    length = values.shape[1]
+    earlier = lax.broadcasted_iota(jnp.int32, (length, length), 0)
+    later = lax.broadcasted_iota(jnp.int32, (length, length), 1)
+    keep = earlier >= later if reverse else earlier <= later
+    return jnp.dot(
+        values,
+        keep.astype(jnp.float32),
+        precision=lax.Precision.HIGHEST,
+        preferred_element_type=jnp.float32,
+    )
+
+
 def attend_forward(items):
     query_all, key_all, value_all, log_forget, starts = items
     length = query_all.shape[0]
     block_rows = min(512, length)
-    decay = jnp.cumsum(log_forget, axis=0).T
+    decay = running_sum(log_forget.T)
     allowed = allowed_pairs(starts, length)
     results = []
     normalizers = []
@@ -93,7 +106,7 @@
     length = query_all.shape[0]
     block_rows = min(512, length)
     scale = query_all.shape[-1] ** (-0.5)
-    decay = jnp.cumsum(log_forget, axis=0).T
+    decay = running_sum(log_forget.T)
     allowed = allowed_pairs(starts, length)
     grad_key = jnp.zeros(key_all.shape, jnp.float32)
     grad_value = jnp.zeros(value_all.shape, jnp.float32)
@@ -141,7 +154,7 @@
         grad_decay = grad_decay.at[:, :reach].add(jnp.sum(signed, axis=1))
         row_parts.append(-jnp.sum(signed, axis=-1))
     grad_decay = grad_decay + jnp.concatenate(row_parts, axis=1)
-    grad_log = jnp.flip(jnp.cumsum(jnp.flip(grad_decay, axis=1), axis=1), axis=1).T
+    grad_log = running_sum(grad_decay, reverse=True).T
     grad_query = jnp.concatenate(query_parts, axis=0)
     return (
         grad_query.astype(jnp.bfloat16),
@@ -389,11 +402,11 @@
     late_sums = ring_reduce_scatter(
         jnp.concatenate(
             [
-                late_grads,
-                bias_col[:, None],
-                grad_attn_gain[:, None],
-                grad_ffn_gain[:, None],
-                grad_output_t,
+                late_grads.astype(jnp.bfloat16),
+                bias_col[:, None].astype(jnp.bfloat16),
+                grad_attn_gain[:, None].astype(jnp.bfloat16),
+                grad_ffn_gain[:, None].astype(jnp.bfloat16),
+                grad_output_t.astype(jnp.bfloat16),
             ],
             axis=1,
         ),

time: 628 us -> 601 us (0.957)
  local copies, waits for them, and re-layouts: 111 us -> 88.4 us
  other arithmetic: 108 us -> 96.6 us
  waiting for transfers between devices: 203 us -> 210 us
    rev x2 -> x0, local copies, waits for them, and re-layouts: 8.43 us -> none  [the longest x1 4.22 us: attend_backward(): jnp.flip(jnp.cumsum(jnp.flip(grad_decay, axis=1), axis=1), axis=1)]
    unnamed x198 -> x196, local copies, waits for them, and re-layouts: 19.2 us -> 14.9 us
  transfers between devices with their start and end apart: 28 -> 28, of which waited for: 17 -> 17; matrix products, arithmetic and copies ran while one was open for 50% -> 46% of each run, Pallas kernels for 0% -> 0%
where the time goes in v6:
time: 601 us; the launch traced here: 594 us
  waiting for transfers between devices  210 us (35%)
  matrix products  144 us (24%)
  other arithmetic  96.6 us (16%)
  local copies, waits for them, and re-layouts  88.4 us (15%)
  between operations  33.7 us (6%)
  starting transfers between devices  21.5 us (4%)
    ppermute x4, waiting for transfers between devices, tensor_sum(): lax.ppermute(mine.astype(term.dtype), axis, across).astype(jnp.float32)  78.3 us
    ppermute x4, waiting for transfers between devices, ring_reduce_scatter(): part_next = lax.ppermute(part_next.astype(jnp.bfloat16), axis, to_next)  51.1 us
    dot_general x5, matrix products, project(): return jnp.dot(left, right, preferred_element_type=jnp.float32)  35.9 us
    ppermute x4, waiting for transfers between devices, ring_gather(): moving_next = lax.ppermute(moving_next, axis, to_next)  29.6 us
    dot_general x4, matrix products, contract_cols(): lax.dot_general(left, right, (((1,), (1,)), ((), ())), preferred_element_...  27 us
    all_gather x1, waiting for transfers between devices, on_device(): ffn_full = lax.all_gather(ffn_local, 'dp', axis=0, tiled=True)  22.4 us
    dot_general x3, matrix products, contract_rows(): lax.dot_general(left, right, (((0,), (0,)), ((), ())), preferred_element_...  19.3 us
    dot_general x2, matrix products, attend_backward(): jnp.einsum('qhd,khd->hqk', out_rows, value_rows, preferred_element_type=j...  17.4 us
  transfers between devices with their start and end apart: 28, of which 17 were waited for; matrix products, arithmetic and copies ran while one was open for 46% of the time, Pallas kernels for 0%

profile of v6, /device:TPU:0, one launch (start us, length us, event | category | flops | bytes accessed | tf_op | source)
XLA Modules:
  0.0 594.4 jit_solution(2164285288893743431)
XLA Ops:
  51.2 15.1 %collective-permute-done.3 = bf16[192,1927]{1,0:T(8,128)(2,1)S(1)} collective-permute-done((bf16[192,1927]{1,0:T(8,128)(2,1)S(1)}, bf16[192,1927]{1,0:T(8,128)(2,1)S(1)}, u32[]{:S(2)}, u32[]{:S(2)}) %collective-permute-start.3) | collective-permute-done | bytes 740000 | tf_op jit(solution)/shard_map/ppermute | solution.py:204
  70.3 15.4 %collective-permute-done.4 = bf16[192,1927]{1,0:T(8,128)(2,1)S(1)} collective-permute-done((bf16[192,1927]{1,0:T(8,128)(2,1)S(1)}, bf16[192,1927]{1,0:T(8,128)(2,1)S(1)}, u32[]{:S(2)}, u32[]{:S(2)}) %collective-permute-start.4) | collective-permute-done | bytes 740000 | tf_op jit(solution)/shard_map/ppermute | solution.py:200
  88.2 14.2 %collective-permute-done.6 = bf16[192,1927]{1,0:T(8,128)(2,1)S(1)} collective-permute-done((bf16[192,1927]{1,0:T(8,128)(2,1)S(1)}, bf16[192,1927]{1,0:T(8,128)(2,1)S(1)}, u32[]{:S(2)}, u32[]{:S(2)}) %collective-permute-start.6) | collective-permute-done | bytes 740000 | tf_op jit(solution)/shard_map/ppermute | solution.py:200
  105.4 9.7 %fusion.167 = (bf16[1024,1536]{1,0:T(8,128)(2,1)S(1)}, f32[1024,1536]{1,0:T(8,128)}) fusion(bf16[1536,1927]{1,0:T(8,128)(2,1)} %bitcast.18, bf16[1,1024,1536]{2,1,0:T(8,128)(2,1)S(1)} %copy-done, f32[1536]{0:T(1024)S(1)} %convert_reduce_fusion.1, f32[1024]{0:T(1024)S(1)} %add_rsqrt_fusion.1), kind=kOutput, calls=%fused_computation.252 | convolution fusion | flops 4839702528 | bytes 17311744 | tf_op jit(solution)/shard_map/dot_general | solution.py:14
  138.6 3.9 fusion.168
  172.6 34.9 %collective-permute-done.8 = bf16[512,1536]{1,0:T(8,128)(2,1)S(1)} collective-permute-done((bf16[512,1536]{1,0:T(8,128)(2,1)S(1)}, bf16[512,1536]{1,0:T(8,128)(2,1)S(1)}, u32[]{:S(2)}, u32[]{:S(2)}) %collective-permute-start.8) | collective-permute-done | bytes 1572896 | tf_op jit(solution)/shard_map/ppermute | solution.py:254
  215.0 4.0 convert_select_fusion.7
  223.6 22.4 %all-gather.2.cloned.1.call-done = bf16[1536,3073]{1,0:T(8,128)(2,1)} async-done(((bf16[192,3073]{1,0:T(8,128)(2,1)}), bf16[1536,3073]{1,0:T(8,128)(2,1)}) %all-gather.2.cloned.1.call-update) | async-done | bytes 9440272 | tf_op jit(solution)/shard_map/all_gather | solution.py:300
  247.2 10.8 %fusion.35 = f32[1024,2048]{1,0:T(8,128)S(1)} fusion(bf16[1536,3073]{1,0:T(8,128)(2,1)} %all-gather.2.cloned.1.call-done, f32[1024,1536]{1,0:T(8,128)} %get-tuple-element.324, f32[1536]{0:T(1024)S(1)} %convert_reduce_fusion, f32[1024]{0:T(1024)S(1)} %add_rsqrt_fusion), kind=kOutput, calls=%fused_computation.58 | convolution fusion | flops 6447169536 | bytes 20981760 | tf_op jit(solution)/shard_map/dot_general | solution.py:14
  258.1 6.3 %fusion.45 = (bf16[1024,1024]{1,0:T(8,128)(2,1)S(1)}, bf16[1024,1024]{1,0:T(8,128)(2,1)S(1)}, bf16[1024,1024]{1,0:T(8,128)(2,1)}) fusion(f32[1024,2048]{1,0:T(8,128)S(1)} %fusion.35, bf16[1536,3073]{1,0:T(8,128)(2,1)S(1)} %copy-done.82, bf16[1,1024,1536]{2,1,0:T(8,128)(2,1)S(1)} %copy-done.33), kind=kOutput, calls=%fused_computation.71 | convolution fusion | flops 3238002688 | bytes 20971520 | tf_op jit(solution)/shard_map/dot_general | solution.py:14
  264.4 7.3 %fusion.54 = bf16[1024,1536]{1,0:T(8,128)(2,1)S(1)} fusion(bf16[1536,3073]{1,0:T(8,128)(2,1)S(1)} %copy-done.82, bf16[1024,1024]{1,0:T(8,128)(2,1)S(1)} %get-tuple-element.326, bf16[1024,1024]{1,0:T(8,128)(2,1)S(1)} %get-tuple-element.325), kind=kOutput, calls=%fused_computation.91 | convolution fusion | flops 6452412416 | bytes 13631488 | tf_op jit(solution)/shard_map/dot_general | solution.py:24
  281.1 9.6 %convolution_convert_fusion.1 = bf16[1536,2048]{1,0:T(8,128)(2,1)S(1)} fusion(bf16[1024,1024]{1,0:T(8,128)(2,1)} %copy-done.86, bf16[1024,1024]{1,0:T(8,128)(2,1)} %copy-done.85, f32[1024,1536]{1,0:T(8,128)S(1)} %bitcast.181, f32[1536]{0:T(1024)S(1)} %convert_reduce_fusion, f32[1024]{0:T(1024)S(1)} %add_rsqrt_fusion), kind=kOutput, calls=%fused_computation.26 | convolution fusion | flops 6458703872 | bytes 16787456 | tf_op jit(solution)/shard_map/dot_general | solution.py:18
  290.7 21.5 %collective-permute-done.11 = bf16[512,1536]{1,0:T(8,128)(2,1)S(1)} collective-permute-done((bf16[512,1536]{1,0:T(8,128)(2,1)S(1)}, bf16[512,1536]{1,0:T(8,128)(2,1)S(1)}, u32[]{:S(2)}, u32[]{:S(2)}) %collective-permute-start.11) | collective-permute-done | bytes 1572896 | tf_op jit(solution)/shard_map/ppermute | solution.py:254
  314.0 6.7 %convolution_convert_fusion.4 = bf16[1024,1536]{1,0:T(8,128)(2,1)} fusion(bf16[1024,1024]{1,0:T(8,128)(2,1)S(1)} %copy-done.89, bf16[1536,3073]{1,0:T(8,128)(2,1)} %all-gather.2.cloned.1.call-done), kind=kOutput, calls=%fused_computation.94 | convolution fusion | flops 3222798336 | bytes 8388608 | tf_op jit(solution)/shard_map/dot_general | solution.py:24
  320.7 4.7 pad_maximum_fusion
  331.6 6.2 %multiply_reduce_fusion = (bf16[1536]{0:T(1024)(128)(2,1)}, f32[1024]{0:T(1024)S(1)}) fusion(f32[1024,1536]{1,0:T(8,128)} %pad_maximum_fusion.1, f32[1024,1536]{1,0:T(8,128)} %get-tuple-element.324, f32[1024]{0:T(1024)S(1)} %add_rsqrt_fusion, f32[1536]{0:T(1024)S(1)} %convert_reduce_fusion), kind=kLoop, calls=%fused_computation.43 | loop fusion | flops 9434624 | bytes 12600320 | tf_op jit(solution)/shard_map/reduce_sum | solution.py:353
  344.0 6.9 %multiply_convert_fusion.3 = (bf16[1024,384]{1,0:T(8,128)(2,1)S(1)}, f32[1024,384]{1,0:T(8,128)}) fusion(f32[1024,1536]{1,0:T(8,128)} %get-tuple-element.366, bf16[1536,1927]{1,0:T(8,128)(2,1)} %bitcast.18, f32[1024,1536]{1,0:T(8,128)S(1)} %multiply_add_fusion), kind=kOutput, calls=%fused_computation.145 | convolution fusion | flops 1211498496 | bytes 11403264 | tf_op jit(solution)/shard_map/dot_general | solution.py:14
  352.4 4.8 fusion.104
  357.3 6.6 %fusion.38 = (f32[6,512]{1,0:T(8,128)}, f32[6,512]{1,0:T(8,128)}, bf16[6,512,512]{1,2,0:T(8,128)(2,1)S(1)}) fusion(f32[6,512]{1,0:T(8,128)S(1)} %copy-done.81, f32[6,512]{1,0:T(8,128)S(1)} %bitcast.212, bf16[512,6,64]{0,2,1:T(8,128)(2,1)S(1)} %bitcast.190, bf16[512,6,64]{0,2,1:T(8,128)(2,1)S(1)} %bitcast.209, f32[6,512,512]{1,2,0:T(8,128)} %copy-done.14, ...), kind=kOutput, calls=%fused_computation.61 | convolution fusion | flops 215476224 | bytes 10285056 | tf_op jit(solution)/shard_map/while/body/eval_jaxpr/qhd,khd->hqk/dot_general | solution.py:127
  363.9 10.8 %fusion.6 = (f32[6,1024]{1,0:T(8,128)}, f32[6,512]{1,0:T(8,128)}, bf16[6,512,1024]{2,1,0:T(8,128)(2,1)S(1)}) fusion(f32[6,1024]{1,0:T(8,128)S(1)} %copy-done.75, f32[6,512]{1,0:T(8,128)S(1)} %copy-done.79, f32[6,512]{1,0:T(8,128)S(1)} %bitcast.211, bf16[512,6,64]{0,2,1:T(8,128)(2,1)S(1)} %bitcast.192, bf16[1024,6,64]{0,2,1:T(8,128)(2,1)S(1)} %bitcast.206, ...), kind=kOutput, calls=%fused_computation.12 | convolution fusion | flops 430955520 | bytes 20152320 | tf_op jit(solution)/shard_map/while/body/eval_jaxpr/qhd,khd->hqk/dot_general | solution.py:127
  382.8 7.1 %fusion.81 = bf16[1024,6,64]{0,2,1:T(8,128)(2,1)} fusion(f32[512,6,64]{0,2,1:T(8,128)} %fusion.104, bf16[512,6,64]{0,2,1:T(8,128)(2,1)S(1)} %bitcast.193, f32[6,512,1024]{2,1,0:T(8,128)} %copy-done.4, f32[6,512]{1,0:T(8,128)S(1)} %copy-done.71), kind=kOutput, calls=%fused_computation.131 | convolution fusion | flops 409731072 | bytes 14561280 | tf_op jit(solution)/shard_map/while/body/eval_jaxpr/hqk,qhd->khd/dot_general | solution.py:136
  400.9 4.1 fusion.82
  411.1 9.6 %fusion.51 = bf16[1024,1536]{1,0:T(8,128)(2,1)S(1)} fusion(bf16[1024,1542]{1,0:T(8,128)(2,1)S(1)} %constant_dynamic-update-slice_fusion, bf16[1536,1927]{1,0:T(8,128)(2,1)} %bitcast.18), kind=kOutput, calls=%fused_computation.90 | convolution fusion | flops 4852285440 | bytes 11415552 | tf_op jit(solution)/shard_map/dot_general | solution.py:24
  431.0 5.5 fusion.123
  436.5 5.9 convolution_convert_fusion.5
  442.4 21.8 %collective-permute-done.17 = bf16[512,1536]{1,0:T(8,128)(2,1)} collective-permute-done((bf16[512,1536]{1,0:T(8,128)(2,1)}, bf16[512,1536]{1,0:T(8,128)(2,1)}, u32[]{:S(2)}, u32[]{:S(2)}) %collective-permute-start.17) | collective-permute-done | bytes 1572896 | tf_op jit(solution)/shard_map/ppermute | solution.py:254
  466.3 8.0 %convolution_convert_fusion = bf16[1536,1542]{1,0:T(8,128)(2,1)} fusion(bf16[1024,1542]{1,0:T(8,128)(2,1)S(1)} %copy-done.61, bf16[1,1024,1536]{2,1,0:T(8,128)(2,1)S(1)} %copy-done.1, f32[1536]{0:T(1024)S(1)} %copy-done.63, f32[1024]{0:T(1024)S(1)} %copy-done.73), kind=kOutput, calls=%fused_computation.25 | convolution fusion | flops 4859372544 | bytes 11051008 | tf_op jit(solution)/shard_map/dot_general | solution.py:397
  483.8 11.0 %concatenate.98 = bf16[1536,1929]{1,0:T(8,128)(2,1)} concatenate(bf16[1536,1542]{1,0:T(8,128)(2,1)} %convolution_convert_fusion, bf16[1536,1]{1,0:T(8,128)(2,1)} %fusion.123, bf16[1536,1]{1,0:T(8,128)(2,1)} %convert_element_type.399, bf16[1536,1]{1,0:T(8,128)(2,1)S(1)} %convert_element_type.400, bf16[1536,384]{1,0:T(8,128)(2,1)} %convolution_convert_fusion.5), dimensions={1} | concatenate | bytes 11851776 | tf_op jit(solution)/shard_map/concatenate | solution.py:403
  502.9 14.6 %collective-permute-done.19 = bf16[192,1929]{1,0:T(8,128)(2,1)} collective-permute-done((bf16[192,1929]{1,0:T(8,128)(2,1)}, bf16[192,1929]{1,0:T(8,128)(2,1)}, u32[]{:S(2)}, u32[]{:S(2)}) %collective-permute-start.19) | collective-permute-done | bytes 740768 | tf_op jit(solution)/shard_map/ppermute | solution.py:231
  523.1 15.3 %collective-permute-done.20 = bf16[192,1929]{1,0:T(8,128)(2,1)S(1)} collective-permute-done((bf16[192,1929]{1,0:T(8,128)(2,1)S(1)}, bf16[192,1929]{1,0:T(8,128)(2,1)S(1)}, u32[]{:S(2)}, u32[]{:S(2)}) %collective-permute-start.20) | collective-permute-done | bytes 740768 | tf_op jit(solution)/shard_map/ppermute | solution.py:231
  546.2 12.1 %collective-permute-done.21 = bf16[192,1929]{1,0:T(8,128)(2,1)S(1)} collective-permute-done((bf16[192,1929]{1,0:T(8,128)(2,1)S(1)}, bf16[192,1929]{1,0:T(8,128)(2,1)S(1)}, u32[]{:S(2)}, u32[]{:S(2)}) %collective-permute-start.21) | collective-permute-done | bytes 740768 | tf_op jit(solution)/shard_map/ppermute | solution.py:231
  568.9 9.1 %collective-permute-done.22 = bf16[192,1929]{1,0:T(8,128)(2,1)S(1)} collective-permute-done((bf16[192,1929]{1,0:T(8,128)(2,1)S(1)}, bf16[192,1929]{1,0:T(8,128)(2,1)S(1)}, u32[]{:S(2)}, u32[]{:S(2)}) %collective-permute-start.22) | collective-permute-done | bytes 740768 | tf_op jit(solution)/shard_map/ppermute | solution.py:231
  (360 shorter events, 214.6 us)
Async XLA Ops:
  7.2 238.8 %all-gather.2.cloned.1.call-start = ((), (), s32[]{:S(2)}) async-start(), calls=%async_computation.1 | async-start | bytes 11059200 | tf_op jit(solution)/shard_map/all_gather | solution.py:300
  10.1 37.2 %collective-permute-start.1 = (bf16[192,1927]{1,0:T(8,128)(2,1)S(1)}, bf16[192,1927]{1,0:T(8,128)(2,1)S(1)}, u32[]{:S(2)}, u32[]{:S(2)}) collective-permute-start(bf16[192,1927]{1,0:T(8,128)(2,1)S(1)} %concatenate.80), channel_id=1, source_target_pairs={{0,4},{8,0},{16,8},{24,16},{28,24},{20,28},{12,20},{4,12},{1,5},{9... | collective-permute-start | bytes 2219912 | tf_op jit(solution)/shard_map/ppermute | solution.py:204
  13.2 36.0 %collective-permute-start = (bf16[192,1927]{1,0:T(8,128)(2,1)S(1)}, bf16[192,1927]{1,0:T(8,128)(2,1)S(1)}, u32[]{:S(2)}, u32[]{:S(2)}) collective-permute-start(bf16[192,1927]{1,0:T(8,128)(2,1)S(1)} %concatenate.80), channel_id=1, source_target_pairs={{0,8},{8,16},{16,24},{24,28},{28,20},{20,12},{12,4},{4,0},{1,9},{9... | collective-permute-start | bytes 2219912 | tf_op jit(solution)/shard_map/ppermute | solution.py:200
  47.3 19.0 %collective-permute-start.3 = (bf16[192,1927]{1,0:T(8,128)(2,1)S(1)}, bf16[192,1927]{1,0:T(8,128)(2,1)S(1)}, u32[]{:S(2)}, u32[]{:S(2)}) collective-permute-start(bf16[192,1927]{1,0:T(8,128)(2,1)S(1)} %collective-permute-done.1), channel_id=1, source_target_pairs={{0,4},{8,0},{16,8},{24,16},{28,24},{20,28},{12,20},{4,12},{1,5},{9... | collective-permute-start | bytes 2219912 | tf_op jit(solution)/shard_map/ppermute | solution.py:204
  49.2 18.7 %collective-permute-start.2 = (bf16[192,1927]{1,0:T(8,128)(2,1)S(1)}, bf16[192,1927]{1,0:T(8,128)(2,1)S(1)}, u32[]{:S(2)}, u32[]{:S(2)}) collective-permute-start(bf16[192,1927]{1,0:T(8,128)(2,1)S(1)} %collective-permute-done), channel_id=1, source_target_pairs={{0,8},{8,16},{16,24},{24,28},{28,20},{20,12},{12,4},{4,0},{1,9},{9... | collective-permute-start | bytes 2219912 | tf_op jit(solution)/shard_map/ppermute | solution.py:200
  66.3 20.9 %collective-permute-start.5 = (bf16[192,1927]{1,0:T(8,128)(2,1)S(1)}, bf16[192,1927]{1,0:T(8,128)(2,1)S(1)}, u32[]{:S(2)}, u32[]{:S(2)}) collective-permute-start(bf16[192,1927]{1,0:T(8,128)(2,1)S(1)} %collective-permute-done.3), channel_id=1, source_target_pairs={{0,4},{8,0},{16,8},{24,16},{28,24},{20,28},{12,20},{4,12},{1,5},{9... | collective-permute-start | bytes 2219912 | tf_op jit(solution)/shard_map/ppermute | solution.py:204
  67.9 17.7 %collective-permute-start.4 = (bf16[192,1927]{1,0:T(8,128)(2,1)S(1)}, bf16[192,1927]{1,0:T(8,128)(2,1)S(1)}, u32[]{:S(2)}, u32[]{:S(2)}) collective-permute-start(bf16[192,1927]{1,0:T(8,128)(2,1)S(1)} %collective-permute-done.2), channel_id=1, source_target_pairs={{0,8},{8,16},{16,24},{24,28},{28,20},{20,12},{12,4},{4,0},{1,9},{9... | collective-permute-start | bytes 2219912 | tf_op jit(solution)/shard_map/ppermute | solution.py:200
  70.3 33.1 %copy-start = (bf16[1,1024,1536]{2,1,0:T(8,128)(2,1)S(1)}, bf16[1,1024,1536]{2,1,0:T(8,128)(2,1)}, u32[]{:S(2)}) copy-start(bf16[1,1024,1536]{2,1,0:T(8,128)(2,1)} %param.47) | copy-start | bytes 9437188
  85.6 16.7 %collective-permute-start.6 = (bf16[192,1927]{1,0:T(8,128)(2,1)S(1)}, bf16[192,1927]{1,0:T(8,128)(2,1)S(1)}, u32[]{:S(2)}, u32[]{:S(2)}) collective-permute-start(bf16[192,1927]{1,0:T(8,128)(2,1)S(1)} %collective-permute-done.4), channel_id=1, source_target_pairs={{0,8},{8,16},{16,24},{24,28},{28,20},{20,12},{12,4},{4,0},{1,9},{9... | collective-permute-start | bytes 2219912 | tf_op jit(solution)/shard_map/ppermute | solution.py:200
  103.4 480.2 %reduce-scatter.2.cloned.1.call-start = ((), (), s32[]{:S(2)}) async-start(), calls=%async_computation.2 | async-start | bytes 10616832 | tf_op jit(solution)/shard_map/reduce_scatter | solution.py:348
  165.0 3.8 collective-permute-start.7
  165.0 42.5 %copy-start.27 = (bf16[1024,1536]{1,0:T(8,128)(2,1)S(1)}, bf16[1024,1536]{1,0:T(8,128)(2,1)}, u32[]{:S(2)}) copy-start(bf16[1024,1536]{1,0:T(8,128)(2,1)} %copy-done.26) | copy-start | bytes 9437188
  171.0 36.5 %collective-permute-start.8 = (bf16[512,1536]{1,0:T(8,128)(2,1)S(1)}, bf16[512,1536]{1,0:T(8,128)(2,1)S(1)}, u32[]{:S(2)}, u32[]{:S(2)}) collective-permute-start(bf16[512,1536]{1,0:T(8,128)(2,1)S(1)} %fusion.72), channel_id=1, source_target_pairs={{0,2},{1,3},{2,0},{3,1},{4,6},{5,7},{6,4},{7,5},{8,10},{9,11},{10,... | collective-permute-start | bytes 4718600 | tf_op jit(solution)/shard_map/ppermute | solution.py:254
  211.2 3.8 collective-permute-start.9
  271.7 40.6 %copy-start.25 = (bf16[1024,1536]{1,0:T(8,128)(2,1)}, bf16[1024,1536]{1,0:T(8,128)(2,1)S(1)}, u32[]{:S(2)}) copy-start(bf16[1024,1536]{1,0:T(8,128)(2,1)S(1)} %fusion.54) | copy-start | bytes 9437188
  271.9 3.5 collective-permute-start.10
  275.7 36.5 %collective-permute-start.11 = (bf16[512,1536]{1,0:T(8,128)(2,1)S(1)}, bf16[512,1536]{1,0:T(8,128)(2,1)S(1)}, u32[]{:S(2)}, u32[]{:S(2)}) collective-permute-start(bf16[512,1536]{1,0:T(8,128)(2,1)S(1)} %fusion.73), channel_id=1, source_target_pairs={{0,2},{1,3},{2,0},{3,1},{4,6},{5,7},{6,4},{7,5},{8,10},{9,11},{10,... | collective-permute-start | bytes 4718600 | tf_op jit(solution)/shard_map/ppermute | solution.py:254
  314.0 11.5 %collective-permute-start.12 = (bf16[512,1536]{1,0:T(8,128)(2,1)}, bf16[512,1536]{1,0:T(8,128)(2,1)}, u32[]{:S(2)}, u32[]{:S(2)}) collective-permute-start(bf16[512,1536]{1,0:T(8,128)(2,1)} %fusion.133), channel_id=1, source_target_pairs={{0,1},{1,0},{2,3},{3,2},{4,5},{5,4},{6,7},{7,6},{8,9},{9,8},{10,11... | collective-permute-start | bytes 4718600 | tf_op jit(solution)/shard_map/ppermute | solution.py:255
  420.8 3.6 collective-permute-start.16
  427.2 37.0 %collective-permute-start.17 = (bf16[512,1536]{1,0:T(8,128)(2,1)}, bf16[512,1536]{1,0:T(8,128)(2,1)}, u32[]{:S(2)}, u32[]{:S(2)}) collective-permute-start(bf16[512,1536]{1,0:T(8,128)(2,1)} %fusion.75), channel_id=1, source_target_pairs={{0,2},{1,3},{2,0},{3,1},{4,6},{5,7},{6,4},{7,5},{8,10},{9,11},{10,... | collective-permute-start | bytes 4718600 | tf_op jit(solution)/shard_map/ppermute | solution.py:254
  430.3 44.1 %collective-permute-start.13 = (bf16[512,1536]{1,0:T(8,128)(2,1)S(1)}, bf16[512,1536]{1,0:T(8,128)(2,1)S(1)}, u32[]{:S(2)}, u32[]{:S(2)}) collective-permute-start(bf16[512,1536]{1,0:T(8,128)(2,1)S(1)} %constant_dynamic-slice_fusion.3), channel_id=1, source_target_pairs={{0,1},{1,0},{2,3},{3,2},{4,5},{5,4},{6,7},{7,6},{8,9},{9,8},{10,11... | collective-permute-start | bytes 4718600 | tf_op jit(solution)/shard_map/ppermute | solution.py:253
  436.5 29.8 %copy-start.61 = (bf16[1024,1542]{1,0:T(8,128)(2,1)S(1)}, bf16[1024,1542]{1,0:T(8,128)(2,1)}, u32[]{:S(2)}) copy-start(bf16[1024,1542]{1,0:T(8,128)(2,1)} %copy-done.60) | copy-start | bytes 9474052
  466.2 11.3 %collective-permute-start.18 = (bf16[512,1536]{1,0:T(8,128)(2,1)S(1)}, bf16[512,1536]{1,0:T(8,128)(2,1)S(1)}, u32[]{:S(2)}, u32[]{:S(2)}) collective-permute-start(bf16[512,1536]{1,0:T(8,128)(2,1)S(1)} %fusion.135), channel_id=1, source_target_pairs={{0,1},{1,0},{2,3},{3,2},{4,5},{5,4},{6,7},{7,6},{8,9},{9,8},{10,11... | collective-permute-start | bytes 4718600 | tf_op jit(solution)/shard_map/ppermute | solution.py:255
  476.0 43.8 %collective-permute-start.14 = (bf16[512,1536]{1,0:T(8,128)(2,1)}, bf16[512,1536]{1,0:T(8,128)(2,1)}, u32[]{:S(2)}, u32[]{:S(2)}) collective-permute-start(bf16[512,1536]{1,0:T(8,128)(2,1)} %fusion.74), channel_id=1, source_target_pairs={{0,2},{1,3},{2,0},{3,1},{4,6},{5,7},{6,4},{7,5},{8,10},{9,11},{10,... | collective-permute-start | bytes 4718600 | tf_op jit(solution)/shard_map/ppermute | solution.py:254
  497.5 20.0 %collective-permute-start.19 = (bf16[192,1929]{1,0:T(8,128)(2,1)}, bf16[192,1929]{1,0:T(8,128)(2,1)}, u32[]{:S(2)}, u32[]{:S(2)}) collective-permute-start(bf16[192,1929]{1,0:T(8,128)(2,1)} %get-tuple-element.340), channel_id=1, source_target_pairs={{0,8},{8,16},{16,24},{24,28},{28,20},{20,12},{12,4},{4,0},{1,9},{9... | collective-permute-start | bytes 2222216 | tf_op jit(solution)/shard_map/ppermute | solution.py:231
  500.8 22.2 %collective-permute-start.23 = (bf16[192,1929]{1,0:T(8,128)(2,1)}, bf16[192,1929]{1,0:T(8,128)(2,1)S(1)}, u32[]{:S(2)}, u32[]{:S(2)}) collective-permute-start(bf16[192,1929]{1,0:T(8,128)(2,1)} %get-tuple-element.341), channel_id=1, source_target_pairs={{0,4},{8,0},{16,8},{24,16},{28,24},{20,28},{12,20},{4,12},{1,5},{9... | collective-permute-start | bytes 2222216 | tf_op jit(solution)/shard_map/ppermute | solution.py:235
  519.3 19.0 %collective-permute-start.20 = (bf16[192,1929]{1,0:T(8,128)(2,1)S(1)}, bf16[192,1929]{1,0:T(8,128)(2,1)S(1)}, u32[]{:S(2)}, u32[]{:S(2)}) collective-permute-start(bf16[192,1929]{1,0:T(8,128)(2,1)S(1)} %add_convert_fusion.4), channel_id=1, source_target_pairs={{0,8},{8,16},{16,24},{24,28},{28,20},{20,12},{12,4},{4,0},{1,9},{9... | collective-permute-start | bytes 2222216 | tf_op jit(solution)/shard_map/ppermute | solution.py:231
  523.0 40.0 %collective-permute-start.15 = (bf16[512,1536]{1,0:T(8,128)(2,1)S(1)}, bf16[512,1536]{1,0:T(8,128)(2,1)S(1)}, u32[]{:S(2)}, u32[]{:S(2)}) collective-permute-start(bf16[512,1536]{1,0:T(8,128)(2,1)S(1)} %fusion.134), channel_id=1, source_target_pairs={{0,1},{1,0},{2,3},{3,2},{4,5},{5,4},{6,7},{7,6},{8,9},{9,8},{10,11... | collective-permute-start | bytes 4718600 | tf_op jit(solution)/shard_map/ppermute | solution.py:255
  540.3 18.0 %collective-permute-start.21 = (bf16[192,1929]{1,0:T(8,128)(2,1)S(1)}, bf16[192,1929]{1,0:T(8,128)(2,1)S(1)}, u32[]{:S(2)}, u32[]{:S(2)}) collective-permute-start(bf16[192,1929]{1,0:T(8,128)(2,1)S(1)} %get-tuple-element.338), channel_id=1, source_target_pairs={{0,8},{8,16},{16,24},{24,28},{28,20},{20,12},{12,4},{4,0},{1,9},{9... | collective-permute-start | bytes 2222216 | tf_op jit(solution)/shard_map/ppermute | solution.py:231
  541.0 17.9 %collective-permute-start.24 = (bf16[192,1929]{1,0:T(8,128)(2,1)S(1)}, bf16[192,1929]{1,0:T(8,128)(2,1)S(1)}, u32[]{:S(2)}, u32[]{:S(2)}) collective-permute-start(bf16[192,1929]{1,0:T(8,128)(2,1)S(1)} %get-tuple-element.339), channel_id=1, source_target_pairs={{0,4},{8,0},{16,8},{24,16},{28,24},{20,28},{12,20},{4,12},{1,5},{9... | collective-permute-start | bytes 2222216 | tf_op jit(solution)/shard_map/ppermute | solution.py:235
  560.9 17.1 %collective-permute-start.22 = (bf16[192,1929]{1,0:T(8,128)(2,1)S(1)}, bf16[192,1929]{1,0:T(8,128)(2,1)S(1)}, u32[]{:S(2)}, u32[]{:S(2)}) collective-permute-start(bf16[192,1929]{1,0:T(8,128)(2,1)S(1)} %get-tuple-element.336), channel_id=1, source_target_pairs={{0,8},{8,16},{16,24},{24,28},{28,20},{20,12},{12,4},{4,0},{1,9},{9... | collective-permute-start | bytes 2222216 | tf_op jit(solution)/shard_map/ppermute | solution.py:231
  562.1 16.5 %collective-permute-start.25 = (bf16[192,1929]{1,0:T(8,128)(2,1)S(1)}, bf16[192,1929]{1,0:T(8,128)(2,1)S(1)}, u32[]{:S(2)}, u32[]{:S(2)}) collective-permute-start(bf16[192,1929]{1,0:T(8,128)(2,1)S(1)} %get-tuple-element.337), channel_id=1, source_target_pairs={{0,4},{8,0},{16,8},{24,16},{28,24},{20,28},{12,20},{4,12},{1,5},{9... | collective-permute-start | bytes 2222216 | tf_op jit(solution)/shard_map/ppermute | solution.py:235
  (92 other events, 740.2 us)
Sparse Core Ops, SparseCore 0:
  103.5 142.5 all-gather.1
  331.7 160.4 reduce-scatter.1

commit v7 on v6

--- a/solution.py
+++ b/solution.py
@@ -350,7 +350,6 @@
     )
     ffn_term, grad_normed_two = lax.optimization_barrier((ffn_term, grad_normed_two))
     ffn_out = tensor_sum(ffn_term, "tensor")
-    grad_ffn_gain = jnp.sum(grad_normed_two * unit_two, axis=0)
     grad_unit_two = grad_normed_two * gain_two
     grad_hidden = upstream + scale_two * (
         grad_unit_two - unit_two * jnp.mean(grad_unit_two * unit_two, axis=-1, keepdims=True)
@@ -394,6 +393,8 @@
     bias_col = jnp.where(
         place < heads_here, jnp.take(grad_bias, jnp.minimum(place, heads_here - 1)), 0.0
     )
+    late_normed_two, grad_five = lax.optimization_barrier((grad_normed_two, grad_five))
+    grad_ffn_gain = jnp.sum(late_normed_two * unit_two, axis=0)
     late_grads = lax.dot_general(
         grad_five, normed, (((0,), (0,)), ((), ())), preferred_element_type=jnp.float32
     ).T

time: 601 us -> 598 us (level)
    unnamed x196 -> x198, local copies, waits for them, and re-layouts: 14.9 us -> 15.9 us
  transfers between devices with their start and end apart: 28 -> 28, of which waited for: 17 -> 17; matrix products, arithmetic and copies ran while one was open for 46% -> 47% of each run, Pallas kernels for 0% -> 0%
where the time goes in v7:
time: 598 us; the launch traced here: 592 us
  waiting for transfers between devices  207 us (35%)
  matrix products  141 us (24%)
  other arithmetic  99.9 us (17%)
  local copies, waits for them, and re-layouts  89.1 us (15%)
  between operations  33.2 us (6%)
  starting transfers between devices  21.5 us (4%)
    ppermute x4, waiting for transfers between devices, tensor_sum(): lax.ppermute(mine.astype(term.dtype), axis, across).astype(jnp.float32)  76.6 us
    ppermute x4, waiting for transfers between devices, ring_reduce_scatter(): part_next = lax.ppermute(part_next.astype(jnp.bfloat16), axis, to_next)  51.5 us
    dot_general x5, matrix products, project(): return jnp.dot(left, right, preferred_element_type=jnp.float32)  35.9 us
    ppermute x4, waiting for transfers between devices, ring_gather(): moving_next = lax.ppermute(moving_next, axis, to_next)  29.4 us
    dot_general x4, matrix products, contract_cols(): lax.dot_general(left, right, (((1,), (1,)), ((), ())), preferred_element_...  27 us
    all_gather x1, waiting for transfers between devices, on_device(): ffn_full = lax.all_gather(ffn_local, 'dp', axis=0, tiled=True)  22.5 us
    dot_general x2, matrix products, attend_backward(): jnp.einsum('qhd,khd->hqk', out_rows, value_rows, preferred_element_type=j...  17.4 us
    dot_general x3, matrix products, contract_rows(): lax.dot_general(left, right, (((0,), (0,)), ((), ())), preferred_element_...  16.3 us
  transfers between devices with their start and end apart: 28, of which 17 were waited for; matrix products, arithmetic and copies ran while one was open for 47% of the time, Pallas kernels for 0%

profile of v7, /device:TPU:0, one launch (start us, length us, event | category | flops | bytes accessed | tf_op | source)
XLA Modules:
  0.0 592.2 jit_solution(14487150692387822874)
XLA Ops:
  50.7 15.1 %collective-permute-done.3 = bf16[192,1927]{1,0:T(8,128)(2,1)S(1)} collective-permute-done((bf16[192,1927]{1,0:T(8,128)(2,1)S(1)}, bf16[192,1927]{1,0:T(8,128)(2,1)S(1)}, u32[]{:S(2)}, u32[]{:S(2)}) %collective-permute-start.3) | collective-permute-done | bytes 740000 | tf_op jit(solution)/shard_map/ppermute | solution.py:204
  69.8 15.3 %collective-permute-done.4 = bf16[192,1927]{1,0:T(8,128)(2,1)S(1)} collective-permute-done((bf16[192,1927]{1,0:T(8,128)(2,1)S(1)}, bf16[192,1927]{1,0:T(8,128)(2,1)S(1)}, u32[]{:S(2)}, u32[]{:S(2)}) %collective-permute-start.4) | collective-permute-done | bytes 740000 | tf_op jit(solution)/shard_map/ppermute | solution.py:200
  87.7 14.2 %collective-permute-done.6 = bf16[192,1927]{1,0:T(8,128)(2,1)S(1)} collective-permute-done((bf16[192,1927]{1,0:T(8,128)(2,1)S(1)}, bf16[192,1927]{1,0:T(8,128)(2,1)S(1)}, u32[]{:S(2)}, u32[]{:S(2)}) %collective-permute-start.6) | collective-permute-done | bytes 740000 | tf_op jit(solution)/shard_map/ppermute | solution.py:200
  104.9 9.7 %fusion.167 = (bf16[1024,1536]{1,0:T(8,128)(2,1)S(1)}, f32[1024,1536]{1,0:T(8,128)}) fusion(bf16[1536,1927]{1,0:T(8,128)(2,1)} %bitcast.18, bf16[1,1024,1536]{2,1,0:T(8,128)(2,1)S(1)} %copy-done.1, f32[1536]{0:T(1024)S(1)} %convert_reduce_fusion.1, f32[1024]{0:T(1024)S(1)} %add_rsqrt_fusion.1), kind=kOutput, calls=%fused_computation.252 | convolution fusion | flops 4839702528 | bytes 17311744 | tf_op jit(solution)/shard_map/dot_general | solution.py:14
  138.0 3.9 fusion.168
  172.0 34.9 %collective-permute-done.8 = bf16[512,1536]{1,0:T(8,128)(2,1)S(1)} collective-permute-done((bf16[512,1536]{1,0:T(8,128)(2,1)S(1)}, bf16[512,1536]{1,0:T(8,128)(2,1)S(1)}, u32[]{:S(2)}, u32[]{:S(2)}) %collective-permute-start.8) | collective-permute-done | bytes 1572896 | tf_op jit(solution)/shard_map/ppermute | solution.py:254
  214.4 4.0 convert_select_fusion.7
  223.0 22.5 %all-gather.2.cloned.1.call-done = bf16[1536,3073]{1,0:T(8,128)(2,1)} async-done(((bf16[192,3073]{1,0:T(8,128)(2,1)}), bf16[1536,3073]{1,0:T(8,128)(2,1)}) %all-gather.2.cloned.1.call-update) | async-done | bytes 9440272 | tf_op jit(solution)/shard_map/all_gather | solution.py:300
  246.7 10.8 %fusion.35 = f32[1024,2048]{1,0:T(8,128)S(1)} fusion(bf16[1536,3073]{1,0:T(8,128)(2,1)} %all-gather.2.cloned.1.call-done, f32[1024,1536]{1,0:T(8,128)} %get-tuple-element.326, f32[1536]{0:T(1024)S(1)} %convert_reduce_fusion, f32[1024]{0:T(1024)S(1)} %add_rsqrt_fusion), kind=kOutput, calls=%fused_computation.58 | convolution fusion | flops 6447169536 | bytes 20981760 | tf_op jit(solution)/shard_map/dot_general | solution.py:14
  257.6 6.3 %fusion.45 = (bf16[1024,1024]{1,0:T(8,128)(2,1)S(1)}, bf16[1024,1024]{1,0:T(8,128)(2,1)S(1)}, bf16[1024,1024]{1,0:T(8,128)(2,1)}) fusion(f32[1024,2048]{1,0:T(8,128)S(1)} %fusion.35, bf16[1536,3073]{1,0:T(8,128)(2,1)S(1)} %copy-done.81, bf16[1,1024,1536]{2,1,0:T(8,128)(2,1)S(1)} %copy-done.32), kind=kOutput, calls=%fused_computation.71 | convolution fusion | flops 3238002688 | bytes 20971520 | tf_op jit(solution)/shard_map/dot_general | solution.py:14
  263.8 7.3 %fusion.54 = bf16[1024,1536]{1,0:T(8,128)(2,1)S(1)} fusion(bf16[1536,3073]{1,0:T(8,128)(2,1)S(1)} %copy-done.81, bf16[1024,1024]{1,0:T(8,128)(2,1)S(1)} %get-tuple-element.328, bf16[1024,1024]{1,0:T(8,128)(2,1)S(1)} %get-tuple-element.327), kind=kOutput, calls=%fused_computation.91 | convolution fusion | flops 6452412416 | bytes 13631488 | tf_op jit(solution)/shard_map/dot_general | solution.py:24
  280.6 9.6 %convolution_convert_fusion.1 = bf16[1536,2048]{1,0:T(8,128)(2,1)S(1)} fusion(bf16[1024,1024]{1,0:T(8,128)(2,1)} %copy-done.85, bf16[1024,1024]{1,0:T(8,128)(2,1)} %copy-done.84, f32[1024,1536]{1,0:T(8,128)S(1)} %bitcast.179, f32[1536]{0:T(1024)S(1)} %convert_reduce_fusion, f32[1024]{0:T(1024)S(1)} %add_rsqrt_fusion), kind=kOutput, calls=%fused_computation.26 | convolution fusion | flops 6458703872 | bytes 16787456 | tf_op jit(solution)/shard_map/dot_general | solution.py:18
  290.2 21.5 %collective-permute-done.11 = bf16[512,1536]{1,0:T(8,128)(2,1)S(1)} collective-permute-done((bf16[512,1536]{1,0:T(8,128)(2,1)S(1)}, bf16[512,1536]{1,0:T(8,128)(2,1)S(1)}, u32[]{:S(2)}, u32[]{:S(2)}) %collective-permute-start.11) | collective-permute-done | bytes 1572896 | tf_op jit(solution)/shard_map/ppermute | solution.py:254
  313.5 6.7 %convolution_convert_fusion.4 = bf16[1024,1536]{1,0:T(8,128)(2,1)} fusion(bf16[1024,1024]{1,0:T(8,128)(2,1)S(1)} %copy-done.88, bf16[1536,3073]{1,0:T(8,128)(2,1)} %all-gather.2.cloned.1.call-done), kind=kOutput, calls=%fused_computation.94 | convolution fusion | flops 3222798336 | bytes 8388608 | tf_op jit(solution)/shard_map/dot_general | solution.py:24
  320.2 4.8 pad_maximum_fusion
  331.0 5.7 multiply_reduce_fusion.1
  343.5 7.0 %multiply_convert_fusion.3 = (bf16[1024,384]{1,0:T(8,128)(2,1)S(1)}, f32[1024,384]{1,0:T(8,128)}) fusion(f32[1024,1536]{1,0:T(8,128)} %get-tuple-element.368, bf16[1536,1927]{1,0:T(8,128)(2,1)} %bitcast.18, f32[1024,1536]{1,0:T(8,128)S(1)} %multiply_add_fusion), kind=kOutput, calls=%fused_computation.145 | convolution fusion | flops 1211498496 | bytes 11403264 | tf_op jit(solution)/shard_map/dot_general | solution.py:14
  351.9 4.8 fusion.104
  356.8 6.6 %fusion.38 = (f32[6,512]{1,0:T(8,128)}, f32[6,512]{1,0:T(8,128)}, bf16[6,512,512]{1,2,0:T(8,128)(2,1)S(1)}) fusion(f32[6,512]{1,0:T(8,128)S(1)} %copy-done.80, f32[6,512]{1,0:T(8,128)S(1)} %bitcast.214, bf16[512,6,64]{0,2,1:T(8,128)(2,1)S(1)} %bitcast.192, bf16[512,6,64]{0,2,1:T(8,128)(2,1)S(1)} %bitcast.211, f32[6,512,512]{1,2,0:T(8,128)} %copy-done.14, ...), kind=kOutput, calls=%fused_computation.61 | convolution fusion | flops 215476224 | bytes 10285056 | tf_op jit(solution)/shard_map/while/body/eval_jaxpr/qhd,khd->hqk/dot_general | solution.py:127
  363.4 10.8 %fusion.6 = (f32[6,1024]{1,0:T(8,128)}, f32[6,512]{1,0:T(8,128)}, bf16[6,512,1024]{2,1,0:T(8,128)(2,1)S(1)}) fusion(f32[6,1024]{1,0:T(8,128)S(1)} %copy-done.75, f32[6,512]{1,0:T(8,128)S(1)} %copy-done.78, f32[6,512]{1,0:T(8,128)S(1)} %bitcast.213, bf16[512,6,64]{0,2,1:T(8,128)(2,1)S(1)} %bitcast.194, bf16[1024,6,64]{0,2,1:T(8,128)(2,1)S(1)} %bitcast.208, ...), kind=kOutput, calls=%fused_computation.12 | convolution fusion | flops 430955520 | bytes 20152320 | tf_op jit(solution)/shard_map/while/body/eval_jaxpr/qhd,khd->hqk/dot_general | solution.py:127
  382.2 7.1 %fusion.81 = bf16[1024,6,64]{0,2,1:T(8,128)(2,1)} fusion(f32[512,6,64]{0,2,1:T(8,128)} %fusion.104, bf16[512,6,64]{0,2,1:T(8,128)(2,1)S(1)} %bitcast.195, f32[6,512,1024]{2,1,0:T(8,128)} %copy-done.4, f32[6,512]{1,0:T(8,128)} %log_add_fusion), kind=kOutput, calls=%fused_computation.131 | convolution fusion | flops 409731072 | bytes 14561280 | tf_op jit(solution)/shard_map/while/body/eval_jaxpr/hqk,qhd->khd/dot_general | solution.py:136
  400.2 4.1 fusion.82
  410.5 9.6 %fusion.51 = bf16[1024,1536]{1,0:T(8,128)(2,1)S(1)} fusion(bf16[1024,1542]{1,0:T(8,128)(2,1)S(1)} %constant_dynamic-update-slice_fusion, bf16[1536,1927]{1,0:T(8,128)(2,1)} %bitcast.18), kind=kOutput, calls=%fused_computation.90 | convolution fusion | flops 4852285440 | bytes 11415552 | tf_op jit(solution)/shard_map/dot_general | solution.py:24
  429.6 5.4 multiply_reduce_fusion
  435.9 5.5 fusion.123
  444.3 20.2 %collective-permute-done.17 = bf16[512,1536]{1,0:T(8,128)(2,1)S(1)} collective-permute-done((bf16[512,1536]{1,0:T(8,128)(2,1)S(1)}, bf16[512,1536]{1,0:T(8,128)(2,1)S(1)}, u32[]{:S(2)}, u32[]{:S(2)}) %collective-permute-start.17) | collective-permute-done | bytes 1572896 | tf_op jit(solution)/shard_map/ppermute | solution.py:254
  465.2 8.1 %convolution_convert_fusion = bf16[1536,1542]{1,0:T(8,128)(2,1)} fusion(bf16[1024,1542]{1,0:T(8,128)(2,1)S(1)} %copy-done.60, bf16[1,1024,1536]{2,1,0:T(8,128)(2,1)S(1)} %copy-done.2, f32[1536]{0:T(1024)S(1)} %copy-done.62, f32[1024]{0:T(1024)S(1)} %copy-done.73), kind=kOutput, calls=%fused_computation.25 | convolution fusion | flops 4859372544 | bytes 11051008 | tf_op jit(solution)/shard_map/dot_general | solution.py:398
  481.3 11.0 %concatenate.98 = bf16[1536,1929]{1,0:T(8,128)(2,1)} concatenate(bf16[1536,1542]{1,0:T(8,128)(2,1)} %convolution_convert_fusion, bf16[1536,1]{1,0:T(8,128)(2,1)} %fusion.123, bf16[1536,1]{1,0:T(8,128)(2,1)} %convert_element_type.399, bf16[1536,1]{1,0:T(8,128)(2,1)S(1)} %convert_element_type.400, bf16[1536,384]{1,0:T(8,128)(2,1)} %convolution_convert_fusion.5), dimensions={1} | concatenate | bytes 11851776 | tf_op jit(solution)/shard_map/concatenate | solution.py:404
  500.2 14.7 %collective-permute-done.19 = bf16[192,1929]{1,0:T(8,128)(2,1)} collective-permute-done((bf16[192,1929]{1,0:T(8,128)(2,1)}, bf16[192,1929]{1,0:T(8,128)(2,1)}, u32[]{:S(2)}, u32[]{:S(2)}) %collective-permute-start.19) | collective-permute-done | bytes 740768 | tf_op jit(solution)/shard_map/ppermute | solution.py:231
  520.6 15.4 %collective-permute-done.20 = bf16[192,1929]{1,0:T(8,128)(2,1)S(1)} collective-permute-done((bf16[192,1929]{1,0:T(8,128)(2,1)S(1)}, bf16[192,1929]{1,0:T(8,128)(2,1)S(1)}, u32[]{:S(2)}, u32[]{:S(2)}) %collective-permute-start.20) | collective-permute-done | bytes 740768 | tf_op jit(solution)/shard_map/ppermute | solution.py:231
  543.7 12.2 %collective-permute-done.21 = bf16[192,1929]{1,0:T(8,128)(2,1)S(1)} collective-permute-done((bf16[192,1929]{1,0:T(8,128)(2,1)S(1)}, bf16[192,1929]{1,0:T(8,128)(2,1)S(1)}, u32[]{:S(2)}, u32[]{:S(2)}) %collective-permute-start.21) | collective-permute-done | bytes 740768 | tf_op jit(solution)/shard_map/ppermute | solution.py:231
  566.5 9.2 %collective-permute-done.22 = bf16[192,1929]{1,0:T(8,128)(2,1)S(1)} collective-permute-done((bf16[192,1929]{1,0:T(8,128)(2,1)S(1)}, bf16[192,1929]{1,0:T(8,128)(2,1)S(1)}, u32[]{:S(2)}, u32[]{:S(2)}) %collective-permute-start.22) | collective-permute-done | bytes 740768 | tf_op jit(solution)/shard_map/ppermute | solution.py:231
  (364 shorter events, 215.0 us)
Async XLA Ops:
  7.2 28.0 %copy-start.82 = (bf16[192]{0:T(256)(128)(2,1)S(1)}, bf16[192]{0:T(256)(128)(2,1)}, u32[]{:S(2)}) copy-start(bf16[192]{0:T(256)(128)(2,1)} %param.57) | copy-start | bytes 1156
  7.2 238.3 %all-gather.2.cloned.1.call-start = ((), (), s32[]{:S(2)}) async-start(), calls=%async_computation.1 | async-start | bytes 11059200 | tf_op jit(solution)/shard_map/all_gather | solution.py:300
  10.1 36.7 %collective-permute-start.1 = (bf16[192,1927]{1,0:T(8,128)(2,1)S(1)}, bf16[192,1927]{1,0:T(8,128)(2,1)S(1)}, u32[]{:S(2)}, u32[]{:S(2)}) collective-permute-start(bf16[192,1927]{1,0:T(8,128)(2,1)S(1)} %concatenate.80), channel_id=1, source_target_pairs={{0,4},{8,0},{16,8},{24,16},{28,24},{20,28},{12,20},{4,12},{1,5},{9... | collective-permute-start | bytes 2219912 | tf_op jit(solution)/shard_map/ppermute | solution.py:204
  13.2 35.5 %collective-permute-start = (bf16[192,1927]{1,0:T(8,128)(2,1)S(1)}, bf16[192,1927]{1,0:T(8,128)(2,1)S(1)}, u32[]{:S(2)}, u32[]{:S(2)}) collective-permute-start(bf16[192,1927]{1,0:T(8,128)(2,1)S(1)} %concatenate.80), channel_id=1, source_target_pairs={{0,8},{8,16},{16,24},{24,28},{28,20},{20,12},{12,4},{4,0},{1,9},{9... | collective-permute-start | bytes 2219912 | tf_op jit(solution)/shard_map/ppermute | solution.py:200
  46.8 19.0 %collective-permute-start.3 = (bf16[192,1927]{1,0:T(8,128)(2,1)S(1)}, bf16[192,1927]{1,0:T(8,128)(2,1)S(1)}, u32[]{:S(2)}, u32[]{:S(2)}) collective-permute-start(bf16[192,1927]{1,0:T(8,128)(2,1)S(1)} %collective-permute-done.1), channel_id=1, source_target_pairs={{0,4},{8,0},{16,8},{24,16},{28,24},{20,28},{12,20},{4,12},{1,5},{9... | collective-permute-start | bytes 2219912 | tf_op jit(solution)/shard_map/ppermute | solution.py:204
  48.7 18.7 %collective-permute-start.2 = (bf16[192,1927]{1,0:T(8,128)(2,1)S(1)}, bf16[192,1927]{1,0:T(8,128)(2,1)S(1)}, u32[]{:S(2)}, u32[]{:S(2)}) collective-permute-start(bf16[192,1927]{1,0:T(8,128)(2,1)S(1)} %collective-permute-done), channel_id=1, source_target_pairs={{0,8},{8,16},{16,24},{24,28},{28,20},{20,12},{12,4},{4,0},{1,9},{9... | collective-permute-start | bytes 2219912 | tf_op jit(solution)/shard_map/ppermute | solution.py:200
  65.8 20.9 %collective-permute-start.5 = (bf16[192,1927]{1,0:T(8,128)(2,1)S(1)}, bf16[192,1927]{1,0:T(8,128)(2,1)S(1)}, u32[]{:S(2)}, u32[]{:S(2)}) collective-permute-start(bf16[192,1927]{1,0:T(8,128)(2,1)S(1)} %collective-permute-done.3), channel_id=1, source_target_pairs={{0,4},{8,0},{16,8},{24,16},{28,24},{20,28},{12,20},{4,12},{1,5},{9... | collective-permute-start | bytes 2219912 | tf_op jit(solution)/shard_map/ppermute | solution.py:204
  67.4 17.7 %collective-permute-start.4 = (bf16[192,1927]{1,0:T(8,128)(2,1)S(1)}, bf16[192,1927]{1,0:T(8,128)(2,1)S(1)}, u32[]{:S(2)}, u32[]{:S(2)}) collective-permute-start(bf16[192,1927]{1,0:T(8,128)(2,1)S(1)} %collective-permute-done.2), channel_id=1, source_target_pairs={{0,8},{8,16},{16,24},{24,28},{28,20},{20,12},{12,4},{4,0},{1,9},{9... | collective-permute-start | bytes 2219912 | tf_op jit(solution)/shard_map/ppermute | solution.py:200
  69.8 33.1 %copy-start.1 = (bf16[1,1024,1536]{2,1,0:T(8,128)(2,1)S(1)}, bf16[1,1024,1536]{2,1,0:T(8,128)(2,1)}, u32[]{:S(2)}) copy-start(bf16[1,1024,1536]{2,1,0:T(8,128)(2,1)} %param.47) | copy-start | bytes 9437188
  85.1 16.7 %collective-permute-start.6 = (bf16[192,1927]{1,0:T(8,128)(2,1)S(1)}, bf16[192,1927]{1,0:T(8,128)(2,1)S(1)}, u32[]{:S(2)}, u32[]{:S(2)}) collective-permute-start(bf16[192,1927]{1,0:T(8,128)(2,1)S(1)} %collective-permute-done.4), channel_id=1, source_target_pairs={{0,8},{8,16},{16,24},{24,28},{28,20},{20,12},{12,4},{4,0},{1,9},{9... | collective-permute-start | bytes 2219912 | tf_op jit(solution)/shard_map/ppermute | solution.py:200
  102.8 478.4 %reduce-scatter.2.cloned.1.call-start = ((), (), s32[]{:S(2)}) async-start(), calls=%async_computation.2 | async-start | bytes 10616832 | tf_op jit(solution)/shard_map/reduce_scatter | solution.py:348
  164.4 3.8 collective-permute-start.7
  164.4 42.5 %copy-start.26 = (bf16[1024,1536]{1,0:T(8,128)(2,1)S(1)}, bf16[1024,1536]{1,0:T(8,128)(2,1)}, u32[]{:S(2)}) copy-start(bf16[1024,1536]{1,0:T(8,128)(2,1)} %copy-done.25) | copy-start | bytes 9437188
  170.5 36.5 %collective-permute-start.8 = (bf16[512,1536]{1,0:T(8,128)(2,1)S(1)}, bf16[512,1536]{1,0:T(8,128)(2,1)S(1)}, u32[]{:S(2)}, u32[]{:S(2)}) collective-permute-start(bf16[512,1536]{1,0:T(8,128)(2,1)S(1)} %fusion.72), channel_id=1, source_target_pairs={{0,2},{1,3},{2,0},{3,1},{4,6},{5,7},{6,4},{7,5},{8,10},{9,11},{10,... | collective-permute-start | bytes 4718600 | tf_op jit(solution)/shard_map/ppermute | solution.py:254
  210.7 3.8 collective-permute-start.9
  271.2 40.6 %copy-start.24 = (bf16[1024,1536]{1,0:T(8,128)(2,1)}, bf16[1024,1536]{1,0:T(8,128)(2,1)S(1)}, u32[]{:S(2)}) copy-start(bf16[1024,1536]{1,0:T(8,128)(2,1)S(1)} %fusion.54) | copy-start | bytes 9437188
  271.4 3.5 collective-permute-start.10
  275.2 36.5 %collective-permute-start.11 = (bf16[512,1536]{1,0:T(8,128)(2,1)S(1)}, bf16[512,1536]{1,0:T(8,128)(2,1)S(1)}, u32[]{:S(2)}, u32[]{:S(2)}) collective-permute-start(bf16[512,1536]{1,0:T(8,128)(2,1)S(1)} %fusion.73), channel_id=1, source_target_pairs={{0,2},{1,3},{2,0},{3,1},{4,6},{5,7},{6,4},{7,5},{8,10},{9,11},{10,... | collective-permute-start | bytes 4718600 | tf_op jit(solution)/shard_map/ppermute | solution.py:254
  313.5 11.5 %collective-permute-start.12 = (bf16[512,1536]{1,0:T(8,128)(2,1)}, bf16[512,1536]{1,0:T(8,128)(2,1)}, u32[]{:S(2)}, u32[]{:S(2)}) collective-permute-start(bf16[512,1536]{1,0:T(8,128)(2,1)} %fusion.133), channel_id=1, source_target_pairs={{0,1},{1,0},{2,3},{3,2},{4,5},{5,4},{6,7},{7,6},{8,9},{9,8},{10,11... | collective-permute-start | bytes 4718600 | tf_op jit(solution)/shard_map/ppermute | solution.py:255
  421.8 3.5 collective-permute-start.16
  427.8 36.7 %collective-permute-start.17 = (bf16[512,1536]{1,0:T(8,128)(2,1)S(1)}, bf16[512,1536]{1,0:T(8,128)(2,1)S(1)}, u32[]{:S(2)}, u32[]{:S(2)}) collective-permute-start(bf16[512,1536]{1,0:T(8,128)(2,1)S(1)} %fusion.75), channel_id=1, source_target_pairs={{0,2},{1,3},{2,0},{3,1},{4,6},{5,7},{6,4},{7,5},{8,10},{9,11},{10,... | collective-permute-start | bytes 4718600 | tf_op jit(solution)/shard_map/ppermute | solution.py:254
  429.4 43.9 %collective-permute-start.13 = (bf16[512,1536]{1,0:T(8,128)(2,1)S(1)}, bf16[512,1536]{1,0:T(8,128)(2,1)S(1)}, u32[]{:S(2)}, u32[]{:S(2)}) collective-permute-start(bf16[512,1536]{1,0:T(8,128)(2,1)S(1)} %constant_dynamic-slice_fusion.3), channel_id=1, source_target_pairs={{0,1},{1,0},{2,3},{3,2},{4,5},{5,4},{6,7},{7,6},{8,9},{9,8},{10,11... | collective-permute-start | bytes 4718600 | tf_op jit(solution)/shard_map/ppermute | solution.py:253
  465.1 11.3 %collective-permute-start.18 = (bf16[512,1536]{1,0:T(8,128)(2,1)S(1)}, bf16[512,1536]{1,0:T(8,128)(2,1)S(1)}, u32[]{:S(2)}, u32[]{:S(2)}) collective-permute-start(bf16[512,1536]{1,0:T(8,128)(2,1)S(1)} %fusion.135), channel_id=1, source_target_pairs={{0,1},{1,0},{2,3},{3,2},{4,5},{5,4},{6,7},{7,6},{8,9},{9,8},{10,11... | collective-permute-start | bytes 4718600 | tf_op jit(solution)/shard_map/ppermute | solution.py:255
  475.0 42.3 %collective-permute-start.14 = (bf16[512,1536]{1,0:T(8,128)(2,1)}, bf16[512,1536]{1,0:T(8,128)(2,1)}, u32[]{:S(2)}, u32[]{:S(2)}) collective-permute-start(bf16[512,1536]{1,0:T(8,128)(2,1)} %fusion.74), channel_id=1, source_target_pairs={{0,2},{1,3},{2,0},{3,1},{4,6},{5,7},{6,4},{7,5},{8,10},{9,11},{10,... | collective-permute-start | bytes 4718600 | tf_op jit(solution)/shard_map/ppermute | solution.py:254
  494.9 20.0 %collective-permute-start.19 = (bf16[192,1929]{1,0:T(8,128)(2,1)}, bf16[192,1929]{1,0:T(8,128)(2,1)}, u32[]{:S(2)}, u32[]{:S(2)}) collective-permute-start(bf16[192,1929]{1,0:T(8,128)(2,1)} %get-tuple-element.342), channel_id=1, source_target_pairs={{0,8},{8,16},{16,24},{24,28},{28,20},{20,12},{12,4},{4,0},{1,9},{9... | collective-permute-start | bytes 2222216 | tf_op jit(solution)/shard_map/ppermute | solution.py:231
  498.2 22.4 %collective-permute-start.23 = (bf16[192,1929]{1,0:T(8,128)(2,1)}, bf16[192,1929]{1,0:T(8,128)(2,1)S(1)}, u32[]{:S(2)}, u32[]{:S(2)}) collective-permute-start(bf16[192,1929]{1,0:T(8,128)(2,1)} %get-tuple-element.343), channel_id=1, source_target_pairs={{0,4},{8,0},{16,8},{24,16},{28,24},{20,28},{12,20},{4,12},{1,5},{9... | collective-permute-start | bytes 2222216 | tf_op jit(solution)/shard_map/ppermute | solution.py:235
  516.8 19.1 %collective-permute-start.20 = (bf16[192,1929]{1,0:T(8,128)(2,1)S(1)}, bf16[192,1929]{1,0:T(8,128)(2,1)S(1)}, u32[]{:S(2)}, u32[]{:S(2)}) collective-permute-start(bf16[192,1929]{1,0:T(8,128)(2,1)S(1)} %add_convert_fusion.4), channel_id=1, source_target_pairs={{0,8},{8,16},{16,24},{24,28},{28,20},{20,12},{12,4},{4,0},{1,9},{9... | collective-permute-start | bytes 2222216 | tf_op jit(solution)/shard_map/ppermute | solution.py:231
  520.5 40.1 %collective-permute-start.15 = (bf16[512,1536]{1,0:T(8,128)(2,1)S(1)}, bf16[512,1536]{1,0:T(8,128)(2,1)S(1)}, u32[]{:S(2)}, u32[]{:S(2)}) collective-permute-start(bf16[512,1536]{1,0:T(8,128)(2,1)S(1)} %fusion.134), channel_id=1, source_target_pairs={{0,1},{1,0},{2,3},{3,2},{4,5},{5,4},{6,7},{7,6},{8,9},{9,8},{10,11... | collective-permute-start | bytes 4718600 | tf_op jit(solution)/shard_map/ppermute | solution.py:255
  537.9 18.1 %collective-permute-start.21 = (bf16[192,1929]{1,0:T(8,128)(2,1)S(1)}, bf16[192,1929]{1,0:T(8,128)(2,1)S(1)}, u32[]{:S(2)}, u32[]{:S(2)}) collective-permute-start(bf16[192,1929]{1,0:T(8,128)(2,1)S(1)} %get-tuple-element.340), channel_id=1, source_target_pairs={{0,8},{8,16},{16,24},{24,28},{28,20},{20,12},{12,4},{4,0},{1,9},{9... | collective-permute-start | bytes 2222216 | tf_op jit(solution)/shard_map/ppermute | solution.py:231
  538.5 18.0 %collective-permute-start.24 = (bf16[192,1929]{1,0:T(8,128)(2,1)S(1)}, bf16[192,1929]{1,0:T(8,128)(2,1)S(1)}, u32[]{:S(2)}, u32[]{:S(2)}) collective-permute-start(bf16[192,1929]{1,0:T(8,128)(2,1)S(1)} %get-tuple-element.341), channel_id=1, source_target_pairs={{0,4},{8,0},{16,8},{24,16},{28,24},{20,28},{12,20},{4,12},{1,5},{9... | collective-permute-start | bytes 2222216 | tf_op jit(solution)/shard_map/ppermute | solution.py:235
  558.5 17.2 %collective-permute-start.22 = (bf16[192,1929]{1,0:T(8,128)(2,1)S(1)}, bf16[192,1929]{1,0:T(8,128)(2,1)S(1)}, u32[]{:S(2)}, u32[]{:S(2)}) collective-permute-start(bf16[192,1929]{1,0:T(8,128)(2,1)S(1)} %get-tuple-element.338), channel_id=1, source_target_pairs={{0,8},{8,16},{16,24},{24,28},{28,20},{20,12},{12,4},{4,0},{1,9},{9... | collective-permute-start | bytes 2222216 | tf_op jit(solution)/shard_map/ppermute | solution.py:231
  559.8 16.6 %collective-permute-start.25 = (bf16[192,1929]{1,0:T(8,128)(2,1)S(1)}, bf16[192,1929]{1,0:T(8,128)(2,1)S(1)}, u32[]{:S(2)}, u32[]{:S(2)}) collective-permute-start(bf16[192,1929]{1,0:T(8,128)(2,1)S(1)} %get-tuple-element.339), channel_id=1, source_target_pairs={{0,4},{8,0},{16,8},{24,16},{28,24},{20,28},{12,20},{4,12},{1,5},{9... | collective-permute-start | bytes 2222216 | tf_op jit(solution)/shard_map/ppermute | solution.py:235
  (93 other events, 725.9 us)
Sparse Core Ops, SparseCore 0:
  102.9 142.5 all-gather.1
  331.1 160.4 reduce-scatter.1
